TPU v7x, 1024 devices: a whole 4x8x16 slice. The times are simulated.
1024 devices in a mesh: lat: 16 (over z_lo, core), lon: 64 (over z_hi, y, x).
Axes of the slice: x: 4, y: 8, z: 16 (z_hi: 2, z_lo: 8; z = z_hi * 8 + z_lo), core: 2. Of those that a mesh axis runs over, the one named last changes fastest.
Arguments:
- state: float32 [128, 1152, 192], P('lat', 'lon'), may hold values from -6 to 6
- courant_east: float32 [128, 1152, 192], P('lat', 'lon'), may hold values from -0.9 to 0.9
- courant_north: float32 [128, 1152, 192], P('lat', 'lon'), may hold values from -0.9 to 0.9
- cutoff: int32 [128], P('lat'), may hold values from 1 to 568, as said below
- filter_mask: int32 [128], P('lat'), may hold values from 0 to 1, as said below
Outputs:
- advanced: float32 [128, 1152, 192], P('lat', 'lon')
Inputs may be any that keep to these rules, and one draw needn't show every extreme that they name: Row j's cutoff is at most 144 + 431 * d // 64, where d = min(j, 127 - j), and equals that bound on the two rows with d = 63; the two rows with d = 0 have cutoff 1. filter_mask is 0 on every row j with min(j, 127 - j) >= 32, and 1 on row 0.
All inputs are finite; a program needn't handle non-finite values.
Results may differ from a plain program's by a relative error of at most 0.00012.
Values sent between devices are 32-bit elements; how exact they have to be, the bound alone decides.
No kernel may reach another device: no remote copies, remote signals or barrier semaphores. Data moves between devices by JAX's collectives and lax.ppermute only.
A program may use at most 32 MiB of HBM per device.

v0:
```python
import math

import jax
import jax.numpy as jnp
from jax import lax
from jax.sharding import PartitionSpec as P


def passed_along(block, axis, distance):
    devices = range(lax.axis_size(axis))
    route = [((i - distance) % len(devices), i) for i in devices]
    return lax.ppermute(block, axis, route)


def padded_2(value, sides, width):
    for axis, dim in sides:
        count, length = (lax.axis_size(axis), value.shape[dim])
        up = [(i, (i + 1) % count) for i in range(count)]
        down = [(j, i) for i, j in up]
        last = lax.slice_in_dim(value, length - width, length, axis=dim)
        initial = lax.slice_in_dim(value, 0, width, axis=dim)
        before = lax.ppermute(last, axis, up)
        after = lax.ppermute(initial, axis, down)
        value = jnp.concatenate([before, value, after], axis=dim)
    return value


def face_flux(far_lo, near_lo, near_hi, far_hi, courant):
    centred = (7.0 * (near_lo + near_hi) - (far_lo + far_hi)) / 12.0
    return courant * centred - 0.5 * jnp.abs(courant) * (near_hi - near_lo)


def build_table(n_full, n_half):
    points = jnp.arange(n_full, dtype=jnp.int32)
    waves = jnp.arange(n_half, dtype=jnp.int32)
    phase = points[:, None] * waves[None, :] % n_full
    angle = phase.astype(jnp.float32) * (2.0 * math.pi / n_full)
    return jnp.concatenate([jnp.cos(angle), jnp.sin(angle)], axis=1)


def pole_rows(field):
    return jnp.concatenate([field[:2][::-1], field[::-1][:2]], axis=0)


def send_rows(field):
    return lax.all_to_all(field, "lon", split_axis=2, concat_axis=1, tiled=True)


def return_rows(merged, lon_count):
    smooth = lax.all_to_all(merged, "lon", split_axis=1, concat_axis=2, tiled=True)
    partner = passed_along(pole_rows(smooth), "lon", lon_count // 2)
    return (smooth, partner)


def local(state, courant_east, courant_north, cutoff, filter_mask):
    n_rows, n_cols, n_comp = state.shape
    lon_count = lax.axis_size("lon")
    lat_count = lax.axis_size("lat")
    lat_index = lax.axis_index("lat")
    n_full = n_cols * lon_count
    n_half = n_full // 2 + 1
    n_lat = n_rows * lat_count
    fourier = build_table(n_full, n_half)
    waves = jnp.arange(n_half, dtype=jnp.int32)
    weights = jnp.where((waves == 0) | (waves == n_half - 1), 1.0 / n_full, 2.0 / n_full).astype(
        jnp.float32
    )
    row_lines = send_rows(state)
    kept = jnp.where(waves[None, :] <= cutoff[:, None], weights[None, :], 0.0)
    kept_both = jnp.concatenate([kept, kept], axis=1)
    coeffs = lax.dot_general(
        row_lines, fourier, (((1,), (0,)), ((), ())), precision=lax.Precision.HIGHEST
    )
    coeffs = coeffs * kept_both[:, None, :]
    synth = lax.dot_general(
        coeffs, fourier, (((2,), (1,)), ((), ())), precision=lax.Precision.HIGHEST
    )
    filtered = jnp.transpose(synth, (0, 2, 1))
    merged = jnp.where(filter_mask[:, None, None] == 1, filtered, row_lines)
    smooth, partner = return_rows(merged, lon_count)
    stacked = jnp.stack([smooth, courant_east, courant_north])
    padded = padded_2(stacked, (("lat", 1), ("lon", 2)), 2)
    zonal_p = padded[0, 2:-2]
    zonal_c = padded[1, 2:-2]
    east = face_flux(
        zonal_p[:, 0 : n_cols + 1],
        zonal_p[:, 1 : n_cols + 2],
        zonal_p[:, 2 : n_cols + 3],
        zonal_p[:, 3 : n_cols + 4],
        zonal_c[:, 1 : n_cols + 2],
    )
    zonal = -(east[:, 1:] - east[:, :-1])
    merid_p = padded[0, :, 2:-2]
    south = jnp.where(lat_index == 0, partner[:2], merid_p[:2])
    north = jnp.where(lat_index == lat_count - 1, partner[2:], merid_p[-2:])
    merid_p = jnp.concatenate([south, merid_p[2:-2], north], axis=0)
    merid_c = padded[2, :, 2:-2]
    north_flux = face_flux(
        merid_p[0 : n_rows + 1],
        merid_p[1 : n_rows + 2],
        merid_p[2 : n_rows + 3],
        merid_p[3 : n_rows + 4],
        merid_c[1 : n_rows + 2],
    )
    face_rows = lat_index * n_rows + jnp.arange(-1, n_rows, dtype=jnp.int32)
    cos_face = jnp.sin(
        jnp.minimum(face_rows + 1, n_lat - 1 - face_rows).astype(jnp.float32) * (math.pi / n_lat)
    )
    cell_rows = face_rows[1:]
    cos_cell = jnp.sin(
        (jnp.minimum(cell_rows, n_lat - 1 - cell_rows).astype(jnp.float32) + 0.5)
        * (math.pi / n_lat)
    )
    weighted = cos_face[:, None, None] * north_flux
    meridional = -(weighted[1:] - weighted[:-1]) / cos_cell[:, None, None]
    return smooth + zonal + meridional


def solution(mesh):
    placed = (
        P("lat", "lon", None),
        P("lat", "lon", None),
        P("lat", "lon", None),
        P("lat"),
        P("lat"),
    )
    return jax.shard_map(
        local, mesh=mesh, in_specs=placed, out_specs=P("lat", "lon", None), check_vma=False
    )
```

profile of v0, /device:TPU:1, one launch (start us, length us, event | category | flops | bytes accessed | tf_op | source)
XLA Modules:
  0.0 157.5 jit_solution(15389490167311867194)
XLA Ops:
  0.0 1.2 copy.122
  1.2 1.6 %reshape.33 = f32[64,1,432]{2,1,0:T(1,128)} reshape(f32[192,8,18]{2,1,0:T(8,128)S(1)} %bitcast.70) | data formatting | bytes 221184
  2.9 28.0 %all-to-all-start = ((f32[64,1,432]{2,1,0:T(1,128)}), f32[64,1,432]{2,1,0:T(1,128)S(1)}, u32[]{:S(2)}, u32[]{:S(2)}) async-start(f32[64,1,432]{2,1,0:T(1,128)} %reshape.33), calls=%async_computation | async-start | bytes 262144 | tf_op jit(solution)/shard_map/all_to_all | solution.py:46
  30.9 0.7 fusion.31
  31.6 0.1 pad_maximum_fusion.10
  31.7 0.7 broadcast_compare_fusion
  32.4 11.8 %fusion.6 = (f32[1152,577]{0,1:T(8,128)S(1)}, f32[1152,577]{0,1:T(8,128)}) fusion(), kind=kLoop, calls=%fused_computation.9 | loop fusion | flops 5982336 | bytes 5317632 | tf_op jit(solution)/shard_map/sin | solution.py:38
  44.2 5.2 %all-to-all-done = f32[64,1,432]{2,1,0:T(1,128)S(1)} async-done(((f32[64,1,432]{2,1,0:T(1,128)}), f32[64,1,432]{2,1,0:T(1,128)S(1)}, u32[]{:S(2)}, u32[]{:S(2)}) %all-to-all-start) | async-done | bytes 110624 | tf_op jit(solution)/shard_map/all_to_all | solution.py:46
  49.3 0.6 broadcast.87
  49.9 1.6 %reduce = f32[64,432]{1,0:T(8,128)} reduce(f32[64,1,432]{2,1,0:T(1,128)S(1)} %all-to-all-done, f32[]{:T(128)} %broadcast.87), dimensions={1}, to_apply=%all_to_all.26.reduce_sub_computation | reduce | bytes 221188 | tf_op jit(solution)/shard_map/all_to_all | solution.py:46
  51.5 1.2 reshape.34
  52.7 1.0 copy.123
  53.7 1.5 all_to_all.29
  55.2 6.7 %fusion.10 = f32[8,3,1154]{2,0,1:T(8,128)S(1)} fusion(f32[8,1152,3]{1,0,2:T(8,128)S(1)} %all_to_all.29, f32[1152,577]{0,1:T(8,128)S(1)} %get-tuple-element.15, f32[1152,577]{0,1:T(8,128)} %get-tuple-element.16, f32[8,1154]{1,0:T(8,128)S(1)} %pad_maximum_fusion.10), kind=kOutput, calls=%fused_computation.13 | convolution fusion | flops 384226624 | bytes 5575936 | tf_op jit(solution)/shard_map/dot_general | solution.py:71
  61.9 2.8 %fusion.12 = f32[8,1152,3]{1,0,2:T(8,128)S(1)} fusion(f32[8,1152,3]{1,0,2:T(8,128)S(1)} %all_to_all.29, f32[8,3,1154]{2,0,1:T(8,128)S(1)} %fusion.10, f32[1152,577]{0,1:T(8,128)S(1)} %get-tuple-element.15, f32[1152,577]{0,1:T(8,128)S(1)} %copy-done, pred[8]{0:T(512)(128)(4,1)S(1)} %broadcast_compare_fusion), kind=kOutput, calls=%fused_computation.15 | convolution fusion | flops 384226560 | bytes 5649608 | tf_op jit(solution)/shard_map/dot_general | solution.py:75
  64.8 1.5 copy.124
  66.3 2.2 %reshape.35 = f32[64,1,432]{2,1,0:T(1,128)} reshape(f32[1152,3,8]{2,1,0:T(4,128)S(1)} %bitcast.65) | data formatting | bytes 221184
  68.4 14.5 %all-to-all-start.1 = ((f32[64,1,432]{2,1,0:T(1,128)}), f32[64,1,432]{2,1,0:T(1,128)S(1)}, u32[]{:S(2)}, u32[]{:S(2)}) async-start(f32[64,1,432]{2,1,0:T(1,128)} %reshape.35), calls=%async_computation.1 | async-start | bytes 262144 | tf_op jit(solution)/shard_map/all_to_all | solution.py:50
  83.0 0.1 fusion.37
  83.1 18.0 %all-to-all-done.1 = f32[64,1,432]{2,1,0:T(1,128)S(1)} async-done(((f32[64,1,432]{2,1,0:T(1,128)}), f32[64,1,432]{2,1,0:T(1,128)S(1)}, u32[]{:S(2)}, u32[]{:S(2)}) %all-to-all-start.1) | async-done | bytes 110624 | tf_op jit(solution)/shard_map/all_to_all | solution.py:50
  101.1 0.9 reduce.1
  102.1 1.3 reshape.36
  103.3 1.4 copy.143
  104.8 2.2 %copy.142 = f32[8,64,18,3]{2,1,0,3:T(8,128)} copy(f32[8,64,18,3]{0,3,2,1:T(4,128)S(1)} %bitcast.64) | data formatting | bytes 221184 | tf_op jit(solution)/shard_map/all_to_all | solution.py:50
  107.0 0.4 copy.128
  107.4 0.1 fusion.42
  107.5 6.0 %collective-permute-start = (f32[3,2,18,192]{3,1,2,0:T(2,128)S(1)}, f32[3,2,18,192]{3,1,2,0:T(2,128)S(1)}, u32[]{:S(2)}, u32[]{:S(2)}) collective-permute-start(f32[3,2,18,192]{3,1,2,0:T(2,128)S(1)} %get-tuple-element.11), channel_id=1, source_target_pairs={{0,64},{64,128},{128,192},{192,256},{256,320},{320,384},{384,448},... | collective-permute-start | bytes 248840 | tf_op jit(solution)/shard_map/ppermute | solution.py:22
  113.6 1.1 fusion.41
  114.6 0.2 copy.137
  114.8 0.1 copy.138
  114.9 0.2 slice.134
  115.1 0.2 copy.135
  115.3 0.1 copy.136
  115.4 0.2 rev.4
  115.6 2.2 %collective-permute-start.4 = (f32[4,18,192]{2,0,1:T(4,128)S(1)}, f32[4,18,192]{2,0,1:T(4,128)S(1)}, u32[]{:S(2)}, u32[]{:S(2)}) collective-permute-start(f32[4,18,192]{2,0,1:T(4,128)S(1)} %pad_maximum_fusion.9), channel_id=1, source_target_pairs={{32,0},{33,1},{34,2},{35,3},{36,4},{37,5},{38,6},{39,7},{40,8},{41... | collective-permute-start | bytes 165896 | tf_op jit(solution)/shard_map/ppermute | solution.py:12
  117.8 1.9 %collective-permute-start.1 = (f32[3,2,18,192]{3,1,2,0:T(2,128)S(1)}, f32[3,2,18,192]{3,1,2,0:T(2,128)S(1)}, u32[]{:S(2)}, u32[]{:S(2)}) collective-permute-start(f32[3,2,18,192]{3,1,2,0:T(2,128)S(1)} %get-tuple-element.12), channel_id=1, source_target_pairs={{64,0},{128,64},{192,128},{256,192},{320,256},{384,320},{448,384},... | collective-permute-start | bytes 248840 | tf_op jit(solution)/shard_map/ppermute | solution.py:23
  119.7 0.4 copy.134
  120.1 0.1 copy_dynamic-update-slice_fusion
  120.3 8.2 %collective-permute-done.1 = f32[3,2,18,192]{3,1,2,0:T(2,128)S(1)} collective-permute-done((f32[3,2,18,192]{3,1,2,0:T(2,128)S(1)}, f32[3,2,18,192]{3,1,2,0:T(2,128)S(1)}, u32[]{:S(2)}, u32[]{:S(2)}) %collective-permute-start.1) | collective-permute-done | bytes 82976 | tf_op jit(solution)/shard_map/ppermute | solution.py:23
  128.6 8.9 %collective-permute-start.3 = (f32[3,12,2,192]{3,2,1,0:T(2,128)S(1)}, f32[3,12,2,192]{3,2,1,0:T(2,128)S(1)}, u32[]{:S(2)}, u32[]{:S(2)}) collective-permute-start(f32[3,12,2,192]{3,2,1,0:T(2,128)S(1)} %get-tuple-element.8), channel_id=1, source_target_pairs={{1,0},{2,1},{3,2},{4,3},{5,4},{6,5},{7,6},{8,7},{9,8},{10,9},{11,1... | collective-permute-start | bytes 165896 | tf_op jit(solution)/shard_map/ppermute | solution.py:23
  137.5 1.9 %collective-permute-start.2 = (f32[3,12,2,192]{3,2,1,0:T(2,128)S(1)}, f32[3,12,2,192]{3,2,1,0:T(2,128)S(1)}, u32[]{:S(2)}, u32[]{:S(2)}) collective-permute-start(f32[3,12,2,192]{3,2,1,0:T(2,128)S(1)} %get-tuple-element.7), channel_id=1, source_target_pairs={{0,1},{1,2},{2,3},{3,4},{4,5},{5,6},{6,7},{7,8},{8,9},{9,10},{10,1... | collective-permute-start | bytes 165896 | tf_op jit(solution)/shard_map/ppermute | solution.py:22
  139.5 0.3 fusion.18
  139.8 16.7 %collective-permute-done.2 = f32[3,12,2,192]{3,2,1,0:T(2,128)S(1)} collective-permute-done((f32[3,12,2,192]{3,2,1,0:T(2,128)S(1)}, f32[3,12,2,192]{3,2,1,0:T(2,128)S(1)}, u32[]{:S(2)}, u32[]{:S(2)}) %collective-permute-start.2) | collective-permute-done | bytes 55328 | tf_op jit(solution)/shard_map/ppermute | solution.py:22
  156.5 0.1 pad_maximum_fusion.8
  156.5 0.1 copy.152
  156.6 0.1 copy.153
  156.7 0.1 fusion.23
  156.7 0.7 fusion.26
  (18 shorter events, 0.3 us)
Async XLA Ops:
  2.9 46.5 %all-to-all-start = ((f32[64,1,432]{2,1,0:T(1,128)}), f32[64,1,432]{2,1,0:T(1,128)S(1)}, u32[]{:S(2)}, u32[]{:S(2)}) async-start(f32[64,1,432]{2,1,0:T(1,128)} %reshape.33), calls=%async_computation | async-start | bytes 262144 | tf_op jit(solution)/shard_map/all_to_all | solution.py:46
  55.2 6.7 %copy-start = (f32[1152,577]{0,1:T(8,128)S(1)}, f32[1152,577]{0,1:T(8,128)}, u32[]{:S(2)}) copy-start(f32[1152,577]{0,1:T(8,128)} %get-tuple-element.16) | copy-start | bytes 7976452
  68.4 32.7 %all-to-all-start.1 = ((f32[64,1,432]{2,1,0:T(1,128)}), f32[64,1,432]{2,1,0:T(1,128)S(1)}, u32[]{:S(2)}, u32[]{:S(2)}) async-start(f32[64,1,432]{2,1,0:T(1,128)} %reshape.35), calls=%async_computation.1 | async-start | bytes 262144 | tf_op jit(solution)/shard_map/all_to_all | solution.py:50
  104.8 2.6 %copy-start.1 = (f32[8,18,192]{2,0,1:T(8,128)S(1)}, f32[8,18,192]{2,0,1:T(8,128)}, u32[]{:S(2)}) copy-start(f32[8,18,192]{2,0,1:T(8,128)} %param.7) | copy-start | bytes 331780
  104.8 2.6 %copy-start.2 = (f32[8,18,192]{2,0,1:T(8,128)S(1)}, f32[8,18,192]{2,0,1:T(8,128)}, u32[]{:S(2)}) copy-start(f32[8,18,192]{2,0,1:T(8,128)} %param.6) | copy-start | bytes 331780
  107.5 12.6 %collective-permute-start = (f32[3,2,18,192]{3,1,2,0:T(2,128)S(1)}, f32[3,2,18,192]{3,1,2,0:T(2,128)S(1)}, u32[]{:S(2)}, u32[]{:S(2)}) collective-permute-start(f32[3,2,18,192]{3,1,2,0:T(2,128)S(1)} %get-tuple-element.11), channel_id=1, source_target_pairs={{0,64},{64,128},{128,192},{192,256},{256,320},{320,384},{384,448},... | collective-permute-start | bytes 248840 | tf_op jit(solution)/shard_map/ppermute | solution.py:22
  115.6 23.8 %collective-permute-start.4 = (f32[4,18,192]{2,0,1:T(4,128)S(1)}, f32[4,18,192]{2,0,1:T(4,128)S(1)}, u32[]{:S(2)}, u32[]{:S(2)}) collective-permute-start(f32[4,18,192]{2,0,1:T(4,128)S(1)} %pad_maximum_fusion.9), channel_id=1, source_target_pairs={{32,0},{33,1},{34,2},{35,3},{36,4},{37,5},{38,6},{39,7},{40,8},{41... | collective-permute-start | bytes 165896 | tf_op jit(solution)/shard_map/ppermute | solution.py:12
  117.8 10.7 %collective-permute-start.1 = (f32[3,2,18,192]{3,1,2,0:T(2,128)S(1)}, f32[3,2,18,192]{3,1,2,0:T(2,128)S(1)}, u32[]{:S(2)}, u32[]{:S(2)}) collective-permute-start(f32[3,2,18,192]{3,1,2,0:T(2,128)S(1)} %get-tuple-element.12), channel_id=1, source_target_pairs={{64,0},{128,64},{192,128},{256,192},{320,256},{384,320},{448,384},... | collective-permute-start | bytes 248840 | tf_op jit(solution)/shard_map/ppermute | solution.py:23
  128.6 11.2 %collective-permute-start.3 = (f32[3,12,2,192]{3,2,1,0:T(2,128)S(1)}, f32[3,12,2,192]{3,2,1,0:T(2,128)S(1)}, u32[]{:S(2)}, u32[]{:S(2)}) collective-permute-start(f32[3,12,2,192]{3,2,1,0:T(2,128)S(1)} %get-tuple-element.8), channel_id=1, source_target_pairs={{1,0},{2,1},{3,2},{4,3},{5,4},{6,5},{7,6},{8,7},{9,8},{10,9},{11,1... | collective-permute-start | bytes 165896 | tf_op jit(solution)/shard_map/ppermute | solution.py:23
  137.5 19.0 %collective-permute-start.2 = (f32[3,12,2,192]{3,2,1,0:T(2,128)S(1)}, f32[3,12,2,192]{3,2,1,0:T(2,128)S(1)}, u32[]{:S(2)}, u32[]{:S(2)}) collective-permute-start(f32[3,12,2,192]{3,2,1,0:T(2,128)S(1)} %get-tuple-element.7), channel_id=1, source_target_pairs={{0,1},{1,2},{2,3},{3,4},{4,5},{5,6},{6,7},{7,8},{8,9},{9,10},{10,1... | collective-permute-start | bytes 165896 | tf_op jit(solution)/shard_map/ppermute | solution.py:22
where the time goes:
time: 158 us; the launch traced here: 157 us
  starting transfers between devices  63.4 us (40%)
  waiting for transfers between devices  48.1 us (30%)
  local copies, waits for them, and re-layouts  18.9 us (12%)
  other arithmetic  17.3 us (11%)
  matrix products  9.49 us (6%)
    all_to_all x1, starting transfers between devices, send_rows(): return lax.all_to_all(field, 'lon', split_axis=2, concat_axis=1, tiled=True)  28 us
    all_to_all x1, waiting for transfers between devices, return_rows(): lax.all_to_all(merged, 'lon', split_axis=1, concat_axis=2, tiled=True)  18 us
    ppermute x2, waiting for transfers between devices, padded_2(): before = lax.ppermute(last, axis, up)  16.7 us
    all_to_all x1, starting transfers between devices, return_rows(): lax.all_to_all(merged, 'lon', split_axis=1, concat_axis=2, tiled=True)  14.5 us
    sin x1, other arithmetic, build_table(): return jnp.concatenate([jnp.cos(angle), jnp.sin(angle)], axis=1)  11.8 us
    ppermute x2, starting transfers between devices, padded_2(): after = lax.ppermute(initial, axis, down)  10.8 us
    ppermute x2, waiting for transfers between devices, padded_2(): after = lax.ppermute(initial, axis, down)  8.25 us
    ppermute x2, starting transfers between devices, padded_2(): before = lax.ppermute(last, axis, up)  7.96 us
  transfers between devices with their start and end apart: 7, of which 4 were waited for; matrix products, arithmetic and copies ran while one was open for 10% of the time, Pallas kernels for 0%

commit v1 on v0

v1 whole, which is shorter than its diff:
```python
import math

import jax
import jax.numpy as jnp
from jax import lax
from jax.sharding import PartitionSpec as P


def shifted_from(block, axis, distance):
    count = lax.axis_size(axis)
    route = [(i, (i + distance) % count) for i in range(count)]
    return lax.ppermute(block, axis, route)


def face_flux(far_lo, near_lo, near_hi, far_hi, courant):
    centred = (7.0 * (near_lo + near_hi) - (far_lo + far_hi)) / 12.0
    return courant * centred - 0.5 * jnp.abs(courant) * (near_hi - near_lo)


def build_table(n_full, n_waves):
    points = jnp.arange(n_full, dtype=jnp.int32)
    waves = jnp.arange(n_waves, dtype=jnp.int32)
    phase = points[:, None] * waves[None, :] % n_full
    angle = phase.astype(jnp.float32) * (2.0 * math.pi / n_full)
    return jnp.concatenate([jnp.cos(angle), jnp.sin(angle)], axis=1)


def local(state, courant_east, courant_north, cutoff_all, mask_all):
    n_rows, n_cols, n_comp = state.shape
    lon_count = lax.axis_size("lon")
    lat_count = lax.axis_size("lat")
    lat_index = lax.axis_index("lat")
    n_full = n_cols * lon_count
    n_lat = n_rows * lat_count
    half = n_full // 2
    group = n_comp // lon_count

    top = n_full // 8 + (half - 1 - n_full // 8) * (n_lat // 4 - 1) // (n_lat // 2)
    n_waves = min(top, half - 1) + 1

    from_south = shifted_from(
        jnp.concatenate([state[-2:], courant_north[-1:]], axis=0), "lat", 1
    )
    from_north = shifted_from(state[:2], "lat", -1)
    east_halo = shifted_from(courant_east[:, -1:], "lon", 1)

    rows_ext = jnp.concatenate([from_south[:2], state, from_north], axis=0)
    n_ext = n_rows + 4
    lines = lax.all_to_all(rows_ext, "lon", split_axis=2, concat_axis=1, tiled=True)

    fourier = build_table(n_full, n_waves)
    waves = jnp.arange(n_waves, dtype=jnp.int32)
    weights = jnp.where(waves == 0, 1.0 / n_full, 2.0 / n_full).astype(jnp.float32)
    cut_pad = jnp.pad(cutoff_all, (2, 2))
    mask_pad = jnp.pad(mask_all, (2, 2))
    start = lat_index * n_rows
    cut_ext = lax.dynamic_slice_in_dim(cut_pad, start, n_ext)
    mask_ext = lax.dynamic_slice_in_dim(mask_pad, start, n_ext)
    kept = jnp.where(waves[None, :] <= cut_ext[:, None], weights[None, :], 0.0)
    kept_both = jnp.concatenate([kept, kept], axis=1)
    coeffs = lax.dot_general(
        lines, fourier, (((1,), (0,)), ((), ())), precision=lax.Precision.HIGHEST
    )
    coeffs = coeffs * kept_both[:, None, :]
    synth = lax.dot_general(
        coeffs, fourier, (((2,), (1,)), ((), ())), precision=lax.Precision.HIGHEST
    )
    filtered = jnp.transpose(synth, (0, 2, 1))
    smooth = jnp.where(mask_ext[:, None, None] == 1, filtered, lines)

    south_pole = jnp.roll(smooth[3:1:-1], half, axis=1)
    north_pole = jnp.roll(smooth[n_ext - 3 : n_ext - 5 : -1], half, axis=1)
    low = jnp.where(lat_index == 0, south_pole, smooth[:2])
    high = jnp.where(lat_index == lat_count - 1, north_pole, smooth[-2:])
    smooth = jnp.concatenate([low, smooth[2:-2], high], axis=0)

    tiles = smooth.reshape(n_ext, lon_count, n_cols, group)
    left = jnp.roll(tiles[:, :, -2:], 1, axis=1)
    right = jnp.roll(tiles[:, :, :2], -1, axis=1)
    windows = jnp.concatenate([left, tiles, right], axis=2)
    windows = jnp.transpose(windows, (1, 0, 2, 3))
    back = lax.all_to_all(windows, "lon", split_axis=0, concat_axis=0, tiled=True)
    ext = jnp.transpose(back, (1, 2, 0, 3)).reshape(n_ext, n_cols + 4, n_comp)

    zonal_p = ext[2:-2]
    zonal_c = jnp.concatenate([east_halo, courant_east], axis=1)
    east = face_flux(
        zonal_p[:, 0 : n_cols + 1],
        zonal_p[:, 1 : n_cols + 2],
        zonal_p[:, 2 : n_cols + 3],
        zonal_p[:, 3 : n_cols + 4],
        zonal_c,
    )
    zonal = -(east[:, 1:] - east[:, :-1])

    merid_p = ext[:, 2:-2]
    south_c = jnp.where(lat_index == 0, 0.0, from_south[2:])
    merid_c = jnp.concatenate([south_c, courant_north], axis=0)
    north_flux = face_flux(
        merid_p[0 : n_rows + 1],
        merid_p[1 : n_rows + 2],
        merid_p[2 : n_rows + 3],
        merid_p[3 : n_rows + 4],
        merid_c,
    )
    face_rows = lat_index * n_rows + jnp.arange(-1, n_rows, dtype=jnp.int32)
    cos_face = jnp.sin(
        jnp.minimum(face_rows + 1, n_lat - 1 - face_rows).astype(jnp.float32) * (math.pi / n_lat)
    )
    cell_rows = face_rows[1:]
    cos_cell = jnp.sin(
        (jnp.minimum(cell_rows, n_lat - 1 - cell_rows).astype(jnp.float32) + 0.5)
        * (math.pi / n_lat)
    )
    weighted = cos_face[:, None, None] * north_flux
    meridional = -(weighted[1:] - weighted[:-1]) / cos_cell[:, None, None]
    return zonal_p[:, 2:-2] + zonal + meridional


def solution(mesh):
    placed = (
        P("lat", "lon", None),
        P("lat", "lon", None),
        P("lat", "lon", None),
        P(None),
        P(None),
    )
    return jax.shard_map(
        local, mesh=mesh, in_specs=placed, out_specs=P("lat", "lon", None), check_vma=False
    )
```

time: 158 us -> 160 us (1.013)
  the two profiles are of different devices: /device:TPU:1 before, /device:TPU:8 now
where the time goes in v1:
time: 160 us; the launch traced here: 159 us
  starting transfers between devices  51.3 us (32%)
  local copies, waits for them, and re-layouts  43.7 us (27%)
  waiting for transfers between devices  29.6 us (18%)
  other arithmetic  17.2 us (11%)
  blocking collectives  10 us (6%)
  matrix products  5.93 us (4%)
    unnamed x53, local copies, waits for them, and re-layouts  24.1 us
    all_to_all x1, starting transfers between devices, local(): lax.all_to_all(rows_ext, 'lon', split_axis=2, concat_axis=1, tiled=True)  21.2 us
    ppermute x3, starting transfers between devices, shifted_from(): return lax.ppermute(block, axis, route)  21.1 us
    all_to_all x1, waiting for transfers between devices, local(): lax.all_to_all(windows, 'lon', split_axis=0, concat_axis=0, tiled=True)  18.5 us
    all_to_all x1, waiting for transfers between devices, local(): lax.all_to_all(rows_ext, 'lon', split_axis=2, concat_axis=1, tiled=True)  11.1 us
    unnamed x1, blocking collectives  10 us
    all_to_all x1, starting transfers between devices, local(): lax.all_to_all(windows, 'lon', split_axis=0, concat_axis=0, tiled=True)  8.96 us
    sin x1, other arithmetic, build_table(): return jnp.concatenate([jnp.cos(angle), jnp.sin(angle)], axis=1)  6.67 us
  transfers between devices with their start and end apart: 5, of which 2 were waited for; matrix products, arithmetic and copies ran while one was open for 23% of the time, Pallas kernels for 0%

profile of v1, /device:TPU:8, one launch (start us, length us, event | category | flops | bytes accessed | tf_op | source)
XLA Modules:
  0.0 158.8 jit_solution(9648006139654907838)
XLA Ops:
  0.0 0.9 slice.135
  0.9 1.0 fusion.37
  2.0 1.9 %collective-permute-start = (f32[3,18,192]{2,1,0:T(8,128)S(1)}, f32[3,18,192]{2,1,0:T(8,128)S(1)}, u32[]{:S(2)}, u32[]{:S(2)}) collective-permute-start(f32[3,18,192]{2,1,0:T(8,128)S(1)} %pad_maximum_fusion.3), channel_id=1, source_target_pairs={{0,64},{64,128},{128,192},{192,256},{256,320},{320,384},{384,448},... | collective-permute-start | bytes 124424 | tf_op jit(solution)/shard_map/ppermute | solution.py:12
  3.9 15.8 %collective-permute-start.1 = (f32[2,18,192]{2,1,0:T(8,128)S(1)}, f32[2,18,192]{2,1,0:T(8,128)S(1)}, u32[]{:S(2)}, u32[]{:S(2)}) collective-permute-start(f32[2,18,192]{2,1,0:T(8,128)S(1)} %copy.153), channel_id=1, source_target_pairs={{0,960},{64,0},{128,64},{192,128},{256,192},{320,256},{384,320},{4... | collective-permute-start | bytes 82952 | tf_op jit(solution)/shard_map/ppermute | solution.py:12
  19.7 0.7 slice.156
  20.4 3.4 %collective-permute-start.2 = (f32[8,1,192]{2,0,1:T(8,128)S(1)}, f32[8,1,192]{2,0,1:T(8,128)S(1)}, u32[]{:S(2)}, u32[]{:S(2)}) collective-permute-start(f32[8,1,192]{2,0,1:T(8,128)S(1)} %slice.156), channel_id=1, source_target_pairs={{0,1},{1,2},{2,3},{3,4},{4,5},{5,6},{6,7},{7,8},{8,9},{9,10},{10,1... | collective-permute-start | bytes 18440 | tf_op jit(solution)/shard_map/ppermute | solution.py:12
  23.8 1.3 dynamic-slice
  25.8 0.9 dynamic-update-slice.1
  26.6 0.8 dynamic-update-slice
  27.5 10.0 %all-reduce.4 = (s32[128]{0:T(128)S(1)}, s32[128]{0:T(128)S(1)}) all-reduce(s32[128]{0:T(128)S(1)} %dynamic-update-slice.1, s32[128]{0:T(128)S(1)} %dynamic-update-slice), channel_id=4, replica_groups=mesh['lat'=16,'lon'=64] {'lat'}, use_global_device_ids=true, to_apply=%add.3 | all-reduce | flops 256 | bytes 2048
  37.6 1.2 copy.127
  39.0 0.6 copy-done.13
  40.1 1.6 %reshape.41 = f32[64,1,648]{2,1,0:T(1,128)} reshape(f32[192,12,18]{2,1,0:T(8,128)S(1)} %fusion.38) | data formatting | bytes 331776
  41.8 21.2 %all-to-all-start = ((f32[64,1,648]{2,1,0:T(1,128)}), f32[64,1,648]{2,1,0:T(1,128)S(1)}, u32[]{:S(2)}, u32[]{:S(2)}) async-start(f32[64,1,648]{2,1,0:T(1,128)} %reshape.41), calls=%async_computation | async-start | bytes 393216 | tf_op jit(solution)/shard_map/all_to_all | solution.py:49
  63.1 0.7 fusion.29
  63.7 0.7 pad_maximum_fusion.4
  64.4 6.7 %fusion.8 = (f32[1152,353]{0,1:T(8,128)S(1)}, f32[1152,353]{0,1:T(8,128)S(1)}) fusion(), kind=kLoop, calls=%fused_computation.11 | loop fusion | flops 3659904 | bytes 3253248 | tf_op jit(solution)/shard_map/sin | solution.py:25
  71.1 11.1 %all-to-all-done = f32[64,1,648]{2,1,0:T(1,128)S(1)} async-done(((f32[64,1,648]{2,1,0:T(1,128)}), f32[64,1,648]{2,1,0:T(1,128)S(1)}, u32[]{:S(2)}, u32[]{:S(2)}) %all-to-all-start) | async-done | bytes 165920 | tf_op jit(solution)/shard_map/all_to_all | solution.py:49
  82.2 0.7 copy-done.9
  83.4 2.0 %reduce = f32[64,648]{1,0:T(8,128)S(1)} reduce(f32[64,1,648]{2,1,0:T(1,128)} %copy-done.9, f32[]{:T(128)} %broadcast.89), dimensions={1}, to_apply=%all_to_all.16.reduce_sub_computation | reduce | bytes 331780 | tf_op jit(solution)/shard_map/all_to_all | solution.py:49
  85.4 1.9 %reshape.42 = f32[192,12,18]{2,1,0:T(8,128)} reshape(f32[64,648]{1,0:T(8,128)S(1)} %reduce) | data formatting | bytes 331776
  87.3 2.0 %copy.165 = f32[12,18,64,3]{1,3,2,0:T(4,128)S(1)} copy(f32[12,18,64,3]{1,0,3,2:T(8,128)} %bitcast.45) | data formatting | bytes 331776 | tf_op jit(solution)/shard_map/all_to_all | solution.py:49
  89.3 1.2 copy.130
  90.5 1.9 %all_to_all.19 = f32[12,1152,3]{1,0,2:T(8,128)S(1)} reshape(f32[12,64,18,3]{2,1,0,3:T(8,128)} %copy.130) | data formatting | bytes 331776 | tf_op jit(solution)/shard_map/all_to_all | solution.py:49
  92.3 3.7 %fusion.11 = f32[12,3,706]{2,0,1:T(8,128)S(1)} fusion(f32[12,1152,3]{1,0,2:T(8,128)S(1)} %all_to_all.19, f32[1152,353]{0,1:T(8,128)S(1)} %get-tuple-element.27, f32[1152,353]{0,1:T(8,128)S(1)} %get-tuple-element.28, f32[12,706]{1,0:T(8,128)} %pad_maximum_fusion.4), kind=kOutput, calls=%fused_computation.17 | convolution fusion | flops 352189504 | bytes 3554688 | tf_op jit(solution)/shard_map/dot_general | solution.py:61
  96.1 2.2 %fusion.3 = f32[12,1152,3]{1,0,2:T(8,128)S(1)} fusion(f32[12,1152,3]{1,0,2:T(8,128)S(1)} %all_to_all.19, f32[12,3,706]{2,0,1:T(8,128)S(1)} %fusion.11, f32[1152,353]{0,1:T(8,128)S(1)} %get-tuple-element.27, f32[1152,353]{0,1:T(8,128)S(1)} %get-tuple-element.28, pred[12]{0:T(512)(128)(4,1)S(1)} %copy-done.14), kind=kOutput, calls=%fused_computation.5 | convolution fusion | flops 352205568 | bytes 3686700 | tf_op jit(solution)/shard_map/dot_general | solution.py:65
  99.8 1.1 slice_select_fusion.1
  100.9 1.3 reshape.28
  102.8 0.7 maximum_bitcast_fusion.7
  103.5 0.7 copy.166
  104.3 1.5 reshape.43
  105.8 9.0 %all-to-all-start.1 = ((f32[64,1,792]{2,1,0:T(1,128)}), f32[64,1,792]{2,1,0:T(1,128)S(1)}, u32[]{:S(2)}, u32[]{:S(2)}) async-start(f32[64,1,792]{2,1,0:T(1,128)} %reshape.43), calls=%async_computation.1 | async-start | bytes 458752 | tf_op jit(solution)/shard_map/all_to_all | solution.py:82
  115.0 0.8 slice_select_fusion.2
  115.8 18.5 %all-to-all-done.1 = f32[64,1,792]{2,1,0:T(1,128)S(1)} async-done(((f32[64,1,792]{2,1,0:T(1,128)}), f32[64,1,792]{2,1,0:T(1,128)S(1)}, u32[]{:S(2)}, u32[]{:S(2)}) %all-to-all-start.1) | async-done | bytes 202784 | tf_op jit(solution)/shard_map/all_to_all | solution.py:82
  134.3 1.1 reduce.1
  135.4 0.7 reshape.44
  136.4 1.2 slice.184
  137.5 2.3 %fusion.35 = (f32[8,19,192]{1,0,2:T(8,128)}, f32[8,19,192]{1,0,2:T(8,128)}, f32[8,19,192]{1,0,2:T(8,128)}, f32[8,19,192]{1,0,2:T(8,128)}) fusion(f32[8,22,192]{1,0,2:T(8,128)S(1)} %bitcast.44), kind=kLoop, calls=%fused_computation.60 | loop fusion | bytes 933888 | tf_op jit(solution)/shard_map/slice | solution.py:91
  139.9 3.8 %fusion.32 = (f32[9,18,192]{1,0,2:T(8,128)S(1)}, f32[9,18,192]{1,0,2:T(8,128)}, f32[9,18,192]{1,0,2:T(8,128)}, f32[9,18,192]{1,0,2:T(8,128)}) fusion(f32[12,22,192]{1,0,2:T(8,128)S(1)} %bitcast.42), kind=kLoop, calls=%fused_computation.57 | loop fusion | bytes 995328 | tf_op jit(solution)/shard_map/slice | solution.py:103
  143.7 2.3 %copy.160 = f32[9,18,192]{2,0,1:T(8,128)S(1)} copy(f32[9,18,192]{1,0,2:T(8,128)} %get-tuple-element.9) | data formatting | bytes 248832
  146.0 2.9 %copy.159 = f32[9,18,192]{2,0,1:T(8,128)} copy(f32[9,18,192]{1,0,2:T(8,128)} %get-tuple-element.10) | data formatting | bytes 248832
  148.9 1.6 %copy.161 = f32[9,18,192]{2,0,1:T(8,128)} copy(f32[9,18,192]{1,0,2:T(8,128)S(1)} %copy-done) | data formatting | bytes 248832
  150.5 1.6 copy.162
  152.1 1.0 copy.154
  153.2 1.6 copy.156
  155.9 1.0 multiply_subtract_fusion
  157.0 1.1 fusion.15
  158.1 0.8 fusion.20
  (65 shorter events, 5.1 us)
Async XLA Ops:
  2.0 37.0 %collective-permute-start = (f32[3,18,192]{2,1,0:T(8,128)S(1)}, f32[3,18,192]{2,1,0:T(8,128)S(1)}, u32[]{:S(2)}, u32[]{:S(2)}) collective-permute-start(f32[3,18,192]{2,1,0:T(8,128)S(1)} %pad_maximum_fusion.3), channel_id=1, source_target_pairs={{0,64},{64,128},{128,192},{192,256},{256,320},{320,384},{384,448},... | collective-permute-start | bytes 124424 | tf_op jit(solution)/shard_map/ppermute | solution.py:12
  3.9 34.9 %collective-permute-start.1 = (f32[2,18,192]{2,1,0:T(8,128)S(1)}, f32[2,18,192]{2,1,0:T(8,128)S(1)}, u32[]{:S(2)}, u32[]{:S(2)}) collective-permute-start(f32[2,18,192]{2,1,0:T(8,128)S(1)} %copy.153), channel_id=1, source_target_pairs={{0,960},{64,0},{128,64},{192,128},{256,192},{320,256},{384,320},{4... | collective-permute-start | bytes 82952 | tf_op jit(solution)/shard_map/ppermute | solution.py:12
  20.4 94.5 %collective-permute-start.2 = (f32[8,1,192]{2,0,1:T(8,128)S(1)}, f32[8,1,192]{2,0,1:T(8,128)S(1)}, u32[]{:S(2)}, u32[]{:S(2)}) collective-permute-start(f32[8,1,192]{2,0,1:T(8,128)S(1)} %slice.156), channel_id=1, source_target_pairs={{0,1},{1,2},{2,3},{3,4},{4,5},{5,6},{6,7},{7,8},{8,9},{9,10},{10,1... | collective-permute-start | bytes 18440 | tf_op jit(solution)/shard_map/ppermute | solution.py:12
  39.0 0.6 copy-start.13
  41.8 40.4 %all-to-all-start = ((f32[64,1,648]{2,1,0:T(1,128)}), f32[64,1,648]{2,1,0:T(1,128)S(1)}, u32[]{:S(2)}, u32[]{:S(2)}) async-start(f32[64,1,648]{2,1,0:T(1,128)} %reshape.41), calls=%async_computation | async-start | bytes 393216 | tf_op jit(solution)/shard_map/all_to_all | solution.py:49
  82.2 0.7 copy-start.9
  92.3 3.7 %copy-start.14 = (pred[12]{0:T(512)(128)(4,1)S(1)}, pred[12]{0:T(512)(128)(4,1)}, u32[]{:S(2)}) copy-start(pred[12]{0:T(512)(128)(4,1)} %fusion.29) | copy-start | bytes 40
  98.3 0.7 copy-start.8
  104.2 10.7 %copy-start.12 = (f32[8,18,192]{2,0,1:T(8,128)S(1)}, f32[8,18,192]{2,0,1:T(8,128)}, u32[]{:S(2)}) copy-start(f32[8,18,192]{2,0,1:T(8,128)} %param.6) | copy-start | bytes 331780
  105.8 28.5 %all-to-all-start.1 = ((f32[64,1,792]{2,1,0:T(1,128)}), f32[64,1,792]{2,1,0:T(1,128)S(1)}, u32[]{:S(2)}, u32[]{:S(2)}) async-start(f32[64,1,792]{2,1,0:T(1,128)} %reshape.43), calls=%async_computation.1 | async-start | bytes 458752 | tf_op jit(solution)/shard_map/all_to_all | solution.py:82
  115.0 0.8 copy-start.11
  143.7 5.3 %copy-start = (f32[9,18,192]{1,0,2:T(8,128)S(1)}, f32[9,18,192]{1,0,2:T(8,128)}, u32[]{:S(2)}) copy-start(f32[9,18,192]{1,0,2:T(8,128)} %get-tuple-element.8) | copy-start | bytes 373252
  150.5 1.6 copy-start.4
  152.1 2.6 %copy-start.3 = (f32[8,19,192]{1,0,2:T(8,128)S(1)}, f32[8,19,192]{1,0,2:T(8,128)}, u32[]{:S(2)}) copy-start(f32[8,19,192]{1,0,2:T(8,128)} %get-tuple-element.18) | copy-start | bytes 350212
  152.1 3.0 %copy-start.2 = (f32[8,19,192]{1,0,2:T(8,128)S(1)}, f32[8,19,192]{1,0,2:T(8,128)}, u32[]{:S(2)}) copy-start(f32[8,19,192]{1,0,2:T(8,128)} %get-tuple-element.16) | copy-start | bytes 350212
  153.2 2.4 %copy-start.1 = (f32[8,19,192]{1,0,2:T(8,128)S(1)}, f32[8,19,192]{1,0,2:T(8,128)}, u32[]{:S(2)}) copy-start(f32[8,19,192]{1,0,2:T(8,128)} %get-tuple-element.15) | copy-start | bytes 350212
  155.1 1.8 %copy-start.5 = (f32[9,18,192]{2,0,1:T(8,128)S(1)}, f32[9,18,192]{2,0,1:T(8,128)}, u32[]{:S(2)}) copy-start(f32[9,18,192]{2,0,1:T(8,128)} %copy.159) | copy-start | bytes 373252
  155.1 1.8 %copy-start.6 = (f32[9,18,192]{2,0,1:T(8,128)S(1)}, f32[9,18,192]{2,0,1:T(8,128)}, u32[]{:S(2)}) copy-start(f32[9,18,192]{2,0,1:T(8,128)} %copy.161) | copy-start | bytes 373252
  155.1 1.8 %copy-start.7 = (f32[9,18,192]{2,0,1:T(8,128)S(1)}, f32[9,18,192]{2,0,1:T(8,128)}, u32[]{:S(2)}) copy-start(f32[9,18,192]{2,0,1:T(8,128)} %copy.162) | copy-start | bytes 373252
  155.5 2.5 %copy-start.10 = (f32[8,18,192]{2,0,1:T(8,128)S(1)}, f32[8,18,192]{2,0,1:T(8,128)}, u32[]{:S(2)}) copy-start(f32[8,18,192]{2,0,1:T(8,128)} %copy.154) | copy-start | bytes 331780

commit v2 on v1

--- a/solution.py
+++ b/solution.py
@@ -38,24 +38,34 @@
     top = n_full // 8 + (half - 1 - n_full // 8) * (n_lat // 4 - 1) // (n_lat // 2)
     n_waves = min(top, half - 1) + 1
 
+    def row_info(sel):
+        whole = jnp.concatenate([cutoff_all[sel], mask_all[sel]]).astype(jnp.float32)
+        blank = jnp.zeros((1, n_cols, n_comp), jnp.float32)
+        return blank.at[0, 0, : whole.shape[0]].set(whole)
+
     from_south = shifted_from(
-        jnp.concatenate([state[-2:], courant_north[-1:]], axis=0), "lat", 1
+        jnp.concatenate(
+            [state[-2:], courant_north[-1:], row_info(slice(n_rows - 2, n_rows))], axis=0
+        ),
+        "lat",
+        1,
     )
-    from_north = shifted_from(state[:2], "lat", -1)
+    from_north = shifted_from(
+        jnp.concatenate([state[:2], row_info(slice(0, 2))], axis=0), "lat", -1
+    )
     east_halo = shifted_from(courant_east[:, -1:], "lon", 1)
 
-    rows_ext = jnp.concatenate([from_south[:2], state, from_north], axis=0)
+    rows_ext = jnp.concatenate([from_south[:2], state, from_north[:2]], axis=0)
     n_ext = n_rows + 4
     lines = lax.all_to_all(rows_ext, "lon", split_axis=2, concat_axis=1, tiled=True)
 
     fourier = build_table(n_full, n_waves)
     waves = jnp.arange(n_waves, dtype=jnp.int32)
     weights = jnp.where(waves == 0, 1.0 / n_full, 2.0 / n_full).astype(jnp.float32)
-    cut_pad = jnp.pad(cutoff_all, (2, 2))
-    mask_pad = jnp.pad(mask_all, (2, 2))
-    start = lat_index * n_rows
-    cut_ext = lax.dynamic_slice_in_dim(cut_pad, start, n_ext)
-    mask_ext = lax.dynamic_slice_in_dim(mask_pad, start, n_ext)
+    info_s = from_south[3, 0, :4].astype(jnp.int32)
+    info_n = from_north[2, 0, :4].astype(jnp.int32)
+    cut_ext = jnp.concatenate([info_s[:2], cutoff_all, info_n[:2]])
+    mask_ext = jnp.concatenate([info_s[2:], mask_all, info_n[2:]])
     kept = jnp.where(waves[None, :] <= cut_ext[:, None], weights[None, :], 0.0)
     kept_both = jnp.concatenate([kept, kept], axis=1)
     coeffs = lax.dot_general(
@@ -78,9 +88,8 @@
     left = jnp.roll(tiles[:, :, -2:], 1, axis=1)
     right = jnp.roll(tiles[:, :, :2], -1, axis=1)
     windows = jnp.concatenate([left, tiles, right], axis=2)
-    windows = jnp.transpose(windows, (1, 0, 2, 3))
-    back = lax.all_to_all(windows, "lon", split_axis=0, concat_axis=0, tiled=True)
-    ext = jnp.transpose(back, (1, 2, 0, 3)).reshape(n_ext, n_cols + 4, n_comp)
+    windows = windows.reshape(n_ext, lon_count * (n_cols + 4), group)
+    ext = lax.all_to_all(windows, "lon", split_axis=1, concat_axis=2, tiled=True)
 
     zonal_p = ext[2:-2]
     zonal_c = jnp.concatenate([east_halo, courant_east], axis=1)
@@ -94,7 +103,7 @@
     zonal = -(east[:, 1:] - east[:, :-1])
 
     merid_p = ext[:, 2:-2]
-    south_c = jnp.where(lat_index == 0, 0.0, from_south[2:])
+    south_c = jnp.where(lat_index == 0, 0.0, from_south[2:3])
     merid_c = jnp.concatenate([south_c, courant_north], axis=0)
     north_flux = face_flux(
         merid_p[0 : n_rows + 1],
@@ -122,8 +131,8 @@
         P("lat", "lon", None),
         P("lat", "lon", None),
         P("lat", "lon", None),
-        P(None),
-        P(None),
+        P("lat"),
+        P("lat"),
     )
     return jax.shard_map(
         local, mesh=mesh, in_specs=placed, out_specs=P("lat", "lon", None), check_vma=False

time: 160 us -> 171 us (1.069)
  the two profiles are of different devices: /device:TPU:8 before, /device:TPU:64 now
where the time goes in v2:
time: 171 us; the launch traced here: 170 us
  local copies, waits for them, and re-layouts  57.4 us (34%)
  starting transfers between devices  42.1 us (25%)
  waiting for transfers between devices  40.9 us (24%)
  other arithmetic  23.6 us (14%)
  matrix products  5.72 us (3%)
    all_to_all x1, starting transfers between devices, local(): lax.all_to_all(rows_ext, 'lon', split_axis=2, concat_axis=1, tiled=True)  25 us
    unnamed x60, local copies, waits for them, and re-layouts  23.6 us
    all_to_all x1, waiting for transfers between devices, local(): lax.all_to_all(windows, 'lon', split_axis=1, concat_axis=2, tiled=True)  21.7 us
    all_to_all x1, waiting for transfers between devices, local(): lax.all_to_all(rows_ext, 'lon', split_axis=2, concat_axis=1, tiled=True)  17.8 us
    all_to_all x1, starting transfers between devices, local(): lax.all_to_all(windows, 'lon', split_axis=1, concat_axis=2, tiled=True)  9.25 us
    ppermute x3, starting transfers between devices, shifted_from(): return lax.ppermute(block, axis, route)  7.83 us
    sin x1, other arithmetic, build_table(): return jnp.concatenate([jnp.cos(angle), jnp.sin(angle)], axis=1)  6.67 us
    all_to_all x4, local copies, waits for them, and re-layouts, local(): lax.all_to_all(rows_ext, 'lon', split_axis=2, concat_axis=1, tiled=True)  5.55 us
  transfers between devices with their start and end apart: 5, of which 3 were waited for; matrix products, arithmetic and copies ran while one was open for 32% of the time, Pallas kernels for 0%

profile of v2, /device:TPU:64, one launch (start us, length us, event | category | flops | bytes accessed | tf_op | source)
XLA Modules:
  0.0 170.2 jit_solution(11729100749568442128)
XLA Ops:
  0.7 3.4 %collective-permute-start.2 = (f32[8,1,192]{2,0,1:T(8,128)S(1)}, f32[8,1,192]{2,0,1:T(8,128)S(1)}, u32[]{:S(2)}, u32[]{:S(2)}) collective-permute-start(f32[8,1,192]{2,0,1:T(8,128)S(1)} %slice.258), channel_id=1, source_target_pairs={{0,1},{1,2},{2,3},{3,4},{4,5},{5,6},{6,7},{7,8},{8,9},{9,10},{10,1... | collective-permute-start | bytes 18440 | tf_op jit(solution)/shard_map/ppermute | solution.py:12
  4.1 1.0 fusion.36
  5.1 0.8 slice_bitcast_fusion.3
  6.0 1.9 %collective-permute-start.1 = (f32[3,18,192]{2,1,0:T(8,128)S(1)}, f32[3,18,192]{2,1,0:T(8,128)}, u32[]{:S(2)}, u32[]{:S(2)}) collective-permute-start(f32[3,18,192]{2,1,0:T(8,128)S(1)} %select_maximum_fusion.1), channel_id=1, source_target_pairs={{0,960},{64,0},{128,64},{192,128},{256,192},{320,256},{384,320},{4... | collective-permute-start | bytes 124424 | tf_op jit(solution)/shard_map/ppermute | solution.py:12
  7.9 0.9 slice.222
  9.6 2.5 %collective-permute-start = (f32[4,18,192]{2,1,0:T(8,128)}, f32[4,18,192]{2,1,0:T(8,128)}, u32[]{:S(2)}, u32[]{:S(2)}) collective-permute-start(f32[4,18,192]{2,1,0:T(8,128)} %select_maximum_fusion), channel_id=1, source_target_pairs={{0,64},{64,128},{128,192},{192,256},{256,320},{320,384},{384,448},... | collective-permute-start | bytes 165896 | tf_op jit(solution)/shard_map/ppermute | solution.py:12
  12.2 6.7 %fusion.8 = (f32[1152,353]{0,1:T(8,128)S(1)}, f32[1152,353]{0,1:T(8,128)S(1)}) fusion(), kind=kLoop, calls=%fused_computation.11 | loop fusion | flops 3659904 | bytes 3253248 | tf_op jit(solution)/shard_map/sin | solution.py:25
  19.4 1.2 copy.186
  21.4 1.4 slice.276
  22.8 0.9 copy.187
  23.8 1.4 collective-permute-done
  25.2 1.4 slice.275
  26.6 1.6 copy.185
  28.2 2.7 %fusion.37 = f32[192,12,18]{2,1,0:T(8,128)} fusion(f32[2,18,192]{1,0,2:T(2,128)S(1)} %copy.187, f32[8,18,192]{1,0,2:T(8,128)} %copy.186, f32[2,18,192]{1,0,2:T(2,128)} %copy.185), kind=kLoop, calls=%fused_computation.77 | loop fusion | flops 82944 | bytes 331776
  31.0 3.1 %reshape.157 = f32[64,1,648]{2,1,0:T(1,128)} reshape(f32[192,12,18]{2,1,0:T(8,128)} %fusion.37) | data formatting | bytes 331776
  34.0 25.0 %all-to-all-start = ((f32[64,1,648]{2,1,0:T(1,128)}), f32[64,1,648]{2,1,0:T(1,128)S(1)}, u32[]{:S(2)}, u32[]{:S(2)}) async-start(f32[64,1,648]{2,1,0:T(1,128)} %reshape.157), calls=%async_computation | async-start | bytes 393216 | tf_op jit(solution)/shard_map/all_to_all | solution.py:60
  61.3 17.8 %all-to-all-done = f32[64,1,648]{2,1,0:T(1,128)S(1)} async-done(((f32[64,1,648]{2,1,0:T(1,128)}), f32[64,1,648]{2,1,0:T(1,128)S(1)}, u32[]{:S(2)}, u32[]{:S(2)}) %all-to-all-start) | async-done | bytes 165920 | tf_op jit(solution)/shard_map/all_to_all | solution.py:60
  80.2 1.9 %reduce.4 = f32[64,648]{1,0:T(8,128)S(1)} reduce(f32[64,1,648]{2,1,0:T(1,128)} %copy-done.5, f32[]{:T(128)} %broadcast.142), dimensions={1}, to_apply=%all_to_all.26.reduce_sub_computation | reduce | bytes 331780 | tf_op jit(solution)/shard_map/all_to_all | solution.py:60
  82.1 1.9 %reshape.158 = f32[192,12,18]{2,1,0:T(8,128)} reshape(f32[64,648]{1,0:T(8,128)S(1)} %reduce.4) | data formatting | bytes 331776
  84.0 2.0 %copy.224 = f32[12,18,64,3]{1,3,2,0:T(4,128)S(1)} copy(f32[12,18,64,3]{1,0,3,2:T(8,128)} %bitcast.59) | data formatting | bytes 331776 | tf_op jit(solution)/shard_map/all_to_all | solution.py:60
  86.1 1.2 copy.189
  87.2 1.9 %all_to_all.29 = f32[12,1152,3]{1,0,2:T(8,128)S(1)} reshape(f32[12,64,18,3]{2,1,0,3:T(8,128)} %copy.189) | data formatting | bytes 331776 | tf_op jit(solution)/shard_map/all_to_all | solution.py:60
  89.1 3.7 %fusion.11 = f32[12,3,706]{2,0,1:T(8,128)S(1)} fusion(f32[12,1152,3]{1,0,2:T(8,128)S(1)} %all_to_all.29, f32[1152,353]{0,1:T(8,128)S(1)} %get-tuple-element.59, f32[1152,353]{0,1:T(8,128)S(1)} %get-tuple-element.60, f32[12,706]{1,0:T(8,128)} %pad_maximum_fusion.3), kind=kOutput, calls=%fused_computation.17 | convolution fusion | flops 352189504 | bytes 3554688 | tf_op jit(solution)/shard_map/dot_general | solution.py:71
  92.9 2.0 %fusion.3 = f32[12,1152,3]{1,0,2:T(8,128)S(1)} fusion(f32[12,1152,3]{1,0,2:T(8,128)S(1)} %all_to_all.29, f32[12,3,706]{2,0,1:T(8,128)S(1)} %fusion.11, f32[1152,353]{0,1:T(8,128)S(1)} %get-tuple-element.59, f32[1152,353]{0,1:T(8,128)S(1)} %get-tuple-element.60, pred[12]{0:T(512)(128)(4,1)S(1)} %copy-done.18), kind=kOutput, calls=%fused_computation.5 | convolution fusion | flops 352205568 | bytes 3686700 | tf_op jit(solution)/shard_map/dot_general | solution.py:75
  96.4 1.1 slice_select_fusion.1
  97.5 1.3 reshape.154
  99.4 1.8 %maximum_maximum_fusion = f32[12,64,22,3]{2,1,0,3:T(8,128)} fusion(f32[12,1,2,3]{2,1,0,3:T(1,128)S(1)} %get-tuple-element.34, f32[12,63,2,3]{2,1,0,3:T(8,128)S(1)} %get-tuple-element.36, f32[12,64,18,3]{2,1,0,3:T(8,128)S(1)} %reshape.154, f32[12,63,2,3]{2,1,0,3:T(8,128)S(1)} %get-tuple-element.35, f32[12,1,2,3]{2,1,0,3:T(1,128)S(1)} %get-tuple-element.33), kind=kLoop, calls=%fused_computation.16 | loop fusion | flops 202752 | bytes 405504 | tf_op jit(solution)/shard_map/concatenate | solution.py:90
  101.1 4.1 %copy.207 = f32[12,64,22,3]{0,3,2,1:T(4,128)S(1)} copy(f32[12,64,22,3]{2,1,0,3:T(8,128)} %maximum_maximum_fusion) | data formatting | bytes 405504 | tf_op jit(solution)/shard_map/reshape | solution.py:91
  105.2 2.6 %reshape.159 = f32[64,1,792]{2,1,0:T(1,128)} reshape(f32[1408,3,12]{2,1,0:T(4,128)S(1)} %bitcast.55) | data formatting | bytes 405504
  107.8 9.2 %all-to-all-start.1 = ((f32[64,1,792]{2,1,0:T(1,128)}), f32[64,1,792]{2,1,0:T(1,128)S(1)}, u32[]{:S(2)}, u32[]{:S(2)}) async-start(f32[64,1,792]{2,1,0:T(1,128)} %reshape.159), calls=%async_computation.1 | async-start | bytes 458752 | tf_op jit(solution)/shard_map/all_to_all | solution.py:92
  118.4 0.8 slice_select_fusion.2
  119.8 21.7 %all-to-all-done.1 = f32[64,1,792]{2,1,0:T(1,128)S(1)} async-done(((f32[64,1,792]{2,1,0:T(1,128)}), f32[64,1,792]{2,1,0:T(1,128)S(1)}, u32[]{:S(2)}, u32[]{:S(2)}) %all-to-all-start.1) | async-done | bytes 202784 | tf_op jit(solution)/shard_map/all_to_all | solution.py:92
  141.5 1.1 reduce.5
  142.6 1.9 %reshape.160 = f32[1408,3,12]{2,1,0:T(4,128)S(1)} reshape(f32[64,792]{1,0:T(8,128)S(1)} %reduce.5) | data formatting | bytes 405504
  144.5 3.3 %copy.208 = f32[12,64,22,3]{2,1,0,3:T(8,128)} copy(f32[12,64,22,3]{0,3,2,1:T(4,128)S(1)} %bitcast.56) | data formatting | bytes 405504 | tf_op jit(solution)/shard_map/all_to_all | solution.py:92
  147.8 1.3 slice.288
  149.3 0.8 copy.200
  150.6 1.1 slice.289
  151.7 2.1 %fusion.34 = (f32[8,19,192]{1,0,2:T(8,128)}, f32[8,19,192]{1,0,2:T(8,128)}, f32[8,19,192]{1,0,2:T(8,128)}, f32[8,19,192]{1,0,2:T(8,128)S(1)}) fusion(f32[8,22,192]{1,0,2:T(8,128)S(1)} %bitcast.54), kind=kLoop, calls=%fused_computation.74 | loop fusion | bytes 933888 | tf_op jit(solution)/shard_map/slice | solution.py:100
  154.4 2.3 %copy.212 = f32[8,18,192]{2,0,1:T(8,128)} copy(f32[8,18,192]{1,0,2:T(8,128)} %slice.289) | data formatting | bytes 221184
  156.7 2.1 %copy.216 = f32[8,19,192]{2,0,1:T(8,128)} copy(f32[8,19,192]{1,0,2:T(8,128)} %get-tuple-element.37) | data formatting | bytes 233472
  158.8 1.0 copy.215
  159.9 1.0 copy.214
  160.9 1.0 copy.213
  161.9 2.2 %fusion.31 = (f32[9,18,192]{1,2,0:T(8,128)}, f32[9,18,192]{1,2,0:T(8,128)}, f32[9,18,192]{1,2,0:T(8,128)S(1)}, f32[9,18,192]{1,2,0:T(8,128)S(1)}) fusion(f32[12,22,192]{1,2,0:T(8,128)S(1)} %all_to_all.33), kind=kLoop, calls=%fused_computation.71 | loop fusion | bytes 995328 | tf_op jit(solution)/shard_map/slice | solution.py:112
  164.1 1.9 %copy.220 = f32[9,18,192]{2,0,1:T(8,128)S(1)} copy(f32[9,18,192]{1,2,0:T(8,128)} %get-tuple-element.29) | data formatting | bytes 248832
  168.2 1.1 multiply_subtract_fusion
  169.5 0.7 fusion.20
  (83 shorter events, 13.8 us)
Async XLA Ops:
  0.7 117.7 %collective-permute-start.2 = (f32[8,1,192]{2,0,1:T(8,128)S(1)}, f32[8,1,192]{2,0,1:T(8,128)S(1)}, u32[]{:S(2)}, u32[]{:S(2)}) collective-permute-start(f32[8,1,192]{2,0,1:T(8,128)S(1)} %slice.258), channel_id=1, source_target_pairs={{0,1},{1,2},{2,3},{3,4},{4,5},{5,6},{6,7},{7,8},{8,9},{9,10},{10,1... | collective-permute-start | bytes 18440 | tf_op jit(solution)/shard_map/ppermute | solution.py:12
  6.0 14.6 %collective-permute-start.1 = (f32[3,18,192]{2,1,0:T(8,128)S(1)}, f32[3,18,192]{2,1,0:T(8,128)}, u32[]{:S(2)}, u32[]{:S(2)}) collective-permute-start(f32[3,18,192]{2,1,0:T(8,128)S(1)} %select_maximum_fusion.1), channel_id=1, source_target_pairs={{0,960},{64,0},{128,64},{192,128},{256,192},{320,256},{384,320},{4... | collective-permute-start | bytes 124424 | tf_op jit(solution)/shard_map/ppermute | solution.py:12
  9.6 9.8 %copy-start.10 = (f32[8,18,192]{2,0,1:T(8,128)S(1)}, f32[8,18,192]{2,0,1:T(8,128)}, u32[]{:S(2)}) copy-start(f32[8,18,192]{2,0,1:T(8,128)} %param.9) | copy-start | bytes 331780
  9.6 15.6 %collective-permute-start = (f32[4,18,192]{2,1,0:T(8,128)}, f32[4,18,192]{2,1,0:T(8,128)}, u32[]{:S(2)}, u32[]{:S(2)}) collective-permute-start(f32[4,18,192]{2,1,0:T(8,128)} %select_maximum_fusion), channel_id=1, source_target_pairs={{0,64},{64,128},{128,192},{192,256},{256,320},{320,384},{384,448},... | collective-permute-start | bytes 165896 | tf_op jit(solution)/shard_map/ppermute | solution.py:12
  30.9 28.9 %copy-start.16 = (s32[8]{0:T(128)S(1)}, s32[8]{0:T(128)}, u32[]{:S(2)}) copy-start(s32[8]{0:T(128)} %param.13) | copy-start | bytes 100
  30.9 29.5 %copy-start.17 = (s32[8]{0:T(128)S(1)}, s32[8]{0:T(128)}, u32[]{:S(2)}) copy-start(s32[8]{0:T(128)} %param.12) | copy-start | bytes 100
  31.0 29.5 %copy-start.15 = (f32[353]{0:T(512)S(1)}, f32[353]{0:T(512)}, u32[]{:S(2)}) copy-start(f32[353]{0:T(512)} %fusion.24) | copy-start | bytes 4240
  34.0 45.0 %all-to-all-start = ((f32[64,1,648]{2,1,0:T(1,128)}), f32[64,1,648]{2,1,0:T(1,128)S(1)}, u32[]{:S(2)}, u32[]{:S(2)}) async-start(f32[64,1,648]{2,1,0:T(1,128)} %reshape.157), calls=%async_computation | async-start | bytes 393216 | tf_op jit(solution)/shard_map/all_to_all | solution.py:60
  79.0 0.7 copy-start.5
  89.1 3.7 %copy-start.18 = (pred[12]{0:T(512)(128)(4,1)S(1)}, pred[12]{0:T(512)(128)(4,1)}, u32[]{:S(2)}) copy-start(pred[12]{0:T(512)(128)(4,1)} %add_compare_fusion) | copy-start | bytes 40
  94.9 0.7 copy-start.4
  105.2 13.2 %copy-start.13 = (f32[8,18,192]{2,0,1:T(8,128)S(1)}, f32[8,18,192]{2,0,1:T(8,128)}, u32[]{:S(2)}) copy-start(f32[8,18,192]{2,0,1:T(8,128)} %param.10) | copy-start | bytes 331780
  107.8 33.7 %all-to-all-start.1 = ((f32[64,1,792]{2,1,0:T(1,128)}), f32[64,1,792]{2,1,0:T(1,128)S(1)}, u32[]{:S(2)}, u32[]{:S(2)}) async-start(f32[64,1,792]{2,1,0:T(1,128)} %reshape.159), calls=%async_computation.1 | async-start | bytes 458752 | tf_op jit(solution)/shard_map/all_to_all | solution.py:92
  118.4 0.8 copy-start.12
  147.8 1.5 copy-start
  154.4 4.4 %copy-start.3 = (f32[8,19,192]{1,0,2:T(8,128)S(1)}, f32[8,19,192]{1,0,2:T(8,128)}, u32[]{:S(2)}) copy-start(f32[8,19,192]{1,0,2:T(8,128)} %get-tuple-element.38) | copy-start | bytes 350212
  154.4 5.5 %copy-start.2 = (f32[8,19,192]{1,0,2:T(8,128)S(1)}, f32[8,19,192]{1,0,2:T(8,128)}, u32[]{:S(2)}) copy-start(f32[8,19,192]{1,0,2:T(8,128)} %get-tuple-element.39) | copy-start | bytes 350212
  164.1 1.9 %copy-start.1 = (f32[9,18,192]{1,2,0:T(8,128)S(1)}, f32[9,18,192]{1,2,0:T(8,128)}, u32[]{:S(2)}) copy-start(f32[9,18,192]{1,2,0:T(8,128)} %get-tuple-element.30) | copy-start | bytes 373252
  166.0 2.1 %copy-start.6 = (f32[8,19,192]{2,0,1:T(8,128)S(1)}, f32[8,19,192]{2,0,1:T(8,128)}, u32[]{:S(2)}) copy-start(f32[8,19,192]{2,0,1:T(8,128)} %copy.216) | copy-start | bytes 350212
  166.0 2.1 %copy-start.7 = (f32[8,19,192]{2,0,1:T(8,128)S(1)}, f32[8,19,192]{2,0,1:T(8,128)}, u32[]{:S(2)}) copy-start(f32[8,19,192]{2,0,1:T(8,128)} %copy.215) | copy-start | bytes 350212
  166.7 1.4 copy-start.8
  166.7 2.5 %copy-start.14 = (f32[1,18,192]{2,0,1:T(1,128)S(1)}, f32[1,18,192]{2,0,1:T(1,128)}, u32[]{:S(2)}) copy-start(f32[1,18,192]{2,0,1:T(1,128)} %copy.199) | copy-start | bytes 41476
  166.8 2.5 %copy-start.20 = (f32[9]{0:T(128)S(1)}, f32[9]{0:T(128)}, u32[]{:S(2)}) copy-start(f32[9]{0:T(128)} %multiply_sine_fusion) | copy-start | bytes 112
  167.4 1.8 %copy-start.11 = (f32[8,18,192]{2,0,1:T(8,128)S(1)}, f32[8,18,192]{2,0,1:T(8,128)}, u32[]{:S(2)}) copy-start(f32[8,18,192]{2,0,1:T(8,128)} %param.11) | copy-start | bytes 331780
  167.5 2.0 %copy-start.9 = (f32[8,18,192]{2,0,1:T(8,128)S(1)}, f32[8,18,192]{2,0,1:T(8,128)}, u32[]{:S(2)}) copy-start(f32[8,18,192]{2,0,1:T(8,128)} %copy.212) | copy-start | bytes 331780
  167.5 2.0 %copy-start.19 = (f32[8]{0:T(128)S(1)}, f32[8]{0:T(128)}, u32[]{:S(2)}) copy-start(f32[8]{0:T(128)} %fusion.28) | copy-start | bytes 100

commit v3 on v1

v3 whole, which is shorter than its diff:
```python
import math

import jax
import jax.numpy as jnp
from jax import lax
from jax.sharding import PartitionSpec as P


def shifted_from(block, axis, distance):
    count = lax.axis_size(axis)
    route = [(i, (i + distance) % count) for i in range(count)]
    return lax.ppermute(block, axis, route)


def face_flux(far_lo, near_lo, near_hi, far_hi, courant):
    centred = (7.0 * (near_lo + near_hi) - (far_lo + far_hi)) / 12.0
    return courant * centred - 0.5 * jnp.abs(courant) * (near_hi - near_lo)


def build_table(n_full, n_waves):
    points = jnp.arange(n_full, dtype=jnp.int32)
    waves = jnp.arange(n_waves, dtype=jnp.int32)
    phase = points[:, None] * waves[None, :] % n_full
    angle = phase.astype(jnp.float32) * (2.0 * math.pi / n_full)
    return jnp.concatenate([jnp.cos(angle), jnp.sin(angle)], axis=1)


def local(state, courant_east, courant_north, cutoff, filter_mask):
    n_rows, n_cols, n_comp = state.shape
    lon_count = lax.axis_size("lon")
    lat_count = lax.axis_size("lat")
    lat_index = lax.axis_index("lat")
    n_full = n_cols * lon_count
    n_lat = n_rows * lat_count
    half = n_full // 2

    top = n_full // 8 + (half - 1 - n_full // 8) * (n_lat // 4 - 1) // (n_lat // 2)
    n_waves = min(top, half - 1) + 1

    east_halo = shifted_from(courant_east[:, -1:], "lon", 1)
    north_halo = shifted_from(courant_north[-1:], "lat", 1)

    lines = lax.all_to_all(state, "lon", split_axis=2, concat_axis=1, tiled=True)
    fourier = build_table(n_full, n_waves)
    waves = jnp.arange(n_waves, dtype=jnp.int32)
    weights = jnp.where(waves == 0, 1.0 / n_full, 2.0 / n_full).astype(jnp.float32)
    kept = jnp.where(waves[None, :] <= cutoff[:, None], weights[None, :], 0.0)
    kept_both = jnp.concatenate([kept, kept], axis=1)
    coeffs = lax.dot_general(
        lines, fourier, (((1,), (0,)), ((), ())), precision=lax.Precision.HIGHEST
    )
    coeffs = coeffs * kept_both[:, None, :]
    synth = lax.dot_general(
        coeffs, fourier, (((2,), (1,)), ((), ())), precision=lax.Precision.HIGHEST
    )
    filtered = jnp.transpose(synth, (0, 2, 1))
    merged = jnp.where(filter_mask[:, None, None] == 1, filtered, lines)
    smooth = lax.all_to_all(merged, "lon", split_axis=1, concat_axis=2, tiled=True)

    from_south = shifted_from(smooth[-2:], "lat", 1)
    from_north = shifted_from(smooth[:2], "lat", -1)
    from_west = shifted_from(smooth[:, -2:], "lon", 1)
    from_east = shifted_from(smooth[:, :2], "lon", -1)
    poles = jnp.concatenate([smooth[1::-1], smooth[:-3:-1]], axis=0)
    partner = shifted_from(poles, "lon", lon_count // 2)

    zonal_p = jnp.concatenate([from_west, smooth, from_east], axis=1)
    zonal_c = jnp.concatenate([east_halo, courant_east], axis=1)
    east = face_flux(
        zonal_p[:, 0 : n_cols + 1],
        zonal_p[:, 1 : n_cols + 2],
        zonal_p[:, 2 : n_cols + 3],
        zonal_p[:, 3 : n_cols + 4],
        zonal_c,
    )
    zonal = -(east[:, 1:] - east[:, :-1])

    south = jnp.where(lat_index == 0, partner[:2], from_south)
    north = jnp.where(lat_index == lat_count - 1, partner[2:], from_north)
    merid_p = jnp.concatenate([south, smooth, north], axis=0)
    south_c = jnp.where(lat_index == 0, 0.0, north_halo)
    merid_c = jnp.concatenate([south_c, courant_north], axis=0)
    north_flux = face_flux(
        merid_p[0 : n_rows + 1],
        merid_p[1 : n_rows + 2],
        merid_p[2 : n_rows + 3],
        merid_p[3 : n_rows + 4],
        merid_c,
    )
    face_rows = lat_index * n_rows + jnp.arange(-1, n_rows, dtype=jnp.int32)
    cos_face = jnp.sin(
        jnp.minimum(face_rows + 1, n_lat - 1 - face_rows).astype(jnp.float32) * (math.pi / n_lat)
    )
    cell_rows = face_rows[1:]
    cos_cell = jnp.sin(
        (jnp.minimum(cell_rows, n_lat - 1 - cell_rows).astype(jnp.float32) + 0.5)
        * (math.pi / n_lat)
    )
    weighted = cos_face[:, None, None] * north_flux
    meridional = -(weighted[1:] - weighted[:-1]) / cos_cell[:, None, None]
    return smooth + zonal + meridional


def solution(mesh):
    placed = (
        P("lat", "lon", None),
        P("lat", "lon", None),
        P("lat", "lon", None),
        P("lat"),
        P("lat"),
    )
    return jax.shard_map(
        local, mesh=mesh, in_specs=placed, out_specs=P("lat", "lon", None), check_vma=False
    )
```

time: 160 us -> 154 us (0.963)
  the two profiles are of different devices: /device:TPU:8 before, /device:TPU:62 now
where the time goes in v3:
time: 154 us; the launch traced here: 153 us
  starting transfers between devices  86.9 us (56%)
  waiting for transfers between devices  26.8 us (17%)
  local copies, waits for them, and re-layouts  21.4 us (14%)
  other arithmetic  12.7 us (8%)
  matrix products  4.95 us (3%)
    ppermute x7, starting transfers between devices, shifted_from(): return lax.ppermute(block, axis, route)  49.1 us
    all_to_all x1, starting transfers between devices, local(): lax.all_to_all(state, 'lon', split_axis=2, concat_axis=1, tiled=True)  26.8 us
    all_to_all x1, waiting for transfers between devices, local(): lax.all_to_all(merged, 'lon', split_axis=1, concat_axis=2, tiled=True)  16 us
    all_to_all x1, starting transfers between devices, local(): lax.all_to_all(merged, 'lon', split_axis=1, concat_axis=2, tiled=True)  11 us
    ppermute x7, waiting for transfers between devices, shifted_from(): return lax.ppermute(block, axis, route)  10.8 us
    unnamed x22, local copies, waits for them, and re-layouts  8.25 us
    sin x1, other arithmetic, build_table(): return jnp.concatenate([jnp.cos(angle), jnp.sin(angle)], axis=1)  6.67 us
    all_to_all x3, local copies, waits for them, and re-layouts, local(): lax.all_to_all(state, 'lon', split_axis=2, concat_axis=1, tiled=True)  4.22 us
  transfers between devices with their start and end apart: 9, of which 2 were waited for; matrix products, arithmetic and copies ran while one was open for 19% of the time, Pallas kernels for 0%

profile of v3, /device:TPU:62, one launch (start us, length us, event | category | flops | bytes accessed | tf_op | source)
XLA Modules:
  0.0 153.2 jit_solution(8298702822881010567)
XLA Ops:
  0.0 1.3 copy.103
  1.3 1.6 %reshape.24 = f32[64,1,432]{2,1,0:T(1,128)} reshape(f32[192,8,18]{2,1,0:T(8,128)S(1)} %bitcast.46) | data formatting | bytes 221184
  2.9 26.8 %all-to-all-start = ((f32[64,1,432]{2,1,0:T(1,128)}), f32[64,1,432]{2,1,0:T(1,128)S(1)}, u32[]{:S(2)}, u32[]{:S(2)}) async-start(f32[64,1,432]{2,1,0:T(1,128)} %reshape.24), calls=%async_computation | async-start | bytes 262144 | tf_op jit(solution)/shard_map/all_to_all | solution.py:43
  29.7 1.5 slice.88
  31.2 1.9 %collective-permute-start.3 = (f32[1,18,192]{2,0,1:T(1,128)}, f32[1,18,192]{2,0,1:T(1,128)}, u32[]{:S(2)}, u32[]{:S(2)}) collective-permute-start(f32[1,18,192]{2,0,1:T(1,128)} %slice.88), channel_id=1, source_target_pairs={{0,64},{64,128},{128,192},{192,256},{256,320},{320,384},{384,448},... | collective-permute-start | bytes 41480 | tf_op jit(solution)/shard_map/ppermute | solution.py:12
  33.1 0.7 slice.79
  33.8 12.1 %collective-permute-start = (f32[8,1,192]{2,0,1:T(8,128)S(1)}, f32[8,1,192]{2,0,1:T(8,128)S(1)}, u32[]{:S(2)}, u32[]{:S(2)}) collective-permute-start(f32[8,1,192]{2,0,1:T(8,128)S(1)} %slice.79), channel_id=1, source_target_pairs={{0,1},{1,2},{2,3},{3,4},{4,5},{5,6},{6,7},{7,8},{8,9},{9,10},{10,1... | collective-permute-start | bytes 18440 | tf_op jit(solution)/shard_map/ppermute | solution.py:12
  45.9 0.1 fusion.34
  46.0 0.1 pad_maximum_fusion.6
  46.1 0.6 broadcast_compare_fusion
  46.7 0.6 fusion.39
  47.3 0.6 multiply_sine_fusion
  47.9 6.7 %fusion.8 = (f32[1152,353]{0,1:T(8,128)S(1)}, f32[1152,353]{0,1:T(8,128)S(1)}) fusion(), kind=kLoop, calls=%fused_computation.11 | loop fusion | flops 3659904 | bytes 3253248 | tf_op jit(solution)/shard_map/sin | solution.py:25
  54.6 0.6 copy-done
  55.3 0.5 broadcast.83
  55.8 1.9 %reduce = f32[64,432]{1,0:T(8,128)S(1)} reduce(f32[64,1,432]{2,1,0:T(1,128)} %copy-done, f32[]{:T(128)} %broadcast.83), dimensions={1}, to_apply=%all_to_all.26.reduce_sub_computation | reduce | bytes 221188 | tf_op jit(solution)/shard_map/all_to_all | solution.py:43
  57.7 1.2 reshape.25
  58.9 2.2 %copy.104 = f32[8,64,18,3]{2,1,0,3:T(8,128)} copy(f32[8,64,18,3]{2,0,3,1:T(8,128)} %bitcast.45) | data formatting | bytes 221184 | tf_op jit(solution)/shard_map/all_to_all | solution.py:43
  61.1 1.5 all_to_all.29
  62.6 3.0 %fusion.12 = f32[8,3,706]{2,0,1:T(8,128)S(1)} fusion(f32[8,1152,3]{1,0,2:T(8,128)S(1)} %all_to_all.29, f32[1152,353]{0,1:T(8,128)S(1)} %get-tuple-element.11, f32[1152,353]{0,1:T(8,128)S(1)} %get-tuple-element.12, f32[8,706]{1,0:T(8,128)S(1)} %pad_maximum_fusion.6), kind=kOutput, calls=%fused_computation.15 | convolution fusion | flops 235064112 | bytes 3454208 | tf_op jit(solution)/shard_map/dot_general | solution.py:49
  65.6 2.0 %fusion.3 = f32[8,1152,3]{1,0,2:T(8,128)S(1)} fusion(f32[8,1152,3]{1,0,2:T(8,128)S(1)} %all_to_all.29, f32[8,3,706]{2,0,1:T(8,128)S(1)} %fusion.12, f32[1152,353]{0,1:T(8,128)S(1)} %get-tuple-element.11, f32[1152,353]{0,1:T(8,128)S(1)} %get-tuple-element.12, pred[8]{0:T(512)(128)(4,1)S(1)} %copy-done.6), kind=kOutput, calls=%fused_computation.5 | convolution fusion | flops 235074816 | bytes 3542216 | tf_op jit(solution)/shard_map/dot_general | solution.py:53
  67.6 1.5 copy.105
  69.1 2.2 %reshape.26 = f32[64,1,432]{2,1,0:T(1,128)} reshape(f32[1152,3,8]{2,1,0:T(4,128)S(1)} %bitcast.44) | data formatting | bytes 221184
  71.3 11.0 %all-to-all-start.1 = ((f32[64,1,432]{2,1,0:T(1,128)}), f32[64,1,432]{2,1,0:T(1,128)S(1)}, u32[]{:S(2)}, u32[]{:S(2)}) async-start(f32[64,1,432]{2,1,0:T(1,128)} %reshape.26), calls=%async_computation.1 | async-start | bytes 262144 | tf_op jit(solution)/shard_map/all_to_all | solution.py:58
  82.4 16.0 %all-to-all-done.1 = f32[64,1,432]{2,1,0:T(1,128)S(1)} async-done(((f32[64,1,432]{2,1,0:T(1,128)}), f32[64,1,432]{2,1,0:T(1,128)S(1)}, u32[]{:S(2)}, u32[]{:S(2)}) %all-to-all-start.1) | async-done | bytes 110624 | tf_op jit(solution)/shard_map/all_to_all | solution.py:58
  98.4 0.9 reduce.1
  99.4 1.3 reshape.27
  100.6 1.5 %copy.122 = f32[8,64,18,3]{2,1,0,3:T(8,128)S(1)} copy(f32[8,64,18,3]{0,3,2,1:T(4,128)S(1)} %bitcast.40) | data formatting | bytes 221184 | tf_op jit(solution)/shard_map/all_to_all | solution.py:58
  102.2 0.2 copy.115
  102.4 0.1 copy.116
  102.5 1.9 %collective-permute-start.5 = (f32[2,18,192]{2,0,1:T(2,128)S(1)}, f32[2,18,192]{2,0,1:T(2,128)S(1)}, u32[]{:S(2)}, u32[]{:S(2)}) collective-permute-start(f32[2,18,192]{2,0,1:T(2,128)S(1)} %copy.116), channel_id=1, source_target_pairs={{0,64},{64,128},{128,192},{192,256},{256,320},{320,384},{384,448},... | collective-permute-start | bytes 82952 | tf_op jit(solution)/shard_map/ppermute | solution.py:12
  104.4 0.2 rev.7
  104.6 0.2 copy.113
  104.8 0.1 copy.114
  104.9 0.2 rev.6
  105.1 10.2 %collective-permute-start.6 = (f32[2,18,192]{2,0,1:T(2,128)S(1)}, f32[2,18,192]{2,0,1:T(2,128)S(1)}, u32[]{:S(2)}, u32[]{:S(2)}) collective-permute-start(f32[2,18,192]{2,0,1:T(2,128)S(1)} %copy.114), channel_id=1, source_target_pairs={{0,960},{64,0},{128,64},{192,128},{256,192},{320,256},{384,320},{4... | collective-permute-start | bytes 82952 | tf_op jit(solution)/shard_map/ppermute | solution.py:12
  115.3 1.4 copy.123
  116.7 0.3 fusion.42
  117.0 0.4 copy.110
  117.4 3.2 %collective-permute-start.2 = (f32[8,2,192]{2,0,1:T(8,128)S(1)}, f32[8,2,192]{2,0,1:T(8,128)S(1)}, u32[]{:S(2)}, u32[]{:S(2)}) collective-permute-start(f32[8,2,192]{2,0,1:T(8,128)S(1)} %copy.110), channel_id=1, source_target_pairs={{0,63},{1,0},{2,1},{3,2},{4,3},{5,4},{6,5},{7,6},{8,7},{9,8},{10,9... | collective-permute-start | bytes 36872 | tf_op jit(solution)/shard_map/ppermute | solution.py:12
  120.5 0.4 copy.108
  120.9 15.8 %collective-permute-start.1 = (f32[8,2,192]{2,0,1:T(8,128)S(1)}, f32[8,2,192]{2,0,1:T(8,128)S(1)}, u32[]{:S(2)}, u32[]{:S(2)}) collective-permute-start(f32[8,2,192]{2,0,1:T(8,128)S(1)} %copy.108), channel_id=1, source_target_pairs={{0,1},{1,2},{2,3},{3,4},{4,5},{5,6},{6,7},{7,8},{8,9},{9,10},{10,1... | collective-permute-start | bytes 36872 | tf_op jit(solution)/shard_map/ppermute | solution.py:12
  136.7 0.4 copy.112
  137.1 4.1 %collective-permute-start.4 = (f32[4,18,192]{2,0,1:T(4,128)S(1)}, f32[4,18,192]{2,0,1:T(4,128)S(1)}, u32[]{:S(2)}, u32[]{:S(2)}) collective-permute-start(f32[4,18,192]{2,0,1:T(4,128)S(1)} %pad_maximum_fusion.5), channel_id=1, source_target_pairs={{0,32},{1,33},{2,34},{3,35},{4,36},{5,37},{6,38},{7,39},{8,40},{9,... | collective-permute-start | bytes 165896 | tf_op jit(solution)/shard_map/ppermute | solution.py:12
  141.2 0.1 fusion.28
  141.3 10.8 %collective-permute-done.4 = f32[4,18,192]{2,0,1:T(4,128)S(1)} collective-permute-done((f32[4,18,192]{2,0,1:T(4,128)S(1)}, f32[4,18,192]{2,0,1:T(4,128)S(1)}, u32[]{:S(2)}, u32[]{:S(2)}) %collective-permute-start.4) | collective-permute-done | bytes 55328 | tf_op jit(solution)/shard_map/ppermute | solution.py:12
  152.1 0.3 fusion.18
  152.4 0.8 fusion.31
  (30 shorter events, 0.2 us)
Async XLA Ops:
  0.0 45.9 %copy-start.5 = (s32[8]{0:T(128)S(1)}, s32[8]{0:T(128)}, u32[]{:S(2)}) copy-start(s32[8]{0:T(128)} %param.8) | copy-start | bytes 100
  0.0 46.1 %copy-start.7 = (s32[8]{0:T(128)S(1)}, s32[8]{0:T(128)}, u32[]{:S(2)}) copy-start(s32[8]{0:T(128)} %param.9) | copy-start | bytes 100
  2.9 51.7 %all-to-all-start = ((f32[64,1,432]{2,1,0:T(1,128)}), f32[64,1,432]{2,1,0:T(1,128)S(1)}, u32[]{:S(2)}, u32[]{:S(2)}) async-start(f32[64,1,432]{2,1,0:T(1,128)} %reshape.24), calls=%async_computation | async-start | bytes 262144 | tf_op jit(solution)/shard_map/all_to_all | solution.py:43
  31.2 51.1 %collective-permute-start.3 = (f32[1,18,192]{2,0,1:T(1,128)}, f32[1,18,192]{2,0,1:T(1,128)}, u32[]{:S(2)}, u32[]{:S(2)}) collective-permute-start(f32[1,18,192]{2,0,1:T(1,128)} %slice.88), channel_id=1, source_target_pairs={{0,64},{64,128},{128,192},{192,256},{256,320},{320,384},{384,448},... | collective-permute-start | bytes 41480 | tf_op jit(solution)/shard_map/ppermute | solution.py:12
  33.8 48.4 %collective-permute-start = (f32[8,1,192]{2,0,1:T(8,128)S(1)}, f32[8,1,192]{2,0,1:T(8,128)S(1)}, u32[]{:S(2)}, u32[]{:S(2)}) collective-permute-start(f32[8,1,192]{2,0,1:T(8,128)S(1)} %slice.79), channel_id=1, source_target_pairs={{0,1},{1,2},{2,3},{3,4},{4,5},{5,6},{6,7},{7,8},{8,9},{9,10},{10,1... | collective-permute-start | bytes 18440 | tf_op jit(solution)/shard_map/ppermute | solution.py:12
  54.6 0.7 copy-start
  62.6 3.0 %copy-start.6 = (pred[8]{0:T(512)(128)(4,1)S(1)}, pred[8]{0:T(512)(128)(4,1)}, u32[]{:S(2)}) copy-start(pred[8]{0:T(512)(128)(4,1)} %broadcast_compare_fusion) | copy-start | bytes 28
  69.0 13.2 %copy-start.2 = (f32[8,18,192]{2,0,1:T(8,128)S(1)}, f32[8,18,192]{2,0,1:T(8,128)}, u32[]{:S(2)}) copy-start(f32[8,18,192]{2,0,1:T(8,128)} %param.6) | copy-start | bytes 331780
  71.3 27.1 %all-to-all-start.1 = ((f32[64,1,432]{2,1,0:T(1,128)}), f32[64,1,432]{2,1,0:T(1,128)S(1)}, u32[]{:S(2)}, u32[]{:S(2)}) async-start(f32[64,1,432]{2,1,0:T(1,128)} %reshape.26), calls=%async_computation.1 | async-start | bytes 262144 | tf_op jit(solution)/shard_map/all_to_all | solution.py:58
  102.5 38.8 %collective-permute-start.5 = (f32[2,18,192]{2,0,1:T(2,128)S(1)}, f32[2,18,192]{2,0,1:T(2,128)S(1)}, u32[]{:S(2)}, u32[]{:S(2)}) collective-permute-start(f32[2,18,192]{2,0,1:T(2,128)S(1)} %copy.116), channel_id=1, source_target_pairs={{0,64},{64,128},{128,192},{192,256},{256,320},{320,384},{384,448},... | collective-permute-start | bytes 82952 | tf_op jit(solution)/shard_map/ppermute | solution.py:12
  105.1 36.2 %collective-permute-start.6 = (f32[2,18,192]{2,0,1:T(2,128)S(1)}, f32[2,18,192]{2,0,1:T(2,128)S(1)}, u32[]{:S(2)}, u32[]{:S(2)}) collective-permute-start(f32[2,18,192]{2,0,1:T(2,128)S(1)} %copy.114), channel_id=1, source_target_pairs={{0,960},{64,0},{128,64},{192,128},{256,192},{320,256},{384,320},{4... | collective-permute-start | bytes 82952 | tf_op jit(solution)/shard_map/ppermute | solution.py:12
  117.0 35.1 %copy-start.1 = (f32[8,18,192]{2,0,1:T(8,128)S(1)}, f32[8,18,192]{2,0,1:T(8,128)}, u32[]{:S(2)}) copy-start(f32[8,18,192]{2,0,1:T(8,128)} %param.7) | copy-start | bytes 331780
  117.0 35.1 %copy-start.4 = (f32[9]{0:T(128)S(1)}, f32[9]{0:T(128)}, u32[]{:S(2)}) copy-start(f32[9]{0:T(128)} %multiply_sine_fusion) | copy-start | bytes 112
  117.4 35.0 %copy-start.3 = (f32[8]{0:T(128)S(1)}, f32[8]{0:T(128)}, u32[]{:S(2)}) copy-start(f32[8]{0:T(128)} %fusion.39) | copy-start | bytes 100
  117.4 23.8 %collective-permute-start.2 = (f32[8,2,192]{2,0,1:T(8,128)S(1)}, f32[8,2,192]{2,0,1:T(8,128)S(1)}, u32[]{:S(2)}, u32[]{:S(2)}) collective-permute-start(f32[8,2,192]{2,0,1:T(8,128)S(1)} %copy.110), channel_id=1, source_target_pairs={{0,63},{1,0},{2,1},{3,2},{4,3},{5,4},{6,5},{7,6},{8,7},{9,8},{10,9... | collective-permute-start | bytes 36872 | tf_op jit(solution)/shard_map/ppermute | solution.py:12
  120.9 20.3 %collective-permute-start.1 = (f32[8,2,192]{2,0,1:T(8,128)S(1)}, f32[8,2,192]{2,0,1:T(8,128)S(1)}, u32[]{:S(2)}, u32[]{:S(2)}) collective-permute-start(f32[8,2,192]{2,0,1:T(8,128)S(1)} %copy.108), channel_id=1, source_target_pairs={{0,1},{1,2},{2,3},{3,4},{4,5},{5,6},{6,7},{7,8},{8,9},{9,10},{10,1... | collective-permute-start | bytes 36872 | tf_op jit(solution)/shard_map/ppermute | solution.py:12
  137.1 15.0 %collective-permute-start.4 = (f32[4,18,192]{2,0,1:T(4,128)S(1)}, f32[4,18,192]{2,0,1:T(4,128)S(1)}, u32[]{:S(2)}, u32[]{:S(2)}) collective-permute-start(f32[4,18,192]{2,0,1:T(4,128)S(1)} %pad_maximum_fusion.5), channel_id=1, source_target_pairs={{0,32},{1,33},{2,34},{3,35},{4,36},{5,37},{6,38},{7,39},{8,40},{9,... | collective-permute-start | bytes 165896 | tf_op jit(solution)/shard_map/ppermute | solution.py:12

commit v4 on v2

--- a/solution.py
+++ b/solution.py
@@ -25,7 +25,7 @@
     return jnp.concatenate([jnp.cos(angle), jnp.sin(angle)], axis=1)
 
 
-def local(state, courant_east, courant_north, cutoff_all, mask_all):
+def local(state, courant_east, courant_north, cutoff, filter_mask):
     n_rows, n_cols, n_comp = state.shape
     lon_count = lax.axis_size("lon")
     lat_count = lax.axis_size("lat")
@@ -34,12 +34,14 @@
     n_lat = n_rows * lat_count
     half = n_full // 2
     group = n_comp // lon_count
+    n_ext = n_rows + 4
+    n_win = n_cols + 4
 
     top = n_full // 8 + (half - 1 - n_full // 8) * (n_lat // 4 - 1) // (n_lat // 2)
     n_waves = min(top, half - 1) + 1
 
     def row_info(sel):
-        whole = jnp.concatenate([cutoff_all[sel], mask_all[sel]]).astype(jnp.float32)
+        whole = jnp.concatenate([cutoff[sel], filter_mask[sel]]).astype(jnp.float32)
         blank = jnp.zeros((1, n_cols, n_comp), jnp.float32)
         return blank.at[0, 0, : whole.shape[0]].set(whole)
 
@@ -56,40 +58,42 @@
     east_halo = shifted_from(courant_east[:, -1:], "lon", 1)
 
     rows_ext = jnp.concatenate([from_south[:2], state, from_north[:2]], axis=0)
-    n_ext = n_rows + 4
-    lines = lax.all_to_all(rows_ext, "lon", split_axis=2, concat_axis=1, tiled=True)
+    outgoing = rows_ext.reshape(n_ext * n_cols, n_comp).T.reshape(lon_count, -1)
+    incoming = lax.all_to_all(outgoing, "lon", split_axis=0, concat_axis=0, tiled=True)
+    lines = incoming.reshape(lon_count, group * n_ext, n_cols)
+    lines = jnp.transpose(lines, (1, 0, 2)).reshape(group * n_ext, n_full)
+
+    info_s = from_south[3, 0, :4].astype(jnp.int32)
+    info_n = from_north[2, 0, :4].astype(jnp.int32)
+    cut_ext = jnp.concatenate([info_s[:2], cutoff, info_n[:2]])
+    mask_ext = jnp.concatenate([info_s[2:], filter_mask, info_n[2:]])
 
     fourier = build_table(n_full, n_waves)
     waves = jnp.arange(n_waves, dtype=jnp.int32)
     weights = jnp.where(waves == 0, 1.0 / n_full, 2.0 / n_full).astype(jnp.float32)
-    info_s = from_south[3, 0, :4].astype(jnp.int32)
-    info_n = from_north[2, 0, :4].astype(jnp.int32)
-    cut_ext = jnp.concatenate([info_s[:2], cutoff_all, info_n[:2]])
-    mask_ext = jnp.concatenate([info_s[2:], mask_all, info_n[2:]])
     kept = jnp.where(waves[None, :] <= cut_ext[:, None], weights[None, :], 0.0)
-    kept_both = jnp.concatenate([kept, kept], axis=1)
-    coeffs = lax.dot_general(
-        lines, fourier, (((1,), (0,)), ((), ())), precision=lax.Precision.HIGHEST
+    kept_both = jnp.tile(jnp.concatenate([kept, kept], axis=1), (group, 1))
+    coeffs = jnp.dot(lines, fourier, precision=lax.Precision.HIGHEST)
+    coeffs = coeffs * kept_both
+    filtered = lax.dot_general(
+        coeffs, fourier, (((1,), (1,)), ((), ())), precision=lax.Precision.HIGHEST
     )
-    coeffs = coeffs * kept_both[:, None, :]
-    synth = lax.dot_general(
-        coeffs, fourier, (((2,), (1,)), ((), ())), precision=lax.Precision.HIGHEST
-    )
-    filtered = jnp.transpose(synth, (0, 2, 1))
-    smooth = jnp.where(mask_ext[:, None, None] == 1, filtered, lines)
+    keep = jnp.tile(mask_ext, group)[:, None] == 1
+    smooth = jnp.where(keep, filtered, lines).reshape(group, n_ext, n_full)
 
-    south_pole = jnp.roll(smooth[3:1:-1], half, axis=1)
-    north_pole = jnp.roll(smooth[n_ext - 3 : n_ext - 5 : -1], half, axis=1)
-    low = jnp.where(lat_index == 0, south_pole, smooth[:2])
-    high = jnp.where(lat_index == lat_count - 1, north_pole, smooth[-2:])
-    smooth = jnp.concatenate([low, smooth[2:-2], high], axis=0)
+    south_pole = jnp.roll(smooth[:, 3:1:-1], half, axis=2)
+    north_pole = jnp.roll(smooth[:, n_ext - 3 : n_ext - 5 : -1], half, axis=2)
+    low = jnp.where(lat_index == 0, south_pole, smooth[:, :2])
+    high = jnp.where(lat_index == lat_count - 1, north_pole, smooth[:, -2:])
+    smooth = jnp.concatenate([low, smooth[:, 2:-2], high], axis=1)
 
-    tiles = smooth.reshape(n_ext, lon_count, n_cols, group)
-    left = jnp.roll(tiles[:, :, -2:], 1, axis=1)
-    right = jnp.roll(tiles[:, :, :2], -1, axis=1)
-    windows = jnp.concatenate([left, tiles, right], axis=2)
-    windows = windows.reshape(n_ext, lon_count * (n_cols + 4), group)
-    ext = lax.all_to_all(windows, "lon", split_axis=1, concat_axis=2, tiled=True)
+    tiles = smooth.reshape(group, n_ext, lon_count, n_cols)
+    left = jnp.roll(tiles[..., -2:], 1, axis=2)
+    right = jnp.roll(tiles[..., :2], -1, axis=2)
+    windows = jnp.concatenate([left, tiles, right], axis=3)
+    windows = jnp.transpose(windows, (2, 0, 1, 3)).reshape(lon_count, -1)
+    back = lax.all_to_all(windows, "lon", split_axis=0, concat_axis=0, tiled=True)
+    ext = back.reshape(n_comp, n_ext * n_win).T.reshape(n_ext, n_win, n_comp)
 
     zonal_p = ext[2:-2]
     zonal_c = jnp.concatenate([east_halo, courant_east], axis=1)

time: 171 us -> 134 us (0.78)
  local copies, waits for them, and re-layouts: 57.4 us -> 32.2 us
  other arithmetic: 23.6 us -> 14.6 us
  waiting for transfers between devices: 40.9 us -> 36.6 us
  matrix products: 5.72 us -> 7.5 us
    unnamed x60 -> x21, local copies, waits for them, and re-layouts: 23.6 us -> 1.05 us
    all_to_all x7 -> x4, local copies, waits for them, and re-layouts: 10.2 us -> 4.64 us  [the longest x2 3.74 us: local(): lax.all_to_all(outgoing, 'lon', split_axis=0, concat_axis=0, tiled=True)]
    transpose x0 -> x3, local copies, waits for them, and re-layouts: none -> 4.34 us  [the longest x1 2.47 us: local(): lines = jnp.transpose(lines, (1, 0, 2)).reshape(group * n_ext, n_full)]
    reshape x2 -> x8, local copies, waits for them, and re-layouts: 5.36 us -> 9.6 us  [the longest x1 2.53 us: local(): lines = jnp.transpose(lines, (1, 0, 2)).reshape(group * n_ext, n_full)]
    slice x4 -> x3, local copies, waits for them, and re-layouts: 5.4 us -> 1.72 us  [local(): rows_ext = jnp.concatenate([from_south[:2], state, from_north[:2]], axis=0)]
    all_to_all x2, waiting for transfers between devices: 39.5 us -> 36.6 us  [the longest x1 19.7 us: local(): lax.all_to_all(windows, 'lon', split_axis=0, concat_axis=0, tiled=True)]
    unnamed x1, other arithmetic: 2.71 us -> 0.08 us
    all_to_all x2 -> x1, other arithmetic: 3.03 us -> 0.54 us  [local(): lax.all_to_all(windows, 'lon', split_axis=0, concat_axis=0, tiled=True)]
  transfers between devices with their start and end apart: 5 -> 5, of which waited for: 3 -> 2; matrix products, arithmetic and copies ran while one was open for 32% -> 13% of each run, Pallas kernels for 0% -> 0%
where the time goes in v4:
time: 134 us; the launch traced here: 133 us
  starting transfers between devices  41.4 us (31%)
  waiting for transfers between devices  36.6 us (27%)
  local copies, waits for them, and re-layouts  32.2 us (24%)
  other arithmetic  14.6 us (11%)
  matrix products  7.5 us (6%)
    all_to_all x1, starting transfers between devices, local(): lax.all_to_all(outgoing, 'lon', split_axis=0, concat_axis=0, tiled=True)  27 us
    all_to_all x1, waiting for transfers between devices, local(): lax.all_to_all(windows, 'lon', split_axis=0, concat_axis=0, tiled=True)  19.7 us
    all_to_all x1, waiting for transfers between devices, local(): lax.all_to_all(outgoing, 'lon', split_axis=0, concat_axis=0, tiled=True)  16.9 us
    ppermute x3, starting transfers between devices, shifted_from(): return lax.ppermute(block, axis, route)  9.02 us
    sin x1, other arithmetic, build_table(): return jnp.concatenate([jnp.cos(angle), jnp.sin(angle)], axis=1)  7.12 us
    all_to_all x1, starting transfers between devices, local(): lax.all_to_all(windows, 'lon', split_axis=0, concat_axis=0, tiled=True)  5.37 us
    dot_general x1, matrix products, local(): lax.dot_general(coeffs, fourier, (((1,), (1,)), ((), ())), precision=lax....  4 us
    all_to_all x2, local copies, waits for them, and re-layouts, local(): lax.all_to_all(outgoing, 'lon', split_axis=0, concat_axis=0, tiled=True)  3.74 us
  transfers between devices with their start and end apart: 5, of which 2 were waited for; matrix products, arithmetic and copies ran while one was open for 13% of the time, Pallas kernels for 0%

profile of v4, /device:TPU:64, one launch (start us, length us, event | category | flops | bytes accessed | tf_op | source)
XLA Modules:
  0.0 132.6 jit_solution(853670791738029670)
XLA Ops:
  0.0 1.0 copy.25
  1.0 1.1 fusion.37
  2.1 0.8 slice_bitcast_fusion.6
  3.0 0.7 select_maximum_fusion
  3.6 1.9 %collective-permute-start = (f32[4,18,192]{2,1,0:T(8,128)}, f32[4,18,192]{2,1,0:T(8,128)}, u32[]{:S(2)}, u32[]{:S(2)}) collective-permute-start(f32[4,18,192]{2,1,0:T(8,128)} %select_maximum_fusion), channel_id=1, source_target_pairs={{0,64},{64,128},{128,192},{192,256},{256,320},{320,384},{384,448},... | collective-permute-start | bytes 165896 | tf_op jit(solution)/shard_map/ppermute | solution.py:12
  5.6 0.6 select_maximum_fusion.1
  6.3 3.6 %collective-permute-start.1 = (f32[3,18,192]{2,0,1:T(4,128)}, f32[3,18,192]{2,0,1:T(4,128)}, u32[]{:S(2)}, u32[]{:S(2)}) collective-permute-start(f32[3,18,192]{2,0,1:T(4,128)} %select_maximum_fusion.1), channel_id=1, source_target_pairs={{0,960},{64,0},{128,64},{192,128},{256,192},{320,256},{384,320},{4... | collective-permute-start | bytes 124424 | tf_op jit(solution)/shard_map/ppermute | solution.py:12
  9.9 7.1 %fusion.7 = (f32[1152,353]{1,0:T(8,128)S(1)}, f32[1152,353]{1,0:T(8,128)S(1)}) fusion(), kind=kLoop, calls=%fused_computation.10 | loop fusion | flops 3659904 | bytes 3253248 | tf_op jit(solution)/shard_map/sin | solution.py:25
  17.1 0.7 slice_convert_fusion
  17.8 0.5 slice_bitcast_fusion.2
  18.2 0.9 slice.277
  19.2 0.8 slice.276
  20.0 1.0 pad_maximum_fusion.7
  21.0 0.8 copy.28
  21.8 1.7 %reshape.169 = f32[216,192]{1,0:T(8,128)} reshape(f32[12,18,192]{2,1,0:T(8,128)} %copy.28) | data formatting | bytes 331776 | tf_op jit(solution)/shard_map/reshape | solution.py:61
  23.5 1.7 %copy.29 = f32[192,216]{1,0:T(8,128)} copy(f32[192,216]{0,1:T(8,128)} %bitcast.32) | data formatting | bytes 331776 | tf_op jit(solution)/shard_map/transpose | solution.py:61
  25.2 1.9 %all_to_all.16 = f32[64,1,648]{2,1,0:T(1,128)} reshape(f32[192,216]{1,0:T(8,128)} %copy.29) | data formatting | bytes 331776 | tf_op jit(solution)/shard_map/all_to_all | solution.py:62
  27.1 27.0 %all-to-all-start = ((f32[64,1,648]{2,1,0:T(1,128)}), f32[64,1,648]{2,1,0:T(1,128)}, u32[]{:S(2)}, u32[]{:S(2)}) async-start(f32[64,1,648]{2,1,0:T(1,128)} %all_to_all.16), calls=%async_computation | async-start | bytes 393216 | tf_op jit(solution)/shard_map/all_to_all | solution.py:62
  54.1 0.7 slice_convert_fusion.1
  54.8 0.6 slice_bitcast_fusion.5
  55.5 0.6 pad_add_fusion
  56.3 0.7 tile.7
  56.9 1.6 %tile.8 = f32[36,706]{1,0:T(8,128)} reshape(f32[3,12,706]{2,1,0:T(8,128)} %tile.7) | data formatting | bytes 203328 | tf_op jit(solution)/shard_map/tile | solution.py:75
  58.5 0.7 add_compare_fusion
  59.3 16.9 %all-to-all-done = f32[64,1,648]{2,1,0:T(1,128)} async-done(((f32[64,1,648]{2,1,0:T(1,128)}), f32[64,1,648]{2,1,0:T(1,128)}, u32[]{:S(2)}, u32[]{:S(2)}) %all-to-all-start) | async-done | bytes 165920 | tf_op jit(solution)/shard_map/all_to_all | solution.py:62
  76.3 1.8 %copy.31 = f32[64,1,648]{0,2,1:T(8,128)} copy(f32[64,1,648]{2,1,0:T(1,128)} %all-to-all-done) | data formatting | bytes 331776 | tf_op jit(solution)/shard_map/all_to_all | solution.py:62
  78.1 1.8 %reshape.170 = f32[64,36,18]{0,2,1:T(8,128)} reshape(f32[64,1,648]{0,2,1:T(8,128)} %copy.31) | data formatting | bytes 331776 | tf_op jit(solution)/shard_map/reshape | solution.py:63
  79.9 2.5 %copy.32 = f32[36,64,18]{2,1,0:T(8,128)} copy(f32[36,64,18]{1,2,0:T(8,128)} %bitcast.31) | data formatting | bytes 331776 | tf_op jit(solution)/shard_map/transpose | solution.py:64
  82.3 2.5 %reshape.171 = f32[36,1152]{1,0:T(8,128)} reshape(f32[36,64,18]{2,1,0:T(8,128)} %copy.32) | data formatting | bytes 331776 | tf_op jit(solution)/shard_map/reshape | solution.py:64
  84.9 3.5 %fusion.10 = f32[36,706]{1,0:T(8,128)S(1)} fusion(f32[36,706]{1,0:T(8,128)} %tile.8, f32[36,1152]{1,0:T(8,128)} %reshape.171, f32[1152,353]{1,0:T(8,128)S(1)} %get-tuple-element.51, f32[1152,353]{1,0:T(8,128)S(1)} %get-tuple-element.52), kind=kOutput, calls=%fused_computation.13 | convolution fusion | flops 352189504 | bytes 3622464 | tf_op jit(solution)/shard_map/dot_general | solution.py:76
  88.4 4.0 %fusion.2 = f32[36,1152]{1,0:T(8,128)} fusion(f32[36,1152]{1,0:T(8,128)S(1)} %copy-done.1, f32[36,706]{1,0:T(8,128)S(1)} %fusion.10, f32[1152,353]{1,0:T(8,128)S(1)} %get-tuple-element.51, f32[1152,353]{1,0:T(8,128)S(1)} %get-tuple-element.52, pred[36]{0:T(512)(128)(4,1)S(1)} %eq.37), kind=kOutput, calls=%fused_computation.4 | convolution fusion | flops 352205568 | bytes 3686724 | tf_op jit(solution)/shard_map/dot_general | solution.py:78
  92.4 0.9 reshape.172
  93.5 0.2 slice.241
  94.4 1.3 reshape.173
  95.7 0.4 fusion.35
  96.2 1.2 copy.37
  97.3 0.7 fusion.34
  98.1 0.5 copy.34
  98.5 0.5 copy.35
  99.0 0.3 copy.33
  99.4 0.3 copy.36
  99.9 0.9 copy.38
  100.8 5.4 %all-to-all-start.1 = ((f32[64,1,792]{2,1,0:T(1,128)}), f32[64,1,792]{2,1,0:T(1,128)S(1)}, u32[]{:S(2)}, u32[]{:S(2)}) async-start(f32[64,1,792]{2,1,0:T(1,128)} %copy.38), calls=%async_computation.1 | async-start | bytes 458752 | tf_op jit(solution)/shard_map/all_to_all | solution.py:95
  106.2 3.5 %collective-permute-start.2 = (f32[8,1,192]{2,1,0:T(1,128)S(1)}, f32[8,1,192]{2,1,0:T(1,128)S(1)}, u32[]{:S(2)}, u32[]{:S(2)}) collective-permute-start(f32[8,1,192]{2,1,0:T(1,128)S(1)} %copy.40), channel_id=1, source_target_pairs={{0,1},{1,2},{2,3},{3,4},{4,5},{5,6},{6,7},{7,8},{8,9},{9,10},{10,1... | collective-permute-start | bytes 18440 | tf_op jit(solution)/shard_map/ppermute | solution.py:12
  109.9 0.7 slice_select_fusion.2
  110.6 19.7 %all-to-all-done.1 = f32[64,1,792]{2,1,0:T(1,128)S(1)} async-done(((f32[64,1,792]{2,1,0:T(1,128)}), f32[64,1,792]{2,1,0:T(1,128)S(1)}, u32[]{:S(2)}, u32[]{:S(2)}) %all-to-all-start.1) | async-done | bytes 202784 | tf_op jit(solution)/shard_map/all_to_all | solution.py:95
  130.3 0.5 reduce.4
  131.9 0.7 copy.44
  (56 shorter events, 2.7 us)
Async XLA Ops:
  1.0 16.1 %copy-start.2 = (f32[8,18,192]{2,1,0:T(8,128)}, f32[8,18,192]{2,1,0:T(8,128)S(1)}, u32[]{:S(2)}) copy-start(f32[8,18,192]{2,1,0:T(8,128)S(1)} %copy.25) | copy-start | bytes 331780
  3.6 15.5 %collective-permute-start = (f32[4,18,192]{2,1,0:T(8,128)}, f32[4,18,192]{2,1,0:T(8,128)}, u32[]{:S(2)}, u32[]{:S(2)}) collective-permute-start(f32[4,18,192]{2,1,0:T(8,128)} %select_maximum_fusion), channel_id=1, source_target_pairs={{0,64},{64,128},{128,192},{192,256},{256,320},{320,384},{384,448},... | collective-permute-start | bytes 165896 | tf_op jit(solution)/shard_map/ppermute | solution.py:12
  6.3 10.8 %collective-permute-start.1 = (f32[3,18,192]{2,0,1:T(4,128)}, f32[3,18,192]{2,0,1:T(4,128)}, u32[]{:S(2)}, u32[]{:S(2)}) collective-permute-start(f32[3,18,192]{2,0,1:T(4,128)} %select_maximum_fusion.1), channel_id=1, source_target_pairs={{0,960},{64,0},{128,64},{192,128},{256,192},{320,256},{384,320},{4... | collective-permute-start | bytes 124424 | tf_op jit(solution)/shard_map/ppermute | solution.py:12
  17.0 38.4 %copy-start.7 = (s32[8]{0:T(128)S(1)}, s32[8]{0:T(128)}, u32[]{:S(2)}) copy-start(s32[8]{0:T(128)} %param.12) | copy-start | bytes 100
  20.0 38.5 %copy-start.8 = (s32[8]{0:T(128)S(1)}, s32[8]{0:T(128)}, u32[]{:S(2)}) copy-start(s32[8]{0:T(128)} %param.13) | copy-start | bytes 100
  27.1 49.1 %all-to-all-start = ((f32[64,1,648]{2,1,0:T(1,128)}), f32[64,1,648]{2,1,0:T(1,128)}, u32[]{:S(2)}, u32[]{:S(2)}) async-start(f32[64,1,648]{2,1,0:T(1,128)} %all_to_all.16), calls=%async_computation | async-start | bytes 393216 | tf_op jit(solution)/shard_map/all_to_all | solution.py:62
  84.9 3.5 %copy-start.1 = (f32[36,1152]{1,0:T(8,128)S(1)}, f32[36,1152]{1,0:T(8,128)}, u32[]{:S(2)}) copy-start(f32[36,1152]{1,0:T(8,128)} %reshape.171) | copy-start | bytes 497668
  98.1 0.9 copy-start.6
  98.1 1.3 copy-start.5
  98.1 1.6 %copy-start = (f32[3,12,64,18]{2,3,1,0:T(8,128)S(1)}, f32[3,12,64,18]{2,3,1,0:T(8,128)}, u32[]{:S(2)}) copy-start(f32[3,12,64,18]{2,3,1,0:T(8,128)} %copy.37) | copy-start | bytes 497668
  99.0 7.2 %slice-start = ((f32[8,18,192]{2,0,1:T(8,128)}), f32[8,1,192]{2,0,1:T(8,128)S(1)}, s32[]{:S(2)}) async-start(f32[8,18,192]{2,0,1:T(8,128)} %param.10), calls=%async_computation.2 | async-start | bytes 16384 | tf_op jit(solution)/shard_map/slice | solution.py:58
  99.0 10.7 %copy-start.4 = (f32[8,18,192]{2,0,1:T(8,128)S(1)}, f32[8,18,192]{2,0,1:T(8,128)}, u32[]{:S(2)}) copy-start(f32[8,18,192]{2,0,1:T(8,128)} %param.10) | copy-start | bytes 331780
  99.9 31.4 %copy-start.3 = (f32[8,18,192]{2,1,0:T(8,128)S(1)}, f32[8,18,192]{2,1,0:T(8,128)}, u32[]{:S(2)}) copy-start(f32[8,18,192]{2,1,0:T(8,128)} %copy-done.2) | copy-start | bytes 331780
  100.8 29.6 %all-to-all-start.1 = ((f32[64,1,792]{2,1,0:T(1,128)}), f32[64,1,792]{2,1,0:T(1,128)S(1)}, u32[]{:S(2)}, u32[]{:S(2)}) async-start(f32[64,1,792]{2,1,0:T(1,128)} %copy.38), calls=%async_computation.1 | async-start | bytes 458752 | tf_op jit(solution)/shard_map/all_to_all | solution.py:95
  106.2 25.5 %collective-permute-start.2 = (f32[8,1,192]{2,1,0:T(1,128)S(1)}, f32[8,1,192]{2,1,0:T(1,128)S(1)}, u32[]{:S(2)}, u32[]{:S(2)}) collective-permute-start(f32[8,1,192]{2,1,0:T(1,128)S(1)} %copy.40), channel_id=1, source_target_pairs={{0,1},{1,2},{2,3},{3,4},{4,5},{5,6},{6,7},{7,8},{8,9},{9,10},{10,1... | collective-permute-start | bytes 18440 | tf_op jit(solution)/shard_map/ppermute | solution.py:12

commit v5 on v4

--- a/solution.py
+++ b/solution.py
@@ -6,9 +6,11 @@
 from jax.sharding import PartitionSpec as P
 
 
-def shifted_from(block, axis, distance):
+def shifted_from(block, axis, distance, wrap=True):
     count = lax.axis_size(axis)
     route = [(i, (i + distance) % count) for i in range(count)]
+    if not wrap:
+        route = [(i, j) for i, j in route if 0 <= i + distance < count]
     return lax.ppermute(block, axis, route)
 
 
@@ -17,12 +19,18 @@
     return courant * centred - 0.5 * jnp.abs(courant) * (near_hi - near_lo)
 
 
-def build_table(n_full, n_waves):
-    points = jnp.arange(n_full, dtype=jnp.int32)
+def build_table(n_full, n_waves, step):
     waves = jnp.arange(n_waves, dtype=jnp.int32)
-    phase = points[:, None] * waves[None, :] % n_full
-    angle = phase.astype(jnp.float32) * (2.0 * math.pi / n_full)
-    return jnp.concatenate([jnp.cos(angle), jnp.sin(angle)], axis=1)
+    coarse = jnp.arange(n_full // step, dtype=jnp.int32) * step
+    fine = jnp.arange(step, dtype=jnp.int32)
+    scale = 2.0 * math.pi / n_full
+    alpha = (coarse[:, None] * waves[None, :] % n_full).astype(jnp.float32) * scale
+    beta = (fine[:, None] * waves[None, :] % n_full).astype(jnp.float32) * scale
+    ca, sa = jnp.cos(alpha)[:, None], jnp.sin(alpha)[:, None]
+    cb, sb = jnp.cos(beta)[None], jnp.sin(beta)[None]
+    cos_t = (ca * cb - sa * sb).reshape(n_full, n_waves)
+    sin_t = (sa * cb + ca * sb).reshape(n_full, n_waves)
+    return jnp.concatenate([cos_t, sin_t], axis=1)
 
 
 def local(state, courant_east, courant_north, cutoff, filter_mask):
@@ -51,9 +59,10 @@
         ),
         "lat",
         1,
+        wrap=False,
     )
     from_north = shifted_from(
-        jnp.concatenate([state[:2], row_info(slice(0, 2))], axis=0), "lat", -1
+        jnp.concatenate([state[:2], row_info(slice(0, 2))], axis=0), "lat", -1, wrap=False
     )
     east_halo = shifted_from(courant_east[:, -1:], "lon", 1)
 
@@ -68,7 +77,7 @@
     cut_ext = jnp.concatenate([info_s[:2], cutoff, info_n[:2]])
     mask_ext = jnp.concatenate([info_s[2:], filter_mask, info_n[2:]])
 
-    fourier = build_table(n_full, n_waves)
+    fourier = build_table(n_full, n_waves, 32)
     waves = jnp.arange(n_waves, dtype=jnp.int32)
     weights = jnp.where(waves == 0, 1.0 / n_full, 2.0 / n_full).astype(jnp.float32)
     kept = jnp.where(waves[None, :] <= cut_ext[:, None], weights[None, :], 0.0)

time: 134 us -> 132 us (0.985)
  the two profiles are of different devices: /device:TPU:64 before, /device:TPU:1 now
where the time goes in v5:
time: 132 us; the launch traced here: 130 us
  starting transfers between devices  44.8 us (34%)
  waiting for transfers between devices  36.2 us (27%)
  local copies, waits for them, and re-layouts  32.2 us (24%)
  other arithmetic  8.53 us (6%)
  matrix products  7.5 us (6%)
    ppermute x3, starting transfers between devices, shifted_from(): return lax.ppermute(block, axis, route)  20.9 us
    all_to_all x1, starting transfers between devices, local(): lax.all_to_all(outgoing, 'lon', split_axis=0, concat_axis=0, tiled=True)  18.9 us
    all_to_all x1, waiting for transfers between devices, local(): lax.all_to_all(windows, 'lon', split_axis=0, concat_axis=0, tiled=True)  18.6 us
    all_to_all x1, waiting for transfers between devices, local(): lax.all_to_all(outgoing, 'lon', split_axis=0, concat_axis=0, tiled=True)  17.5 us
    all_to_all x1, starting transfers between devices, local(): lax.all_to_all(windows, 'lon', split_axis=0, concat_axis=0, tiled=True)  5.05 us
    dot_general x1, matrix products, local(): lax.dot_general(coeffs, fourier, (((1,), (1,)), ((), ())), precision=lax....  4 us
    all_to_all x2, local copies, waits for them, and re-layouts, local(): lax.all_to_all(outgoing, 'lon', split_axis=0, concat_axis=0, tiled=True)  3.74 us
    dot_general x1, matrix products, local(): coeffs = jnp.dot(lines, fourier, precision=lax.Precision.HIGHEST)  3.5 us
  transfers between devices with their start and end apart: 5, of which 3 were waited for; matrix products, arithmetic and copies ran while one was open for 9% of the time, Pallas kernels for 0%

profile of v5, /device:TPU:1, one launch (start us, length us, event | category | flops | bytes accessed | tf_op | source)
XLA Modules:
  0.0 129.6 jit_solution(8582076712556346552)
XLA Ops:
  0.0 1.0 copy.25
  1.0 1.1 fusion.44
  2.1 0.8 slice_bitcast_fusion.6
  3.0 0.7 select_maximum_fusion
  3.6 5.4 %collective-permute-start = (f32[4,18,192]{2,1,0:T(8,128)}, f32[4,18,192]{2,1,0:T(8,128)}, u32[]{:S(2)}, u32[]{:S(2)}) collective-permute-start(f32[4,18,192]{2,1,0:T(8,128)} %select_maximum_fusion), channel_id=1, source_target_pairs={{0,64},{64,128},{128,192},{192,256},{256,320},{320,384},{384,448},... | collective-permute-start | bytes 165896 | tf_op jit(solution)/shard_map/ppermute | solution.py:14
  9.1 0.7 select_maximum_fusion.1
  9.7 12.6 %collective-permute-start.1 = (f32[3,18,192]{2,0,1:T(4,128)}, f32[3,18,192]{2,0,1:T(4,128)}, u32[]{:S(2)}, u32[]{:S(2)}) collective-permute-start(f32[3,18,192]{2,0,1:T(4,128)} %select_maximum_fusion.1), channel_id=1, source_target_pairs={{64,0},{128,64},{192,128},{256,192},{320,256},{384,320},{448,384},... | collective-permute-start | bytes 124424 | tf_op jit(solution)/shard_map/ppermute | solution.py:14
  22.6 0.3 fusion.23
  22.9 0.5 multiply_subtract_fusion
  23.6 0.7 slice_convert_fusion
  24.2 0.5 slice_bitcast_fusion.2
  24.8 0.9 slice.277
  25.7 0.8 slice.276
  26.5 1.0 pad_maximum_fusion.7
  27.5 0.8 copy.28
  28.3 1.7 %reshape.262 = f32[216,192]{1,0:T(8,128)} reshape(f32[12,18,192]{2,1,0:T(8,128)} %copy.28) | data formatting | bytes 331776 | tf_op jit(solution)/shard_map/reshape | solution.py:70
  30.0 1.7 %copy.29 = f32[192,216]{1,0:T(8,128)} copy(f32[192,216]{0,1:T(8,128)} %bitcast.38) | data formatting | bytes 331776 | tf_op jit(solution)/shard_map/transpose | solution.py:70
  31.8 1.9 %all_to_all.16 = f32[64,1,648]{2,1,0:T(1,128)} reshape(f32[192,216]{1,0:T(8,128)} %copy.29) | data formatting | bytes 331776 | tf_op jit(solution)/shard_map/all_to_all | solution.py:71
  33.7 18.9 %all-to-all-start = ((f32[64,1,648]{2,1,0:T(1,128)}), f32[64,1,648]{2,1,0:T(1,128)}, u32[]{:S(2)}, u32[]{:S(2)}) async-start(f32[64,1,648]{2,1,0:T(1,128)} %all_to_all.16), calls=%async_computation | async-start | bytes 393216 | tf_op jit(solution)/shard_map/all_to_all | solution.py:71
  52.5 0.7 slice_convert_fusion.1
  53.2 0.6 slice_bitcast_fusion.5
  53.8 0.7 pad_add_fusion
  54.6 0.7 tile.7
  55.3 1.6 %tile.8 = f32[36,706]{1,0:T(8,128)} reshape(f32[3,12,706]{2,1,0:T(8,128)} %tile.7) | data formatting | bytes 203328 | tf_op jit(solution)/shard_map/tile | solution.py:84
  56.9 0.7 add_compare_fusion
  57.7 17.5 %all-to-all-done = f32[64,1,648]{2,1,0:T(1,128)} async-done(((f32[64,1,648]{2,1,0:T(1,128)}), f32[64,1,648]{2,1,0:T(1,128)}, u32[]{:S(2)}, u32[]{:S(2)}) %all-to-all-start) | async-done | bytes 165920 | tf_op jit(solution)/shard_map/all_to_all | solution.py:71
  75.1 1.8 %copy.31 = f32[64,1,648]{0,2,1:T(8,128)} copy(f32[64,1,648]{2,1,0:T(1,128)} %all-to-all-done) | data formatting | bytes 331776 | tf_op jit(solution)/shard_map/all_to_all | solution.py:71
  77.0 1.8 %reshape.263 = f32[64,36,18]{0,2,1:T(8,128)} reshape(f32[64,1,648]{0,2,1:T(8,128)} %copy.31) | data formatting | bytes 331776 | tf_op jit(solution)/shard_map/reshape | solution.py:72
  78.8 2.5 %copy.32 = f32[36,64,18]{2,1,0:T(8,128)} copy(f32[36,64,18]{1,2,0:T(8,128)} %bitcast.37) | data formatting | bytes 331776 | tf_op jit(solution)/shard_map/transpose | solution.py:73
  81.3 2.5 %reshape.264 = f32[36,1152]{1,0:T(8,128)} reshape(f32[36,64,18]{2,1,0:T(8,128)} %copy.32) | data formatting | bytes 331776 | tf_op jit(solution)/shard_map/reshape | solution.py:73
  83.8 3.5 %fusion.3 = f32[36,706]{1,0:T(8,128)S(1)} fusion(f32[36,706]{1,0:T(8,128)} %tile.8, f32[36,1152]{1,0:T(8,128)} %reshape.264, f32[1152,353]{1,0:T(8,128)S(1)} %bitcast.33, f32[1152,353]{1,0:T(8,128)S(1)} %bitcast.31), kind=kOutput, calls=%fused_computation.6 | convolution fusion | flops 352189504 | bytes 3622464 | tf_op jit(solution)/shard_map/dot_general | solution.py:85
  87.3 4.0 %fusion.2 = f32[36,1152]{1,0:T(8,128)} fusion(f32[36,1152]{1,0:T(8,128)S(1)} %copy-done.1, f32[36,706]{1,0:T(8,128)S(1)} %fusion.3, f32[1152,353]{1,0:T(8,128)S(1)} %bitcast.34, f32[1152,353]{1,0:T(8,128)S(1)} %bitcast.32, pred[36]{0:T(512)(128)(4,1)S(1)} %eq.39), kind=kOutput, calls=%fused_computation.3 | convolution fusion | flops 352205568 | bytes 3686724 | tf_op jit(solution)/shard_map/dot_general | solution.py:87
  91.3 0.9 reshape.265
  93.3 1.3 reshape.266
  94.6 0.4 fusion.42
  95.1 1.2 copy.37
  96.3 0.7 fusion.41
  97.0 0.5 copy.34
  97.4 0.5 copy.35
  97.9 0.3 copy.33
  98.3 0.3 copy.36
  98.8 0.9 copy.38
  99.7 5.1 %all-to-all-start.1 = ((f32[64,1,792]{2,1,0:T(1,128)}), f32[64,1,792]{2,1,0:T(1,128)S(1)}, u32[]{:S(2)}, u32[]{:S(2)}) async-start(f32[64,1,792]{2,1,0:T(1,128)} %copy.38), calls=%async_computation.1 | async-start | bytes 458752 | tf_op jit(solution)/shard_map/all_to_all | solution.py:104
  104.8 2.9 %collective-permute-start.2 = (f32[8,1,192]{2,1,0:T(1,128)S(1)}, f32[8,1,192]{2,1,0:T(1,128)S(1)}, u32[]{:S(2)}, u32[]{:S(2)}) collective-permute-start(f32[8,1,192]{2,1,0:T(1,128)S(1)} %copy.40), channel_id=1, source_target_pairs={{0,1},{1,2},{2,3},{3,4},{4,5},{5,6},{6,7},{7,8},{8,9},{9,10},{10,1... | collective-permute-start | bytes 18440 | tf_op jit(solution)/shard_map/ppermute | solution.py:14
  108.0 0.7 slice_select_fusion.2
  108.7 18.6 %all-to-all-done.1 = f32[64,1,792]{2,1,0:T(1,128)S(1)} async-done(((f32[64,1,792]{2,1,0:T(1,128)}), f32[64,1,792]{2,1,0:T(1,128)S(1)}, u32[]{:S(2)}, u32[]{:S(2)}) %all-to-all-start.1) | async-done | bytes 202784 | tf_op jit(solution)/shard_map/all_to_all | solution.py:104
  127.3 0.5 reduce.4
  128.9 0.7 copy.44
  (59 shorter events, 3.2 us)
Async XLA Ops:
  1.0 21.9 %copy-start.2 = (f32[8,18,192]{2,1,0:T(8,128)}, f32[8,18,192]{2,1,0:T(8,128)S(1)}, u32[]{:S(2)}) copy-start(f32[8,18,192]{2,1,0:T(8,128)S(1)} %copy.25) | copy-start | bytes 331780
  3.6 22.1 %collective-permute-start = (f32[4,18,192]{2,1,0:T(8,128)}, f32[4,18,192]{2,1,0:T(8,128)}, u32[]{:S(2)}, u32[]{:S(2)}) collective-permute-start(f32[4,18,192]{2,1,0:T(8,128)} %select_maximum_fusion), channel_id=1, source_target_pairs={{0,64},{64,128},{128,192},{192,256},{256,320},{320,384},{384,448},... | collective-permute-start | bytes 165896 | tf_op jit(solution)/shard_map/ppermute | solution.py:14
  9.7 13.8 %collective-permute-start.1 = (f32[3,18,192]{2,0,1:T(4,128)}, f32[3,18,192]{2,0,1:T(4,128)}, u32[]{:S(2)}, u32[]{:S(2)}) collective-permute-start(f32[3,18,192]{2,0,1:T(4,128)} %select_maximum_fusion.1), channel_id=1, source_target_pairs={{64,0},{128,64},{192,128},{256,192},{320,256},{384,320},{448,384},... | collective-permute-start | bytes 124424 | tf_op jit(solution)/shard_map/ppermute | solution.py:14
  23.4 30.3 %copy-start.7 = (s32[8]{0:T(128)S(1)}, s32[8]{0:T(128)}, u32[]{:S(2)}) copy-start(s32[8]{0:T(128)} %param.12) | copy-start | bytes 100
  26.5 30.4 %copy-start.8 = (s32[8]{0:T(128)S(1)}, s32[8]{0:T(128)}, u32[]{:S(2)}) copy-start(s32[8]{0:T(128)} %param.13) | copy-start | bytes 100
  33.7 41.5 %all-to-all-start = ((f32[64,1,648]{2,1,0:T(1,128)}), f32[64,1,648]{2,1,0:T(1,128)}, u32[]{:S(2)}, u32[]{:S(2)}) async-start(f32[64,1,648]{2,1,0:T(1,128)} %all_to_all.16), calls=%async_computation | async-start | bytes 393216 | tf_op jit(solution)/shard_map/all_to_all | solution.py:71
  83.8 3.5 %copy-start.1 = (f32[36,1152]{1,0:T(8,128)S(1)}, f32[36,1152]{1,0:T(8,128)}, u32[]{:S(2)}) copy-start(f32[36,1152]{1,0:T(8,128)} %reshape.264) | copy-start | bytes 497668
  97.0 0.9 copy-start.6
  97.0 1.3 copy-start.5
  97.0 1.6 %copy-start = (f32[3,12,64,18]{2,3,1,0:T(8,128)S(1)}, f32[3,12,64,18]{2,3,1,0:T(8,128)}, u32[]{:S(2)}) copy-start(f32[3,12,64,18]{2,3,1,0:T(8,128)} %copy.37) | copy-start | bytes 497668
  97.9 6.8 %slice-start = ((f32[8,18,192]{2,0,1:T(8,128)}), f32[8,1,192]{2,0,1:T(8,128)S(1)}, s32[]{:S(2)}) async-start(f32[8,18,192]{2,0,1:T(8,128)} %param.10), calls=%async_computation.2 | async-start | bytes 16384 | tf_op jit(solution)/shard_map/slice | solution.py:67
  97.9 9.8 %copy-start.4 = (f32[8,18,192]{2,0,1:T(8,128)S(1)}, f32[8,18,192]{2,0,1:T(8,128)}, u32[]{:S(2)}) copy-start(f32[8,18,192]{2,0,1:T(8,128)} %param.10) | copy-start | bytes 331780
  98.8 29.4 %copy-start.3 = (f32[8,18,192]{2,1,0:T(8,128)S(1)}, f32[8,18,192]{2,1,0:T(8,128)}, u32[]{:S(2)}) copy-start(f32[8,18,192]{2,1,0:T(8,128)} %copy-done.2) | copy-start | bytes 331780
  99.7 27.6 %all-to-all-start.1 = ((f32[64,1,792]{2,1,0:T(1,128)}), f32[64,1,792]{2,1,0:T(1,128)S(1)}, u32[]{:S(2)}, u32[]{:S(2)}) async-start(f32[64,1,792]{2,1,0:T(1,128)} %copy.38), calls=%async_computation.1 | async-start | bytes 458752 | tf_op jit(solution)/shard_map/all_to_all | solution.py:104
  104.8 23.8 %collective-permute-start.2 = (f32[8,1,192]{2,1,0:T(1,128)S(1)}, f32[8,1,192]{2,1,0:T(1,128)S(1)}, u32[]{:S(2)}, u32[]{:S(2)}) collective-permute-start(f32[8,1,192]{2,1,0:T(1,128)S(1)} %copy.40), channel_id=1, source_target_pairs={{0,1},{1,2},{2,3},{3,4},{4,5},{5,6},{6,7},{7,8},{8,9},{9,10},{10,1... | collective-permute-start | bytes 18440 | tf_op jit(solution)/shard_map/ppermute | solution.py:14

commit v6 on v5

--- a/solution.py
+++ b/solution.py
@@ -82,10 +82,10 @@
     weights = jnp.where(waves == 0, 1.0 / n_full, 2.0 / n_full).astype(jnp.float32)
     kept = jnp.where(waves[None, :] <= cut_ext[:, None], weights[None, :], 0.0)
     kept_both = jnp.tile(jnp.concatenate([kept, kept], axis=1), (group, 1))
-    coeffs = jnp.dot(lines, fourier, precision=lax.Precision.HIGHEST)
+    coeffs = jnp.dot(lines, fourier, precision=lax.Precision.HIGH)
     coeffs = coeffs * kept_both
     filtered = lax.dot_general(
-        coeffs, fourier, (((1,), (1,)), ((), ())), precision=lax.Precision.HIGHEST
+        coeffs, fourier, (((1,), (1,)), ((), ())), precision=lax.Precision.HIGH
     )
     keep = jnp.tile(mask_ext, group)[:, None] == 1
     smooth = jnp.where(keep, filtered, lines).reshape(group, n_ext, n_full)

time: 132 us -> 129 us (0.977)
  matrix products: 7.5 us -> 4.91 us
    dot_general x1, matrix products: 4 us -> 2.48 us  [local(): lax.dot_general(coeffs, fourier, (((1,), (1,)), ((), ())), precision=lax....]
where the time goes in v6:
time: 129 us; the launch traced here: 127 us
  starting transfers between devices  44.6 us (35%)
  waiting for transfers between devices  36.4 us (28%)
  local copies, waits for them, and re-layouts  32.2 us (25%)
  other arithmetic  8.53 us (7%)
  matrix products  4.91 us (4%)
    ppermute x3, starting transfers between devices, shifted_from(): return lax.ppermute(block, axis, route)  20.9 us
    all_to_all x1, starting transfers between devices, local(): lax.all_to_all(outgoing, 'lon', split_axis=0, concat_axis=0, tiled=True)  18.7 us
    all_to_all x1, waiting for transfers between devices, local(): lax.all_to_all(windows, 'lon', split_axis=0, concat_axis=0, tiled=True)  18.6 us
    all_to_all x1, waiting for transfers between devices, local(): lax.all_to_all(outgoing, 'lon', split_axis=0, concat_axis=0, tiled=True)  17.7 us
    all_to_all x1, starting transfers between devices, local(): lax.all_to_all(windows, 'lon', split_axis=0, concat_axis=0, tiled=True)  5.05 us
    all_to_all x2, local copies, waits for them, and re-layouts, local(): lax.all_to_all(outgoing, 'lon', split_axis=0, concat_axis=0, tiled=True)  3.74 us
  transfers between devices with their start and end apart: 5, of which 3 were waited for; matrix products, arithmetic and copies ran while one was open for 9% of the time, Pallas kernels for 0%

profile of v6, /device:TPU:1, one launch (start us, length us, event | category | flops | bytes accessed | tf_op | source)
XLA Modules:
  0.0 127.0 jit_solution(15246802257678674109)
XLA Ops:
  0.0 1.0 copy.25
  1.0 1.1 fusion.44
  2.1 0.8 slice_bitcast_fusion.6
  3.0 0.7 select_maximum_fusion
  3.6 5.4 %collective-permute-start = (f32[4,18,192]{2,1,0:T(8,128)}, f32[4,18,192]{2,1,0:T(8,128)}, u32[]{:S(2)}, u32[]{:S(2)}) collective-permute-start(f32[4,18,192]{2,1,0:T(8,128)} %select_maximum_fusion), channel_id=1, source_target_pairs={{0,64},{64,128},{128,192},{192,256},{256,320},{320,384},{384,448},... | collective-permute-start | bytes 165896 | tf_op jit(solution)/shard_map/ppermute | solution.py:14
  9.1 0.7 select_maximum_fusion.1
  9.7 12.6 %collective-permute-start.1 = (f32[3,18,192]{2,0,1:T(4,128)}, f32[3,18,192]{2,0,1:T(4,128)}, u32[]{:S(2)}, u32[]{:S(2)}) collective-permute-start(f32[3,18,192]{2,0,1:T(4,128)} %select_maximum_fusion.1), channel_id=1, source_target_pairs={{64,0},{128,64},{192,128},{256,192},{320,256},{384,320},{448,384},... | collective-permute-start | bytes 124424 | tf_op jit(solution)/shard_map/ppermute | solution.py:14
  22.6 0.3 fusion.23
  22.9 0.5 multiply_subtract_fusion
  23.6 0.7 slice_convert_fusion
  24.2 0.5 slice_bitcast_fusion.2
  24.8 0.9 slice.277
  25.7 0.8 slice.276
  26.5 1.0 pad_maximum_fusion.7
  27.5 0.8 copy.28
  28.3 1.7 %reshape.262 = f32[216,192]{1,0:T(8,128)} reshape(f32[12,18,192]{2,1,0:T(8,128)} %copy.28) | data formatting | bytes 331776 | tf_op jit(solution)/shard_map/reshape | solution.py:70
  30.0 1.7 %copy.29 = f32[192,216]{1,0:T(8,128)} copy(f32[192,216]{0,1:T(8,128)} %bitcast.38) | data formatting | bytes 331776 | tf_op jit(solution)/shard_map/transpose | solution.py:70
  31.8 1.9 %all_to_all.16 = f32[64,1,648]{2,1,0:T(1,128)} reshape(f32[192,216]{1,0:T(8,128)} %copy.29) | data formatting | bytes 331776 | tf_op jit(solution)/shard_map/all_to_all | solution.py:71
  33.7 18.7 %all-to-all-start = ((f32[64,1,648]{2,1,0:T(1,128)}), f32[64,1,648]{2,1,0:T(1,128)}, u32[]{:S(2)}, u32[]{:S(2)}) async-start(f32[64,1,648]{2,1,0:T(1,128)} %all_to_all.16), calls=%async_computation | async-start | bytes 393216 | tf_op jit(solution)/shard_map/all_to_all | solution.py:71
  52.3 0.7 slice_convert_fusion.1
  53.0 0.6 slice_bitcast_fusion.5
  53.6 0.7 pad_add_fusion
  54.5 0.7 tile.7
  55.1 1.6 %tile.8 = f32[36,706]{1,0:T(8,128)} reshape(f32[3,12,706]{2,1,0:T(8,128)} %tile.7) | data formatting | bytes 203328 | tf_op jit(solution)/shard_map/tile | solution.py:84
  56.7 0.7 add_compare_fusion
  57.5 17.7 %all-to-all-done = f32[64,1,648]{2,1,0:T(1,128)} async-done(((f32[64,1,648]{2,1,0:T(1,128)}), f32[64,1,648]{2,1,0:T(1,128)}, u32[]{:S(2)}, u32[]{:S(2)}) %all-to-all-start) | async-done | bytes 165920 | tf_op jit(solution)/shard_map/all_to_all | solution.py:71
  75.1 1.8 %copy.31 = f32[64,1,648]{0,2,1:T(8,128)} copy(f32[64,1,648]{2,1,0:T(1,128)} %all-to-all-done) | data formatting | bytes 331776 | tf_op jit(solution)/shard_map/all_to_all | solution.py:71
  77.0 1.8 %reshape.263 = f32[64,36,18]{0,2,1:T(8,128)} reshape(f32[64,1,648]{0,2,1:T(8,128)} %copy.31) | data formatting | bytes 331776 | tf_op jit(solution)/shard_map/reshape | solution.py:72
  78.8 2.5 %copy.32 = f32[36,64,18]{2,1,0:T(8,128)} copy(f32[36,64,18]{1,2,0:T(8,128)} %bitcast.37) | data formatting | bytes 331776 | tf_op jit(solution)/shard_map/transpose | solution.py:73
  81.3 2.5 %reshape.264 = f32[36,1152]{1,0:T(8,128)} reshape(f32[36,64,18]{2,1,0:T(8,128)} %copy.32) | data formatting | bytes 331776 | tf_op jit(solution)/shard_map/reshape | solution.py:73
  83.8 2.4 %fusion.3 = f32[36,706]{1,0:T(8,128)S(1)} fusion(f32[36,706]{1,0:T(8,128)} %tile.8, f32[36,1152]{1,0:T(8,128)} %reshape.264, f32[1152,353]{1,0:T(8,128)S(1)} %bitcast.33, f32[1152,353]{1,0:T(8,128)S(1)} %bitcast.31), kind=kOutput, calls=%fused_computation.6 | convolution fusion | flops 176514112 | bytes 3622464 | tf_op jit(solution)/shard_map/dot_general | solution.py:85
  86.2 2.5 %fusion.2 = f32[36,1152]{1,0:T(8,128)} fusion(f32[36,1152]{1,0:T(8,128)S(1)} %copy-done.1, f32[36,706]{1,0:T(8,128)S(1)} %fusion.3, f32[1152,353]{1,0:T(8,128)S(1)} %bitcast.34, f32[1152,353]{1,0:T(8,128)S(1)} %bitcast.32, pred[36]{0:T(512)(128)(4,1)S(1)} %eq.39), kind=kOutput, calls=%fused_computation.3 | convolution fusion | flops 176530176 | bytes 3686724 | tf_op jit(solution)/shard_map/dot_general | solution.py:87
  88.7 0.9 reshape.265
  90.8 1.3 %reshape.266 = f32[3,12,64,18]{3,2,1,0:T(8,128)S(1)} reshape(f32[3,12,1152]{2,1,0:T(8,128)S(1)} %pad_maximum_fusion.8) | data formatting | bytes 331776 | tf_op jit(solution)/shard_map/reshape | solution.py:99
  92.1 0.4 fusion.42
  92.5 1.2 copy.37
  93.7 0.7 fusion.41
  94.4 0.5 copy.34
  94.9 0.5 copy.35
  95.4 0.3 copy.33
  95.7 0.3 copy.36
  96.2 0.9 copy.38
  97.1 5.1 %all-to-all-start.1 = ((f32[64,1,792]{2,1,0:T(1,128)}), f32[64,1,792]{2,1,0:T(1,128)S(1)}, u32[]{:S(2)}, u32[]{:S(2)}) async-start(f32[64,1,792]{2,1,0:T(1,128)} %copy.38), calls=%async_computation.1 | async-start | bytes 458752 | tf_op jit(solution)/shard_map/all_to_all | solution.py:104
  102.2 2.9 %collective-permute-start.2 = (f32[8,1,192]{2,1,0:T(1,128)S(1)}, f32[8,1,192]{2,1,0:T(1,128)S(1)}, u32[]{:S(2)}, u32[]{:S(2)}) collective-permute-start(f32[8,1,192]{2,1,0:T(1,128)S(1)} %copy.40), channel_id=1, source_target_pairs={{0,1},{1,2},{2,3},{3,4},{4,5},{5,6},{6,7},{7,8},{8,9},{9,10},{10,1... | collective-permute-start | bytes 18440 | tf_op jit(solution)/shard_map/ppermute | solution.py:14
  105.4 0.7 slice_select_fusion.2
  106.1 18.6 %all-to-all-done.1 = f32[64,1,792]{2,1,0:T(1,128)S(1)} async-done(((f32[64,1,792]{2,1,0:T(1,128)}), f32[64,1,792]{2,1,0:T(1,128)S(1)}, u32[]{:S(2)}, u32[]{:S(2)}) %all-to-all-start.1) | async-done | bytes 202784 | tf_op jit(solution)/shard_map/all_to_all | solution.py:104
  124.7 0.5 reduce.4
  126.3 0.7 copy.44
  (59 shorter events, 3.2 us)
Async XLA Ops:
  1.0 21.9 %copy-start.2 = (f32[8,18,192]{2,1,0:T(8,128)}, f32[8,18,192]{2,1,0:T(8,128)S(1)}, u32[]{:S(2)}) copy-start(f32[8,18,192]{2,1,0:T(8,128)S(1)} %copy.25) | copy-start | bytes 331780
  3.6 22.1 %collective-permute-start = (f32[4,18,192]{2,1,0:T(8,128)}, f32[4,18,192]{2,1,0:T(8,128)}, u32[]{:S(2)}, u32[]{:S(2)}) collective-permute-start(f32[4,18,192]{2,1,0:T(8,128)} %select_maximum_fusion), channel_id=1, source_target_pairs={{0,64},{64,128},{128,192},{192,256},{256,320},{320,384},{384,448},... | collective-permute-start | bytes 165896 | tf_op jit(solution)/shard_map/ppermute | solution.py:14
  9.7 13.8 %collective-permute-start.1 = (f32[3,18,192]{2,0,1:T(4,128)}, f32[3,18,192]{2,0,1:T(4,128)}, u32[]{:S(2)}, u32[]{:S(2)}) collective-permute-start(f32[3,18,192]{2,0,1:T(4,128)} %select_maximum_fusion.1), channel_id=1, source_target_pairs={{64,0},{128,64},{192,128},{256,192},{320,256},{384,320},{448,384},... | collective-permute-start | bytes 124424 | tf_op jit(solution)/shard_map/ppermute | solution.py:14
  23.4 30.2 %copy-start.7 = (s32[8]{0:T(128)S(1)}, s32[8]{0:T(128)}, u32[]{:S(2)}) copy-start(s32[8]{0:T(128)} %param.12) | copy-start | bytes 100
  26.5 30.2 %copy-start.8 = (s32[8]{0:T(128)S(1)}, s32[8]{0:T(128)}, u32[]{:S(2)}) copy-start(s32[8]{0:T(128)} %param.13) | copy-start | bytes 100
  33.7 41.5 %all-to-all-start = ((f32[64,1,648]{2,1,0:T(1,128)}), f32[64,1,648]{2,1,0:T(1,128)}, u32[]{:S(2)}, u32[]{:S(2)}) async-start(f32[64,1,648]{2,1,0:T(1,128)} %all_to_all.16), calls=%async_computation | async-start | bytes 393216 | tf_op jit(solution)/shard_map/all_to_all | solution.py:71
  83.8 2.4 %copy-start.1 = (f32[36,1152]{1,0:T(8,128)S(1)}, f32[36,1152]{1,0:T(8,128)}, u32[]{:S(2)}) copy-start(f32[36,1152]{1,0:T(8,128)} %reshape.264) | copy-start | bytes 497668
  94.4 0.9 copy-start.6
  94.4 1.3 %copy-start.5 = (f32[3,12,1,2]{3,2,1,0:T(1,128)S(1)}, f32[3,12,1,2]{3,2,1,0:T(1,128)}, u32[]{:S(2)}) copy-start(f32[3,12,1,2]{3,2,1,0:T(1,128)} %get-tuple-element.30) | copy-start | bytes 868
  94.4 1.6 %copy-start = (f32[3,12,64,18]{2,3,1,0:T(8,128)S(1)}, f32[3,12,64,18]{2,3,1,0:T(8,128)}, u32[]{:S(2)}) copy-start(f32[3,12,64,18]{2,3,1,0:T(8,128)} %copy.37) | copy-start | bytes 497668
  95.3 6.8 %slice-start = ((f32[8,18,192]{2,0,1:T(8,128)}), f32[8,1,192]{2,0,1:T(8,128)S(1)}, s32[]{:S(2)}) async-start(f32[8,18,192]{2,0,1:T(8,128)} %param.10), calls=%async_computation.2 | async-start | bytes 16384 | tf_op jit(solution)/shard_map/slice | solution.py:67
  95.3 9.8 %copy-start.4 = (f32[8,18,192]{2,0,1:T(8,128)S(1)}, f32[8,18,192]{2,0,1:T(8,128)}, u32[]{:S(2)}) copy-start(f32[8,18,192]{2,0,1:T(8,128)} %param.10) | copy-start | bytes 331780
  96.2 29.4 %copy-start.3 = (f32[8,18,192]{2,1,0:T(8,128)S(1)}, f32[8,18,192]{2,1,0:T(8,128)}, u32[]{:S(2)}) copy-start(f32[8,18,192]{2,1,0:T(8,128)} %copy-done.2) | copy-start | bytes 331780
  97.1 27.6 %all-to-all-start.1 = ((f32[64,1,792]{2,1,0:T(1,128)}), f32[64,1,792]{2,1,0:T(1,128)S(1)}, u32[]{:S(2)}, u32[]{:S(2)}) async-start(f32[64,1,792]{2,1,0:T(1,128)} %copy.38), calls=%async_computation.1 | async-start | bytes 458752 | tf_op jit(solution)/shard_map/all_to_all | solution.py:104
  102.2 23.8 %collective-permute-start.2 = (f32[8,1,192]{2,1,0:T(1,128)S(1)}, f32[8,1,192]{2,1,0:T(1,128)S(1)}, u32[]{:S(2)}, u32[]{:S(2)}) collective-permute-start(f32[8,1,192]{2,1,0:T(1,128)S(1)} %copy.40), channel_id=1, source_target_pairs={{0,1},{1,2},{2,3},{3,4},{4,5},{5,6},{6,7},{7,8},{8,9},{9,10},{10,1... | collective-permute-start | bytes 18440 | tf_op jit(solution)/shard_map/ppermute | solution.py:14

commit v7 on v6

--- a/solution.py
+++ b/solution.py
@@ -42,80 +42,66 @@
     n_lat = n_rows * lat_count
     half = n_full // 2
     group = n_comp // lon_count
-    n_ext = n_rows + 4
+    n_send = n_rows + 2
     n_win = n_cols + 4
 
     top = n_full // 8 + (half - 1 - n_full // 8) * (n_lat // 4 - 1) // (n_lat // 2)
     n_waves = min(top, half - 1) + 1
 
-    def row_info(sel):
-        whole = jnp.concatenate([cutoff[sel], filter_mask[sel]]).astype(jnp.float32)
-        blank = jnp.zeros((1, n_cols, n_comp), jnp.float32)
-        return blank.at[0, 0, : whole.shape[0]].set(whole)
-
-    from_south = shifted_from(
-        jnp.concatenate(
-            [state[-2:], courant_north[-1:], row_info(slice(n_rows - 2, n_rows))], axis=0
-        ),
-        "lat",
-        1,
-        wrap=False,
-    )
-    from_north = shifted_from(
-        jnp.concatenate([state[:2], row_info(slice(0, 2))], axis=0), "lat", -1, wrap=False
-    )
     east_halo = shifted_from(courant_east[:, -1:], "lon", 1)
 
-    rows_ext = jnp.concatenate([from_south[:2], state, from_north[:2]], axis=0)
-    outgoing = rows_ext.reshape(n_ext * n_cols, n_comp).T.reshape(lon_count, -1)
+    outgoing = state.reshape(n_rows * n_cols, n_comp).T.reshape(lon_count, -1)
     incoming = lax.all_to_all(outgoing, "lon", split_axis=0, concat_axis=0, tiled=True)
-    lines = incoming.reshape(lon_count, group * n_ext, n_cols)
-    lines = jnp.transpose(lines, (1, 0, 2)).reshape(group * n_ext, n_full)
-
-    info_s = from_south[3, 0, :4].astype(jnp.int32)
-    info_n = from_north[2, 0, :4].astype(jnp.int32)
-    cut_ext = jnp.concatenate([info_s[:2], cutoff, info_n[:2]])
-    mask_ext = jnp.concatenate([info_s[2:], filter_mask, info_n[2:]])
+    lines = incoming.reshape(lon_count, group * n_rows, n_cols)
+    lines = jnp.transpose(lines, (1, 0, 2)).reshape(group * n_rows, n_full)
 
     fourier = build_table(n_full, n_waves, 32)
     waves = jnp.arange(n_waves, dtype=jnp.int32)
     weights = jnp.where(waves == 0, 1.0 / n_full, 2.0 / n_full).astype(jnp.float32)
-    kept = jnp.where(waves[None, :] <= cut_ext[:, None], weights[None, :], 0.0)
+    kept = jnp.where(waves[None, :] <= cutoff[:, None], weights[None, :], 0.0)
     kept_both = jnp.tile(jnp.concatenate([kept, kept], axis=1), (group, 1))
     coeffs = jnp.dot(lines, fourier, precision=lax.Precision.HIGH)
     coeffs = coeffs * kept_both
     filtered = lax.dot_general(
         coeffs, fourier, (((1,), (1,)), ((), ())), precision=lax.Precision.HIGH
     )
-    keep = jnp.tile(mask_ext, group)[:, None] == 1
-    smooth = jnp.where(keep, filtered, lines).reshape(group, n_ext, n_full)
+    keep = jnp.tile(filter_mask, group)[:, None] == 1
+    smooth = jnp.where(keep, filtered, lines).reshape(group, n_rows, n_full)
 
-    south_pole = jnp.roll(smooth[:, 3:1:-1], half, axis=2)
-    north_pole = jnp.roll(smooth[:, n_ext - 3 : n_ext - 5 : -1], half, axis=2)
-    low = jnp.where(lat_index == 0, south_pole, smooth[:, :2])
-    high = jnp.where(lat_index == lat_count - 1, north_pole, smooth[:, -2:])
-    smooth = jnp.concatenate([low, smooth[:, 2:-2], high], axis=1)
+    south_pole = smooth[:, 1::-1]
+    north_pole = smooth[:, : n_rows - 3 : -1]
+    pole = jnp.roll(jnp.where(lat_index == 0, south_pole, north_pole), half, axis=2)
+    rows_out = jnp.concatenate([pole, smooth], axis=1)
 
-    tiles = smooth.reshape(group, n_ext, lon_count, n_cols)
+    tiles = rows_out.reshape(group, n_send, lon_count, n_cols)
     left = jnp.roll(tiles[..., -2:], 1, axis=2)
     right = jnp.roll(tiles[..., :2], -1, axis=2)
     windows = jnp.concatenate([left, tiles, right], axis=3)
     windows = jnp.transpose(windows, (2, 0, 1, 3)).reshape(lon_count, -1)
     back = lax.all_to_all(windows, "lon", split_axis=0, concat_axis=0, tiled=True)
-    ext = back.reshape(n_comp, n_ext * n_win).T.reshape(n_ext, n_win, n_comp)
+    ext = back.reshape(n_comp, n_send * n_win).T.reshape(n_send, n_win, n_comp)
+    own = ext[2:]
+    centre = own[:, 2:-2]
 
-    zonal_p = ext[2:-2]
+    from_south = shifted_from(
+        jnp.concatenate([centre[-2:], courant_north[-1:]], axis=0), "lat", 1, wrap=False
+    )
+    from_north = shifted_from(centre[:2], "lat", -1, wrap=False)
+
     zonal_c = jnp.concatenate([east_halo, courant_east], axis=1)
     east = face_flux(
-        zonal_p[:, 0 : n_cols + 1],
-        zonal_p[:, 1 : n_cols + 2],
-        zonal_p[:, 2 : n_cols + 3],
-        zonal_p[:, 3 : n_cols + 4],
+        own[:, 0 : n_cols + 1],
+        own[:, 1 : n_cols + 2],
+        own[:, 2 : n_cols + 3],
+        own[:, 3 : n_cols + 4],
         zonal_c,
     )
     zonal = -(east[:, 1:] - east[:, :-1])
 
-    merid_p = ext[:, 2:-2]
+    pole_rows = ext[:2, 2:-2]
+    south = jnp.where(lat_index == 0, pole_rows, from_south[:2])
+    north = jnp.where(lat_index == lat_count - 1, pole_rows, from_north)
+    merid_p = jnp.concatenate([south, centre, north], axis=0)
     south_c = jnp.where(lat_index == 0, 0.0, from_south[2:3])
     merid_c = jnp.concatenate([south_c, courant_north], axis=0)
     north_flux = face_flux(
@@ -136,7 +122,7 @@
     )
     weighted = cos_face[:, None, None] * north_flux
     meridional = -(weighted[1:] - weighted[:-1]) / cos_cell[:, None, None]
-    return zonal_p[:, 2:-2] + zonal + meridional
+    return centre + zonal + meridional
 
 
 def solution(mesh):

time: 129 us -> 108 us (0.84); the launches traced: 127 us -> 108 us
  local copies, waits for them, and re-layouts: 32.2 us -> 15.4 us
  starting transfers between devices: 44.6 us -> 48.6 us
  waiting for transfers between devices: 36.4 us -> 33 us
  other arithmetic: 8.53 us -> 5.98 us
    all_to_all x1, starting transfers between devices: 18.7 us -> 28.3 us  [local(): lax.all_to_all(outgoing, 'lon', split_axis=0, concat_axis=0, tiled=True)]
    slice x21 -> x7, local copies, waits for them, and re-layouts: 7.79 us -> 0.37 us  [the longest x3 0.24 us: local(): own = ext[2:]]
    ppermute x3, starting transfers between devices: 20.9 us -> 14.5 us  [shifted_from(): return lax.ppermute(block, axis, route)]
    reshape x8 -> x5, local copies, waits for them, and re-layouts: 9.61 us -> 4.02 us  [the longest x1 2.14 us: local(): lines = jnp.transpose(lines, (1, 0, 2)).reshape(group * n_rows, n_full)]
    all_to_all x1, waiting for transfers between devices: 17.7 us -> 13.5 us  [local(): lax.all_to_all(outgoing, 'lon', split_axis=0, concat_axis=0, tiled=True)]
    ppermute x3, waiting for transfers between devices: 0.09 us -> 3.46 us  [shifted_from(): return lax.ppermute(block, axis, route)]
    concatenate x5 -> x2, other arithmetic: 3.03 us -> 0.1 us  [the longest x1 0.09 us: local(): jnp.roll(jnp.where(lat_index == 0, south_pole, north_pole), half, axis=2)]
    all_to_all x1, waiting for transfers between devices: 18.6 us -> 16 us  [local(): lax.all_to_all(windows, 'lon', split_axis=0, concat_axis=0, tiled=True)]
  transfers between devices with their start and end apart: 5 -> 5, of which waited for: 3 -> 3; matrix products, arithmetic and copies ran while one was open for 9% -> 6% of each run, Pallas kernels for 0% -> 0%
where the time goes in v7:
time: 108 us
  starting transfers between devices  48.6 us (45%)
  waiting for transfers between devices  33 us (31%)
  local copies, waits for them, and re-layouts  15.4 us (14%)
  other arithmetic  5.98 us (6%)
  matrix products  4.48 us (4%)
    all_to_all x1, starting transfers between devices, local(): lax.all_to_all(outgoing, 'lon', split_axis=0, concat_axis=0, tiled=True)  28.3 us
    all_to_all x1, waiting for transfers between devices, local(): lax.all_to_all(windows, 'lon', split_axis=0, concat_axis=0, tiled=True)  16 us
    ppermute x3, starting transfers between devices, shifted_from(): return lax.ppermute(block, axis, route)  14.5 us
    all_to_all x1, waiting for transfers between devices, local(): lax.all_to_all(outgoing, 'lon', split_axis=0, concat_axis=0, tiled=True)  13.5 us
    all_to_all x1, starting transfers between devices, local(): lax.all_to_all(windows, 'lon', split_axis=0, concat_axis=0, tiled=True)  5.87 us
    ppermute x3, waiting for transfers between devices, shifted_from(): return lax.ppermute(block, axis, route)  3.46 us
    all_to_all x2, local copies, waits for them, and re-layouts, local(): lax.all_to_all(outgoing, 'lon', split_axis=0, concat_axis=0, tiled=True)  2.76 us
    concatenate x4, local copies, waits for them, and re-layouts, local(): rows_out = jnp.concatenate([pole, smooth], axis=1)  2.44 us
  transfers between devices with their start and end apart: 5, of which 3 were waited for; matrix products, arithmetic and copies ran while one was open for 6% of the time, Pallas kernels for 0%

profile of v7, /device:TPU:1, one launch (start us, length us, event | category | flops | bytes accessed | tf_op | source)
XLA Modules:
  0.0 107.9 jit_solution(6673984589621143172)
XLA Ops:
  0.0 1.0 copy.29
  1.0 0.1 copy.30
  1.1 1.0 all_to_all.16
  2.1 28.3 %all-to-all-start = ((f32[64,1,432]{2,1,0:T(1,128)}), f32[64,1,432]{2,1,0:T(1,128)}, u32[]{:S(2)}, u32[]{:S(2)}) async-start(f32[64,1,432]{2,1,0:T(1,128)} %all_to_all.16), calls=%async_computation | async-start | bytes 262144 | tf_op jit(solution)/shard_map/all_to_all | solution.py:54
  30.4 1.0 fusion.32
  31.4 0.7 broadcast_compare_fusion
  32.1 0.7 fusion.41
  32.8 0.7 pad_maximum_fusion.19
  33.5 0.1 eq.36
  33.6 0.2 fusion.38
  33.8 1.4 %multiply_subtract_fusion = (f32[36,32,353]{2,1,0:T(8,128)S(1)}, f32[36,32,353]{2,1,0:T(8,128)S(1)}) fusion(f32[32,353]{1,0:T(8,128)S(1)} %get-tuple-element.17, f32[36,353]{1,0:T(8,128)} %get-tuple-element.16, f32[32,353]{1,0:T(8,128)S(1)} %get-tuple-element.18, f32[36,353]{1,0:T(8,128)} %get-tuple-element.15), kind=kLoop, calls=%fused_computation.5 | loop fusion | flops 2439936 | bytes 3445280 | tf_op jit(solution)/shard_map/sub | solution.py:31
  35.2 13.5 %all-to-all-done = f32[64,1,432]{2,1,0:T(1,128)} async-done(((f32[64,1,432]{2,1,0:T(1,128)}), f32[64,1,432]{2,1,0:T(1,128)}, u32[]{:S(2)}, u32[]{:S(2)}) %all-to-all-start) | async-done | bytes 110624 | tf_op jit(solution)/shard_map/all_to_all | solution.py:54
  48.7 1.7 %copy.32 = f32[64,1,432]{0,2,1:T(8,128)} copy(f32[64,1,432]{2,1,0:T(1,128)} %all-to-all-done) | data formatting | bytes 221184 | tf_op jit(solution)/shard_map/all_to_all | solution.py:54
  50.4 1.7 %reshape.159 = f32[64,24,18]{0,2,1:T(8,128)} reshape(f32[64,1,432]{0,2,1:T(8,128)} %copy.32) | data formatting | bytes 221184 | tf_op jit(solution)/shard_map/reshape | solution.py:55
  52.1 2.2 %copy.33 = f32[24,64,18]{2,1,0:T(8,128)} copy(f32[24,64,18]{1,2,0:T(8,128)} %bitcast.26) | data formatting | bytes 221184 | tf_op jit(solution)/shard_map/transpose | solution.py:56
  54.3 2.1 %reshape.160 = f32[24,1152]{1,0:T(8,128)} reshape(f32[24,64,18]{2,1,0:T(8,128)} %copy.33) | data formatting | bytes 221184 | tf_op jit(solution)/shard_map/reshape | solution.py:56
  56.4 2.1 %fusion.4 = f32[24,706]{1,0:T(8,128)S(1)} fusion(f32[24,1152]{1,0:T(8,128)} %reshape.160, f32[1152,353]{1,0:T(8,128)S(1)} %bitcast.22, f32[1152,353]{1,0:T(8,128)S(1)} %bitcast.20, f32[8,706]{1,0:T(8,128)} %pad_maximum_fusion.19), kind=kOutput, calls=%fused_computation.7 | convolution fusion | flops 117947184 | bytes 3454208 | tf_op jit(solution)/shard_map/dot_general | solution.py:63
  58.6 0.0 copy-done
  58.6 2.4 %fusion.2 = f32[24,1152]{1,0:T(8,128)} fusion(f32[24,1152]{1,0:T(8,128)S(1)} %copy-done, f32[24,706]{1,0:T(8,128)S(1)} %fusion.4, f32[1152,353]{1,0:T(8,128)S(1)} %bitcast.23, f32[1152,353]{1,0:T(8,128)S(1)} %bitcast.21, pred[24]{0:T(512)(128)(4,1)S(1)} %eq.36), kind=kOutput, calls=%fused_computation.3 | convolution fusion | flops 117957888 | bytes 3542232 | tf_op jit(solution)/shard_map/dot_general | solution.py:65
  60.9 1.8 %concatenate.51 = f32[3,8,64,18]{3,2,1,0:T(8,128)S(1)} reshape(f32[24,1152]{1,0:T(8,128)} %fusion.2) | data formatting | bytes 221184 | tf_op jit(solution)/shard_map/concatenate | solution.py:74
  62.7 0.3 copy.35
  63.1 0.3 rev.6
  63.4 0.0 copy-start.3
  63.4 0.3 rev.7
  63.8 0.1 fusion.51
  63.9 0.1 pad_maximum_fusion.18
  64.0 0.2 concatenate.50
  64.2 0.1 copy.34
  64.3 0.2 fusion.7
  64.5 0.8 copy.36
  65.4 5.9 %all-to-all-start.1 = ((f32[64,1,660]{2,1,0:T(1,128)}), f32[64,1,660]{2,1,0:T(1,128)S(1)}, u32[]{:S(2)}, u32[]{:S(2)}) async-start(f32[64,1,660]{2,1,0:T(1,128)} %copy.36), calls=%async_computation.1 | async-start | bytes 393216 | tf_op jit(solution)/shard_map/all_to_all | solution.py:81
  71.3 2.9 %collective-permute-start = (f32[8,1,192]{2,1,0:T(1,128)S(1)}, f32[8,1,192]{2,1,0:T(1,128)S(1)}, u32[]{:S(2)}, u32[]{:S(2)}) collective-permute-start(f32[8,1,192]{2,1,0:T(1,128)S(1)} %copy.38), channel_id=1, source_target_pairs={{0,1},{1,2},{2,3},{3,4},{4,5},{5,6},{6,7},{7,8},{8,9},{9,10},{10,1... | collective-permute-start | bytes 18440 | tf_op jit(solution)/shard_map/ppermute | solution.py:14
  74.4 0.1 fusion.46
  74.5 16.0 %all-to-all-done.1 = f32[64,1,660]{2,1,0:T(1,128)S(1)} async-done(((f32[64,1,660]{2,1,0:T(1,128)}), f32[64,1,660]{2,1,0:T(1,128)S(1)}, u32[]{:S(2)}, u32[]{:S(2)}) %all-to-all-start.1) | async-done | bytes 168992 | tf_op jit(solution)/shard_map/all_to_all | solution.py:81
  90.6 0.5 reduce
  91.0 0.1 reshape.162
  91.2 0.1 slice.146
  91.3 0.1 copy.37
  91.5 9.7 %collective-permute-start.1 = (f32[3,18,192]{2,1,0:T(8,128)S(1)}, f32[3,18,192]{2,1,0:T(8,128)S(1)}, u32[]{:S(2)}, u32[]{:S(2)}) collective-permute-start(f32[3,18,192]{2,1,0:T(8,128)S(1)} %pad_maximum_fusion.17), channel_id=1, source_target_pairs={{0,64},{64,128},{128,192},{192,256},{256,320},{320,384},{384,448},... | collective-permute-start | bytes 124424 | tf_op jit(solution)/shard_map/ppermute | solution.py:14
  101.2 0.0 collective-permute-done
  101.2 0.1 fusion.26
  101.3 0.1 copy.42
  101.5 1.9 %collective-permute-start.2 = (f32[2,18,192]{2,1,0:T(8,128)S(1)}, f32[2,18,192]{2,1,0:T(8,128)S(1)}, u32[]{:S(2)}, u32[]{:S(2)}) collective-permute-start(f32[2,18,192]{2,1,0:T(8,128)S(1)} %get-tuple-element.10), channel_id=1, source_target_pairs={{64,0},{128,64},{192,128},{256,192},{320,256},{384,320},{448,384},... | collective-permute-start | bytes 82952 | tf_op jit(solution)/shard_map/ppermute | solution.py:14
  103.4 0.0 collective-permute-done.1
  103.5 3.5 %collective-permute-done.2 = f32[2,18,192]{2,1,0:T(8,128)S(1)} collective-permute-done((f32[2,18,192]{2,1,0:T(8,128)S(1)}, f32[2,18,192]{2,1,0:T(8,128)S(1)}, u32[]{:S(2)}, u32[]{:S(2)}) %collective-permute-start.2) | collective-permute-done | bytes 27680 | tf_op jit(solution)/shard_map/ppermute | solution.py:14
  106.9 0.1 fusion.17
  107.0 0.1 fusion.20
  107.1 0.7 copy.43
  (28 shorter events, 0.4 us)
Async XLA Ops:
  2.1 46.6 %all-to-all-start = ((f32[64,1,432]{2,1,0:T(1,128)}), f32[64,1,432]{2,1,0:T(1,128)}, u32[]{:S(2)}, u32[]{:S(2)}) async-start(f32[64,1,432]{2,1,0:T(1,128)} %all_to_all.16), calls=%async_computation | async-start | bytes 262144 | tf_op jit(solution)/shard_map/all_to_all | solution.py:54
  56.4 2.1 %copy-start = (f32[24,1152]{1,0:T(8,128)S(1)}, f32[24,1152]{1,0:T(8,128)}, u32[]{:S(2)}) copy-start(f32[24,1152]{1,0:T(8,128)} %reshape.160) | copy-start | bytes 331780
  60.9 2.1 %copy-start.1 = (f32[24,1152]{1,0:T(8,128)S(1)}, f32[24,1152]{1,0:T(8,128)}, u32[]{:S(2)}) copy-start(f32[24,1152]{1,0:T(8,128)} %fusion.2) | copy-start | bytes 331780
  63.0 8.2 %slice-start = ((f32[8,18,192]{2,0,1:T(8,128)}), f32[8,1,192]{2,0,1:T(8,128)S(1)}, s32[]{:S(2)}) async-start(f32[8,18,192]{2,0,1:T(8,128)} %param.6), calls=%async_computation.2 | async-start | bytes 16384 | tf_op jit(solution)/shard_map/slice | solution.py:51
  63.1 11.2 %copy-start.2 = (f32[8,18,192]{2,0,1:T(8,128)S(1)}, f32[8,18,192]{2,0,1:T(8,128)}, u32[]{:S(2)}) copy-start(f32[8,18,192]{2,0,1:T(8,128)} %param.6) | copy-start | bytes 331780
  63.4 10.8 %copy-start.3 = (f32[8,18,192]{2,0,1:T(8,128)S(1)}, f32[8,18,192]{2,0,1:T(8,128)}, u32[]{:S(2)}) copy-start(f32[8,18,192]{2,0,1:T(8,128)} %param.7) | copy-start | bytes 331780
  65.4 25.2 %all-to-all-start.1 = ((f32[64,1,660]{2,1,0:T(1,128)}), f32[64,1,660]{2,1,0:T(1,128)S(1)}, u32[]{:S(2)}, u32[]{:S(2)}) async-start(f32[64,1,660]{2,1,0:T(1,128)} %copy.36), calls=%async_computation.1 | async-start | bytes 393216 | tf_op jit(solution)/shard_map/all_to_all | solution.py:81
  71.3 29.9 %collective-permute-start = (f32[8,1,192]{2,1,0:T(1,128)S(1)}, f32[8,1,192]{2,1,0:T(1,128)S(1)}, u32[]{:S(2)}, u32[]{:S(2)}) collective-permute-start(f32[8,1,192]{2,1,0:T(1,128)S(1)} %copy.38), channel_id=1, source_target_pairs={{0,1},{1,2},{2,3},{3,4},{4,5},{5,6},{6,7},{7,8},{8,9},{9,10},{10,1... | collective-permute-start | bytes 18440 | tf_op jit(solution)/shard_map/ppermute | solution.py:14
  91.5 12.0 %collective-permute-start.1 = (f32[3,18,192]{2,1,0:T(8,128)S(1)}, f32[3,18,192]{2,1,0:T(8,128)S(1)}, u32[]{:S(2)}, u32[]{:S(2)}) collective-permute-start(f32[3,18,192]{2,1,0:T(8,128)S(1)} %pad_maximum_fusion.17), channel_id=1, source_target_pairs={{0,64},{64,128},{128,192},{192,256},{256,320},{320,384},{384,448},... | collective-permute-start | bytes 124424 | tf_op jit(solution)/shard_map/ppermute | solution.py:14
  101.5 5.4 %collective-permute-start.2 = (f32[2,18,192]{2,1,0:T(8,128)S(1)}, f32[2,18,192]{2,1,0:T(8,128)S(1)}, u32[]{:S(2)}, u32[]{:S(2)}) collective-permute-start(f32[2,18,192]{2,1,0:T(8,128)S(1)} %get-tuple-element.10), channel_id=1, source_target_pairs={{64,0},{128,64},{192,128},{256,192},{320,256},{384,320},{448,384},... | collective-permute-start | bytes 82952 | tf_op jit(solution)/shard_map/ppermute | solution.py:14

commit v8 on v7

--- a/solution.py
+++ b/solution.py
@@ -50,36 +50,49 @@
 
     east_halo = shifted_from(courant_east[:, -1:], "lon", 1)
 
-    outgoing = state.reshape(n_rows * n_cols, n_comp).T.reshape(lon_count, -1)
-    incoming = lax.all_to_all(outgoing, "lon", split_axis=0, concat_axis=0, tiled=True)
-    lines = incoming.reshape(lon_count, group * n_rows, n_cols)
-    lines = jnp.transpose(lines, (1, 0, 2)).reshape(group * n_rows, n_full)
+    def through_filter(state, cutoff, filter_mask):
+        outgoing = state.reshape(n_rows * n_cols, n_comp).T.reshape(lon_count, -1)
+        incoming = lax.all_to_all(outgoing, "lon", split_axis=0, concat_axis=0, tiled=True)
+        lines = incoming.reshape(lon_count, group * n_rows, n_cols)
+        lines = jnp.transpose(lines, (1, 0, 2)).reshape(group * n_rows, n_full)
 
-    fourier = build_table(n_full, n_waves, 32)
-    waves = jnp.arange(n_waves, dtype=jnp.int32)
-    weights = jnp.where(waves == 0, 1.0 / n_full, 2.0 / n_full).astype(jnp.float32)
-    kept = jnp.where(waves[None, :] <= cutoff[:, None], weights[None, :], 0.0)
-    kept_both = jnp.tile(jnp.concatenate([kept, kept], axis=1), (group, 1))
-    coeffs = jnp.dot(lines, fourier, precision=lax.Precision.HIGH)
-    coeffs = coeffs * kept_both
-    filtered = lax.dot_general(
-        coeffs, fourier, (((1,), (1,)), ((), ())), precision=lax.Precision.HIGH
-    )
-    keep = jnp.tile(filter_mask, group)[:, None] == 1
-    smooth = jnp.where(keep, filtered, lines).reshape(group, n_rows, n_full)
+        fourier = build_table(n_full, n_waves, 32)
+        waves = jnp.arange(n_waves, dtype=jnp.int32)
+        weights = jnp.where(waves == 0, 1.0 / n_full, 2.0 / n_full).astype(jnp.float32)
+        kept = jnp.where(waves[None, :] <= cutoff[:, None], weights[None, :], 0.0)
+        kept_both = jnp.tile(jnp.concatenate([kept, kept], axis=1), (group, 1))
+        coeffs = jnp.dot(lines, fourier, precision=lax.Precision.HIGH)
+        coeffs = coeffs * kept_both
+        filtered = lax.dot_general(
+            coeffs, fourier, (((1,), (1,)), ((), ())), precision=lax.Precision.HIGH
+        )
+        keep = jnp.tile(filter_mask, group)[:, None] == 1
+        smooth = jnp.where(keep, filtered, lines).reshape(group, n_rows, n_full)
 
-    south_pole = smooth[:, 1::-1]
-    north_pole = smooth[:, : n_rows - 3 : -1]
-    pole = jnp.roll(jnp.where(lat_index == 0, south_pole, north_pole), half, axis=2)
-    rows_out = jnp.concatenate([pole, smooth], axis=1)
+        south_pole = smooth[:, 1::-1]
+        north_pole = smooth[:, : n_rows - 3 : -1]
+        pole = jnp.roll(jnp.where(lat_index == 0, south_pole, north_pole), half, axis=2)
+        rows_out = jnp.concatenate([pole, smooth], axis=1)
 
-    tiles = rows_out.reshape(group, n_send, lon_count, n_cols)
-    left = jnp.roll(tiles[..., -2:], 1, axis=2)
-    right = jnp.roll(tiles[..., :2], -1, axis=2)
-    windows = jnp.concatenate([left, tiles, right], axis=3)
-    windows = jnp.transpose(windows, (2, 0, 1, 3)).reshape(lon_count, -1)
-    back = lax.all_to_all(windows, "lon", split_axis=0, concat_axis=0, tiled=True)
-    ext = back.reshape(n_comp, n_send * n_win).T.reshape(n_send, n_win, n_comp)
+        tiles = rows_out.reshape(group, n_send, lon_count, n_cols)
+        left = jnp.roll(tiles[..., -2:], 1, axis=2)
+        right = jnp.roll(tiles[..., :2], -1, axis=2)
+        windows = jnp.concatenate([left, tiles, right], axis=3)
+        windows = jnp.transpose(windows, (2, 0, 1, 3)).reshape(lon_count, -1)
+        back = lax.all_to_all(windows, "lon", split_axis=0, concat_axis=0, tiled=True)
+        ext = back.reshape(n_comp, n_send * n_win).T.reshape(n_send, n_win, n_comp)
+        return ext
+
+    def as_state(state, cutoff, filter_mask):
+        from_west = shifted_from(state[:, -2:], "lon", 1)
+        from_east = shifted_from(state[:, :2], "lon", -1)
+        rows = jnp.concatenate([from_west, state, from_east], axis=1)
+        return jnp.concatenate([jnp.zeros_like(rows[:2]), rows], axis=0)
+
+    reach = n_lat // 4
+    first = lat_index * n_rows
+    plain = (first >= reach) & (first + n_rows - 1 <= n_lat - 1 - reach)
+    ext = lax.cond(plain, as_state, through_filter, state, cutoff, filter_mask)
     own = ext[2:]
     centre = own[:, 2:-2]
 

time: 108 us -> 120 us (1.11)
  blocking collectives: 0 us -> 24.2 us
  starting transfers between devices: 48.6 us -> 38.2 us
  waiting for transfers between devices: 33 us -> 28.3 us
  other arithmetic: 5.98 us -> 7.71 us
    all_to_all x0 -> x1, blocking collectives: none -> 24.2 us  [through_filter(): lax.all_to_all(windows, 'lon', split_axis=0, concat_axis=0, tiled=True)]
    all_to_all x2 -> x1, waiting for transfers between devices: 29.5 us -> 13.5 us  [through_filter(): lax.all_to_all(outgoing, 'lon', split_axis=0, concat_axis=0, tiled=True)]
    ppermute x3, waiting for transfers between devices: 3.46 us -> 14.8 us  [shifted_from(): return lax.ppermute(block, axis, route)]
    all_to_all x2 -> x1, starting transfers between devices: 34.1 us -> 28.3 us  [through_filter(): lax.all_to_all(outgoing, 'lon', split_axis=0, concat_axis=0, tiled=True)]
    ppermute x3, starting transfers between devices: 14.5 us -> 9.89 us  [shifted_from(): return lax.ppermute(block, axis, route)]
    slice x1, local copies, waits for them, and re-layouts: 0.01 us -> 1.52 us  [local(): courant_north[-1:]]
    concatenate x4 -> x5, local copies, waits for them, and re-layouts: 2.44 us -> 2.45 us  [the longest x4 2.44 us: through_filter(): rows_out = jnp.concatenate([pole, smooth], axis=1)]
  transfers between devices with their start and end apart: 5 -> 4, of which waited for: 3 -> 2; matrix products, arithmetic and copies ran while one was open for 6% -> 5% of each run, Pallas kernels for 0% -> 0%
where the time goes in v8:
time: 120 us; the launch traced here: 119 us
  starting transfers between devices  38.2 us (32%)
  waiting for transfers between devices  28.3 us (24%)
  blocking collectives  24.2 us (20%)
  local copies, waits for them, and re-layouts  16 us (13%)
  other arithmetic  7.71 us (6%)
  matrix products  4.48 us (4%)
    all_to_all x1, starting transfers between devices, through_filter(): lax.all_to_all(outgoing, 'lon', split_axis=0, concat_axis=0, tiled=True)  28.3 us
    all_to_all x1, blocking collectives, through_filter(): lax.all_to_all(windows, 'lon', split_axis=0, concat_axis=0, tiled=True)  24.2 us
    ppermute x3, waiting for transfers between devices, shifted_from(): return lax.ppermute(block, axis, route)  14.8 us
    all_to_all x1, waiting for transfers between devices, through_filter(): lax.all_to_all(outgoing, 'lon', split_axis=0, concat_axis=0, tiled=True)  13.5 us
    ppermute x3, starting transfers between devices, shifted_from(): return lax.ppermute(block, axis, route)  9.89 us
    all_to_all x2, local copies, waits for them, and re-layouts, through_filter(): lax.all_to_all(outgoing, 'lon', split_axis=0, concat_axis=0, tiled=True)  2.75 us
    concatenate x4, local copies, waits for them, and re-layouts, through_filter(): rows_out = jnp.concatenate([pole, smooth], axis=1)  2.44 us
  transfers between devices with their start and end apart: 4, of which 2 were waited for; matrix products, arithmetic and copies ran while one was open for 5% of the time, Pallas kernels for 0%

profile of v8, /device:TPU:1, one launch (start us, length us, event | category | flops | bytes accessed | tf_op | source)
XLA Modules:
  0.0 119.2 jit_solution(12051575877589783644)
XLA Ops:
  0.0 1.5 %slice.126 = f32[1,18,192]{2,0,1:T(1,128)} slice(f32[8,18,192]{2,0,1:T(8,128)} %param.9), slice={[7:8], [0:18], [0:192]} | slice | bytes 27648 | tf_op jit(solution)/shard_map/slice | solution.py:100
  1.5 89.6 %conditional.1 = (f32[10,22,192]{2,1,0:T(8,128)S(1)}) conditional(s32[]{:T(128)} %convert_element_type.37, (s32[]{:T(128)}, s32[8]{0:T(128)}, f32[8,18,192]{2,0,1:T(8,128)}, s32[8]{0:T(128)}) %tuple.11, (f32[8,18,192]{2,0,1:T(8,128)}) %tuple.16), branch_computations={%region_0.1_spmd, %region_1.2_spmd} | conditional | flops 238967072 | bytes 17349574 | solution.py:95
  1.5 1.0 copy.56
  2.5 0.1 copy.48
  2.6 1.0 all_to_all.12
  3.7 28.3 %all-to-all-start = ((f32[64,1,432]{2,1,0:T(1,128)}), f32[64,1,432]{2,1,0:T(1,128)}, u32[]{:S(2)}, u32[]{:S(2)}) async-start(f32[64,1,432]{2,1,0:T(1,128)} %all_to_all.12), calls=%async_computation | async-start | bytes 262144 | tf_op jit(solution)/shard_map/cond/branch_0_fun/all_to_all | solution.py:55
  32.0 1.0 fusion.15
  33.0 0.7 broadcast_compare_fusion
  33.6 0.7 fusion.24
  34.3 0.7 pad_maximum_fusion.14
  35.0 0.1 eq.29
  35.1 0.2 fusion.21
  35.3 1.4 %multiply_subtract_fusion = (f32[36,32,353]{2,1,0:T(8,128)S(1)}, f32[36,32,353]{2,1,0:T(8,128)S(1)}) fusion(f32[32,353]{1,0:T(8,128)S(1)} %get-tuple-element.52, f32[36,353]{1,0:T(8,128)} %get-tuple-element.51, f32[32,353]{1,0:T(8,128)S(1)} %get-tuple-element.53, f32[36,353]{1,0:T(8,128)} %get-tuple-element.50), kind=kLoop, calls=%fused_computation.8 | loop fusion | flops 2439936 | bytes 3445280 | tf_op jit(solution)/shard_map/cond/branch_0_fun/sub | solution.py:31
  36.7 13.5 %all-to-all-done = f32[64,1,432]{2,1,0:T(1,128)} async-done(((f32[64,1,432]{2,1,0:T(1,128)}), f32[64,1,432]{2,1,0:T(1,128)}, u32[]{:S(2)}, u32[]{:S(2)}) %all-to-all-start) | async-done | bytes 110624 | tf_op jit(solution)/shard_map/cond/branch_0_fun/all_to_all | solution.py:55
  50.2 1.7 %copy.50 = f32[64,1,432]{0,2,1:T(8,128)} copy(f32[64,1,432]{2,1,0:T(1,128)} %all-to-all-done) | data formatting | bytes 221184 | tf_op jit(solution)/shard_map/cond/branch_0_fun/all_to_all | solution.py:55
  51.9 1.7 %reshape.152 = f32[64,24,18]{0,2,1:T(8,128)} reshape(f32[64,1,432]{0,2,1:T(8,128)} %copy.50) | data formatting | bytes 221184 | tf_op jit(solution)/shard_map/cond/branch_0_fun/reshape | solution.py:56
  53.6 2.2 %copy.51 = f32[24,64,18]{2,1,0:T(8,128)} copy(f32[24,64,18]{1,2,0:T(8,128)} %bitcast.24) | data formatting | bytes 221184 | tf_op jit(solution)/shard_map/cond/branch_0_fun/transpose | solution.py:57
  55.8 2.1 %reshape.153 = f32[24,1152]{1,0:T(8,128)} reshape(f32[24,64,18]{2,1,0:T(8,128)} %copy.51) | data formatting | bytes 221184 | tf_op jit(solution)/shard_map/cond/branch_0_fun/reshape | solution.py:57
  57.9 2.1 %fusion.4 = f32[24,706]{1,0:T(8,128)S(1)} fusion(f32[24,1152]{1,0:T(8,128)} %reshape.153, f32[1152,353]{1,0:T(8,128)S(1)} %bitcast.22, f32[1152,353]{1,0:T(8,128)S(1)} %bitcast.20, f32[8,706]{1,0:T(8,128)} %pad_maximum_fusion.14), kind=kOutput, calls=%fused_computation.10 | convolution fusion | flops 117947184 | bytes 3454208 | tf_op jit(solution)/shard_map/cond/branch_0_fun/dot_general | solution.py:64
  60.0 2.4 %fusion.2 = f32[24,1152]{1,0:T(8,128)} fusion(f32[24,1152]{1,0:T(8,128)S(1)} %copy-done, f32[24,706]{1,0:T(8,128)S(1)} %fusion.4, f32[1152,353]{1,0:T(8,128)S(1)} %bitcast.23, f32[1152,353]{1,0:T(8,128)S(1)} %bitcast.21, pred[24]{0:T(512)(128)(4,1)S(1)} %eq.29), kind=kOutput, calls=%fused_computation.6 | convolution fusion | flops 117957888 | bytes 3542232 | tf_op jit(solution)/shard_map/cond/branch_0_fun/dot_general | solution.py:66
  62.4 1.8 %concatenate.41 = f32[3,8,64,18]{3,2,1,0:T(8,128)S(1)} reshape(f32[24,1152]{1,0:T(8,128)} %fusion.2) | data formatting | bytes 221184 | tf_op jit(solution)/shard_map/cond/branch_0_fun/concatenate | solution.py:75
  64.2 0.3 copy.53
  64.6 0.3 rev.4
  64.9 0.3 rev.5
  65.2 0.1 fusion.52
  65.3 0.1 pad_maximum_fusion.13
  65.4 0.2 concatenate.40
  65.6 0.1 copy.52
  65.7 0.2 fusion.7
  66.0 0.2 copy.54
  66.2 24.2 %all_to_all.15 = f32[64,1,660]{2,1,0:T(1,128)S(1)} all-to-all(f32[64,1,660]{2,1,0:T(1,128)S(1)} %copy.54), channel_id=1, replica_groups=mesh['lat'=16,'lon'=64] {'lon'}, dimensions={0} | all-to-all | bytes 337920 | tf_op jit(solution)/shard_map/cond/branch_0_fun/all_to_all | solution.py:82
  90.4 0.5 reduce
  90.8 0.1 reshape.155
  91.0 0.1 copy.55
  91.2 0.0 copy-start.3
  91.2 0.8 pad_maximum_fusion.18
  92.0 5.6 %collective-permute-start.3 = (f32[3,18,192]{2,0,1:T(4,128)S(1)}, f32[3,18,192]{2,0,1:T(4,128)S(1)}, u32[]{:S(2)}, u32[]{:S(2)}) collective-permute-start(f32[3,18,192]{2,0,1:T(4,128)S(1)} %pad_maximum_fusion.18), channel_id=1, source_target_pairs={{0,64},{64,128},{128,192},{192,256},{256,320},{320,384},{384,448},... | collective-permute-start | bytes 124424 | tf_op jit(solution)/shard_map/ppermute | solution.py:14
  97.7 1.9 %collective-permute-start.4 = (f32[2,18,192]{2,0,1:T(2,128)S(1)}, f32[2,18,192]{2,0,1:T(2,128)S(1)}, u32[]{:S(2)}, u32[]{:S(2)}) collective-permute-start(f32[2,18,192]{2,0,1:T(2,128)S(1)} %copy.74), channel_id=1, source_target_pairs={{64,0},{128,64},{192,128},{256,192},{320,256},{384,320},{448,384},... | collective-permute-start | bytes 82952 | tf_op jit(solution)/shard_map/ppermute | solution.py:14
  99.6 0.7 slice.118
  100.3 2.3 %collective-permute-start.2 = (f32[8,1,192]{2,0,1:T(8,128)S(1)}, f32[8,1,192]{2,0,1:T(8,128)S(1)}, u32[]{:S(2)}, u32[]{:S(2)}) collective-permute-start(f32[8,1,192]{2,0,1:T(8,128)S(1)} %slice.118), channel_id=1, source_target_pairs={{0,1},{1,2},{2,3},{3,4},{4,5},{5,6},{6,7},{7,8},{8,9},{9,10},{10,1... | collective-permute-start | bytes 18440 | tf_op jit(solution)/shard_map/ppermute | solution.py:14
  102.7 0.1 fusion.53
  102.8 0.1 fusion.49
  103.0 0.1 copy.67
  103.0 14.8 %collective-permute-done.2 = f32[8,1,192]{2,0,1:T(8,128)S(1)} collective-permute-done((f32[8,1,192]{2,0,1:T(8,128)S(1)}, f32[8,1,192]{2,0,1:T(8,128)S(1)}, u32[]{:S(2)}, u32[]{:S(2)}) %collective-permute-start.2) | collective-permute-done | bytes 6176 | tf_op jit(solution)/shard_map/ppermute | solution.py:14
  117.8 0.2 fusion.40
  118.0 0.0 collective-permute-done.3
  118.1 0.3 fusion.33
  118.4 0.8 fusion.43
  (26 shorter events, 0.4 us)
Async XLA Ops:
  3.7 46.5 %all-to-all-start = ((f32[64,1,432]{2,1,0:T(1,128)}), f32[64,1,432]{2,1,0:T(1,128)}, u32[]{:S(2)}, u32[]{:S(2)}) async-start(f32[64,1,432]{2,1,0:T(1,128)} %all_to_all.12), calls=%async_computation | async-start | bytes 262144 | tf_op jit(solution)/shard_map/cond/branch_0_fun/all_to_all | solution.py:55
  57.9 2.1 %copy-start = (f32[24,1152]{1,0:T(8,128)S(1)}, f32[24,1152]{1,0:T(8,128)}, u32[]{:S(2)}) copy-start(f32[24,1152]{1,0:T(8,128)} %reshape.153) | copy-start | bytes 331780 | tf_op jit(solution)/shard_map/cond
  62.4 2.1 %copy-start.1 = (f32[24,1152]{1,0:T(8,128)S(1)}, f32[24,1152]{1,0:T(8,128)}, u32[]{:S(2)}) copy-start(f32[24,1152]{1,0:T(8,128)} %fusion.2) | copy-start | bytes 331780 | tf_op jit(solution)/shard_map/cond
  91.2 26.6 %copy-start.3 = (f32[8,18,192]{2,0,1:T(8,128)S(1)}, f32[8,18,192]{2,0,1:T(8,128)}, u32[]{:S(2)}) copy-start(f32[8,18,192]{2,0,1:T(8,128)} %param.8) | copy-start | bytes 331780
  92.0 26.0 %collective-permute-start.3 = (f32[3,18,192]{2,0,1:T(4,128)S(1)}, f32[3,18,192]{2,0,1:T(4,128)S(1)}, u32[]{:S(2)}, u32[]{:S(2)}) collective-permute-start(f32[3,18,192]{2,0,1:T(4,128)S(1)} %pad_maximum_fusion.18), channel_id=1, source_target_pairs={{0,64},{64,128},{128,192},{192,256},{256,320},{320,384},{384,448},... | collective-permute-start | bytes 124424 | tf_op jit(solution)/shard_map/ppermute | solution.py:14
  97.7 20.4 %collective-permute-start.4 = (f32[2,18,192]{2,0,1:T(2,128)S(1)}, f32[2,18,192]{2,0,1:T(2,128)S(1)}, u32[]{:S(2)}, u32[]{:S(2)}) collective-permute-start(f32[2,18,192]{2,0,1:T(2,128)S(1)} %copy.74), channel_id=1, source_target_pairs={{64,0},{128,64},{192,128},{256,192},{320,256},{384,320},{448,384},... | collective-permute-start | bytes 82952 | tf_op jit(solution)/shard_map/ppermute | solution.py:14
  100.3 17.8 %copy-start.2 = (f32[8,18,192]{2,0,1:T(8,128)S(1)}, f32[8,18,192]{2,0,1:T(8,128)}, u32[]{:S(2)}) copy-start(f32[8,18,192]{2,0,1:T(8,128)} %param.9) | copy-start | bytes 331780
  100.3 17.4 %collective-permute-start.2 = (f32[8,1,192]{2,0,1:T(8,128)S(1)}, f32[8,1,192]{2,0,1:T(8,128)S(1)}, u32[]{:S(2)}, u32[]{:S(2)}) collective-permute-start(f32[8,1,192]{2,0,1:T(8,128)S(1)} %slice.118), channel_id=1, source_target_pairs={{0,1},{1,2},{2,3},{3,4},{4,5},{5,6},{6,7},{7,8},{8,9},{9,10},{10,1... | collective-permute-start | bytes 18440 | tf_op jit(solution)/shard_map/ppermute | solution.py:14

commit v9 on v7

--- a/solution.py
+++ b/solution.py
@@ -52,21 +52,29 @@
 
     outgoing = state.reshape(n_rows * n_cols, n_comp).T.reshape(lon_count, -1)
     incoming = lax.all_to_all(outgoing, "lon", split_axis=0, concat_axis=0, tiled=True)
-    lines = incoming.reshape(lon_count, group * n_rows, n_cols)
-    lines = jnp.transpose(lines, (1, 0, 2)).reshape(group * n_rows, n_full)
+    blocks = incoming.reshape(lon_count, group * n_rows, n_cols)
 
     fourier = build_table(n_full, n_waves, 32)
     waves = jnp.arange(n_waves, dtype=jnp.int32)
     weights = jnp.where(waves == 0, 1.0 / n_full, 2.0 / n_full).astype(jnp.float32)
     kept = jnp.where(waves[None, :] <= cutoff[:, None], weights[None, :], 0.0)
     kept_both = jnp.tile(jnp.concatenate([kept, kept], axis=1), (group, 1))
-    coeffs = jnp.dot(lines, fourier, precision=lax.Precision.HIGH)
+    coeffs = lax.dot_general(
+        blocks,
+        fourier.reshape(lon_count, n_cols, -1),
+        (((0, 2), (0, 1)), ((), ())),
+        precision=lax.Precision.HIGH,
+    )
     coeffs = coeffs * kept_both
     filtered = lax.dot_general(
-        coeffs, fourier, (((1,), (1,)), ((), ())), precision=lax.Precision.HIGH
+        coeffs,
+        fourier.reshape(lon_count, n_cols, -1),
+        (((1,), (2,)), ((), ())),
+        precision=lax.Precision.HIGH,
     )
-    keep = jnp.tile(filter_mask, group)[:, None] == 1
-    smooth = jnp.where(keep, filtered, lines).reshape(group, n_rows, n_full)
+    keep = jnp.tile(filter_mask, group)[:, None, None] == 1
+    smooth = jnp.where(keep, filtered, jnp.transpose(blocks, (1, 0, 2)))
+    smooth = smooth.reshape(group, n_rows, n_full)
 
     south_pole = smooth[:, 1::-1]
     north_pole = smooth[:, : n_rows - 3 : -1]

time: 108 us -> 109 us (level)
  waiting for transfers between devices: 33 us -> 27.3 us
  starting transfers between devices: 48.6 us -> 54 us
  other arithmetic: 5.98 us -> 3.15 us
  local copies, waits for them, and re-layouts: 15.4 us -> 18 us
    all_to_all x1, waiting for transfers between devices: 13.5 us -> 8.94 us  [local(): lax.all_to_all(outgoing, 'lon', split_axis=0, concat_axis=0, tiled=True)]
    all_to_all x1, starting transfers between devices: 5.87 us -> 10.4 us  [local(): lax.all_to_all(windows, 'lon', split_axis=0, concat_axis=0, tiled=True)]
    add x0 -> x2, local copies, waits for them, and re-layouts: none -> 3.69 us  [build_table(): sin_t = (sa * cb + ca * sb).reshape(n_full, n_waves)]
    sub x0 -> x2, local copies, waits for them, and re-layouts: none -> 3.66 us  [build_table(): cos_t = (ca * cb - sa * sb).reshape(n_full, n_waves)]
    transpose x1 -> x0, local copies, waits for them, and re-layouts: 2.18 us -> none  [local(): lines = jnp.transpose(lines, (1, 0, 2)).reshape(group * n_rows, n_full)]
    concatenate x4 -> x3, local copies, waits for them, and re-layouts: 2.44 us -> 0.39 us  [local(): rows_out = jnp.concatenate([pole, smooth], axis=1)]
    reshape x2, local copies, waits for them, and re-layouts: 3.82 us -> 2.03 us  [the longest x1 1.66 us: local(): blocks = incoming.reshape(lon_count, group * n_rows, n_cols)]
    select_n x0 -> x1, local copies, waits for them, and re-layouts: none -> 1.32 us  [local(): smooth = jnp.where(keep, filtered, jnp.transpose(blocks, (1, 0, 2)))]
  transfers between devices with their start and end apart: 5 -> 5, of which waited for: 3 -> 3; matrix products, arithmetic and copies ran while one was open for 6% -> 10% of each run, Pallas kernels for 0% -> 0%
where the time goes in v9:
time: 109 us; the launch traced here: 108 us
  starting transfers between devices  54 us (50%)
  waiting for transfers between devices  27.3 us (25%)
  local copies, waits for them, and re-layouts  18 us (17%)
  matrix products  5.2 us (5%)
  other arithmetic  3.15 us (3%)
    all_to_all x1, starting transfers between devices, local(): lax.all_to_all(outgoing, 'lon', split_axis=0, concat_axis=0, tiled=True)  28.3 us
    all_to_all x1, waiting for transfers between devices, local(): lax.all_to_all(windows, 'lon', split_axis=0, concat_axis=0, tiled=True)  15.3 us
    ppermute x3, starting transfers between devices, shifted_from(): return lax.ppermute(block, axis, route)  15.3 us
    all_to_all x1, starting transfers between devices, local(): lax.all_to_all(windows, 'lon', split_axis=0, concat_axis=0, tiled=True)  10.4 us
    all_to_all x1, waiting for transfers between devices, local(): lax.all_to_all(outgoing, 'lon', split_axis=0, concat_axis=0, tiled=True)  8.94 us
    add x2, local copies, waits for them, and re-layouts, build_table(): sin_t = (sa * cb + ca * sb).reshape(n_full, n_waves)  3.69 us
    sub x2, local copies, waits for them, and re-layouts, build_table(): cos_t = (ca * cb - sa * sb).reshape(n_full, n_waves)  3.66 us
    ppermute x3, waiting for transfers between devices, shifted_from(): return lax.ppermute(block, axis, route)  3.11 us
  transfers between devices with their start and end apart: 5, of which 3 were waited for; matrix products, arithmetic and copies ran while one was open for 10% of the time, Pallas kernels for 0%

profile of v9, /device:TPU:1, one launch (start us, length us, event | category | flops | bytes accessed | tf_op | source)
XLA Modules:
  0.0 108.1 jit_solution(13291936096592955816)
XLA Ops:
  0.0 1.0 copy.40
  1.0 0.1 copy.41
  1.1 1.0 all_to_all.16
  2.1 28.3 %all-to-all-start = ((f32[64,1,432]{2,1,0:T(1,128)}), f32[64,1,432]{2,1,0:T(1,128)}, u32[]{:S(2)}, u32[]{:S(2)}) async-start(f32[64,1,432]{2,1,0:T(1,128)} %all_to_all.16), calls=%async_computation | async-start | bytes 262144 | tf_op jit(solution)/shard_map/all_to_all | solution.py:54
  30.4 0.2 fusion.40
  30.7 0.3 fusion.34
  31.0 0.5 multiply_subtract_fusion
  31.5 1.7 %sub.43 = f32[64,18,353]{2,1,0:T(8,128)} reshape(f32[36,32,353]{2,1,0:T(8,128)S(1)} %get-tuple-element.7) | data formatting | bytes 3253248 | tf_op jit(solution)/shard_map/sub | solution.py:31
  33.2 2.0 %copy.38 = f32[64,18,353]{2,0,1:T(8,128)S(1)} copy(f32[64,18,353]{2,1,0:T(8,128)} %sub.43) | data formatting | bytes 3253248 | tf_op jit(solution)/shard_map/sub | solution.py:31
  35.2 1.7 %add.86 = f32[64,18,353]{2,1,0:T(8,128)} reshape(f32[36,32,353]{2,1,0:T(8,128)S(1)} %get-tuple-element.8) | data formatting | bytes 3253248 | tf_op jit(solution)/shard_map/add | solution.py:32
  36.9 2.0 %copy.39 = f32[64,18,353]{2,0,1:T(8,128)S(1)} copy(f32[64,18,353]{2,1,0:T(8,128)} %add.86) | data formatting | bytes 3253248 | tf_op jit(solution)/shard_map/add | solution.py:32
  38.9 0.1 eq.36
  39.0 0.1 fusion.43
  39.1 0.7 pad_maximum_fusion.21
  39.8 8.9 %all-to-all-done = f32[64,1,432]{2,1,0:T(1,128)} async-done(((f32[64,1,432]{2,1,0:T(1,128)}), f32[64,1,432]{2,1,0:T(1,128)}, u32[]{:S(2)}, u32[]{:S(2)}) %all-to-all-start) | async-done | bytes 110624 | tf_op jit(solution)/shard_map/all_to_all | solution.py:54
  48.7 1.7 %copy.43 = f32[64,1,432]{0,2,1:T(8,128)} copy(f32[64,1,432]{2,1,0:T(1,128)} %all-to-all-done) | data formatting | bytes 221184 | tf_op jit(solution)/shard_map/all_to_all | solution.py:54
  50.4 1.7 %reshape.168 = f32[64,24,18]{0,2,1:T(8,128)} reshape(f32[64,1,432]{0,2,1:T(8,128)} %copy.43) | data formatting | bytes 221184 | tf_op jit(solution)/shard_map/reshape | solution.py:55
  52.1 2.3 %fusion.5 = f32[24,706,1]{1,0,2:T(8,128)S(1)} fusion(f32[64,18,353]{2,0,1:T(8,128)S(1)} %copy.39, f32[64,18,353]{2,0,1:T(8,128)S(1)} %copy.38, f32[64,24,18]{0,2,1:T(8,128)} %reshape.168, f32[8,706]{1,0:T(8,128)} %pad_maximum_fusion.21), kind=kOutput, calls=%fused_computation.8 | convolution fusion | flops 117947184 | bytes 3454208 | tf_op jit(solution)/shard_map/dot_general | solution.py:62
  54.4 2.9 %fusion.2 = f32[24,64,18]{1,0,2:T(8,128)} fusion(f32[24,706,1]{1,0,2:T(8,128)S(1)} %fusion.5, f32[64,18,353]{2,0,1:T(8,128)S(1)} %copy.39, f32[64,18,353]{2,0,1:T(8,128)S(1)} %copy.38, f32[64,24,18]{0,2,1:T(8,128)S(1)} %copy-done.1, pred[24]{0:T(512)(128)(4,1)S(1)} %eq.36), kind=kOutput, calls=%fused_computation.5 | convolution fusion | flops 117957888 | bytes 3542232 | tf_op jit(solution)/shard_map/dot_general | solution.py:69
  57.3 1.3 %copy.46 = f32[24,64,18]{2,1,0:T(8,128)S(1)} copy(f32[24,64,18]{1,0,2:T(8,128)} %fusion.2) | data formatting | bytes 221184 | tf_op jit(solution)/shard_map/jit(_where)/select_n | solution.py:76
  58.6 0.4 reshape.169
  59.0 0.3 rev.6
  59.4 0.3 rev.7
  59.7 0.0 slice-start
  59.7 0.1 fusion.53
  59.8 0.1 pad_maximum_fusion.20
  59.9 0.2 concatenate.51
  60.1 0.0 copy-start.3
  60.1 0.1 copy.47
  60.3 0.1 copy.48
  60.3 0.2 fusion.8
  60.5 0.8 copy.49
  61.4 10.4 %all-to-all-start.1 = ((f32[64,1,660]{2,1,0:T(1,128)}), f32[64,1,660]{2,1,0:T(1,128)S(1)}, u32[]{:S(2)}, u32[]{:S(2)}) async-start(f32[64,1,660]{2,1,0:T(1,128)} %copy.49), calls=%async_computation.1 | async-start | bytes 393216 | tf_op jit(solution)/shard_map/all_to_all | solution.py:89
  71.8 2.9 %collective-permute-start = (f32[8,1,192]{2,1,0:T(1,128)S(1)}, f32[8,1,192]{2,1,0:T(1,128)S(1)}, u32[]{:S(2)}, u32[]{:S(2)}) collective-permute-start(f32[8,1,192]{2,1,0:T(1,128)S(1)} %copy.51), channel_id=1, source_target_pairs={{0,1},{1,2},{2,3},{3,4},{4,5},{5,6},{6,7},{7,8},{8,9},{9,10},{10,1... | collective-permute-start | bytes 18440 | tf_op jit(solution)/shard_map/ppermute | solution.py:14
  75.0 0.1 fusion.48
  75.1 15.3 %all-to-all-done.1 = f32[64,1,660]{2,1,0:T(1,128)S(1)} async-done(((f32[64,1,660]{2,1,0:T(1,128)}), f32[64,1,660]{2,1,0:T(1,128)S(1)}, u32[]{:S(2)}, u32[]{:S(2)}) %all-to-all-start.1) | async-done | bytes 168992 | tf_op jit(solution)/shard_map/all_to_all | solution.py:89
  90.4 0.5 reduce
  90.8 0.1 reshape.170
  91.0 0.1 slice.146
  91.1 0.1 copy.50
  91.3 10.4 %collective-permute-start.1 = (f32[3,18,192]{2,1,0:T(8,128)S(1)}, f32[3,18,192]{2,1,0:T(8,128)S(1)}, u32[]{:S(2)}, u32[]{:S(2)}) collective-permute-start(f32[3,18,192]{2,1,0:T(8,128)S(1)} %pad_maximum_fusion.19), channel_id=1, source_target_pairs={{0,64},{64,128},{128,192},{192,256},{256,320},{320,384},{384,448},... | collective-permute-start | bytes 124424 | tf_op jit(solution)/shard_map/ppermute | solution.py:14
  101.7 1.9 %collective-permute-start.2 = (f32[2,18,192]{2,1,0:T(8,128)S(1)}, f32[2,18,192]{2,1,0:T(8,128)S(1)}, u32[]{:S(2)}, u32[]{:S(2)}) collective-permute-start(f32[2,18,192]{2,1,0:T(8,128)S(1)} %get-tuple-element.10), channel_id=1, source_target_pairs={{64,0},{128,64},{192,128},{256,192},{320,256},{384,320},{448,384},... | collective-permute-start | bytes 82952 | tf_op jit(solution)/shard_map/ppermute | solution.py:14
  103.7 0.1 fusion.27
  103.8 0.1 copy.55
  104.0 3.1 %collective-permute-done.2 = f32[2,18,192]{2,1,0:T(8,128)S(1)} collective-permute-done((f32[2,18,192]{2,1,0:T(8,128)S(1)}, f32[2,18,192]{2,1,0:T(8,128)S(1)}, u32[]{:S(2)}, u32[]{:S(2)}) %collective-permute-start.2) | collective-permute-done | bytes 27680 | tf_op jit(solution)/shard_map/ppermute | solution.py:14
  107.1 0.1 fusion.18
  107.3 0.1 fusion.21
  107.4 0.7 copy.56
  (35 shorter events, 0.4 us)
Async XLA Ops:
  2.1 46.6 %all-to-all-start = ((f32[64,1,432]{2,1,0:T(1,128)}), f32[64,1,432]{2,1,0:T(1,128)}, u32[]{:S(2)}, u32[]{:S(2)}) async-start(f32[64,1,432]{2,1,0:T(1,128)} %all_to_all.16), calls=%async_computation | async-start | bytes 262144 | tf_op jit(solution)/shard_map/all_to_all | solution.py:54
  36.8 2.0 %copy-start.5 = (s32[8]{0:T(128)S(1)}, s32[8]{0:T(128)}, u32[]{:S(2)}) copy-start(s32[8]{0:T(128)} %param.9) | copy-start | bytes 100
  36.8 2.2 %copy-start.4 = (s32[8]{0:T(128)S(1)}, s32[8]{0:T(128)}, u32[]{:S(2)}) copy-start(s32[8]{0:T(128)} %param.8) | copy-start | bytes 100
  52.1 2.3 %copy-start.1 = (f32[64,24,18]{0,2,1:T(8,128)S(1)}, f32[64,24,18]{0,2,1:T(8,128)}, u32[]{:S(2)}) copy-start(f32[64,24,18]{0,2,1:T(8,128)} %reshape.168) | copy-start | bytes 331780
  57.3 2.9 %copy-start = (f32[24,64,18]{1,0,2:T(8,128)S(1)}, f32[24,64,18]{1,0,2:T(8,128)}, u32[]{:S(2)}) copy-start(f32[24,64,18]{1,0,2:T(8,128)} %fusion.2) | copy-start | bytes 331780
  59.7 12.1 %slice-start = ((f32[8,18,192]{2,0,1:T(8,128)}), f32[8,1,192]{2,0,1:T(8,128)S(1)}, s32[]{:S(2)}) async-start(f32[8,18,192]{2,0,1:T(8,128)} %param.6), calls=%async_computation.2 | async-start | bytes 16384 | tf_op jit(solution)/shard_map/slice | solution.py:51
  59.7 15.0 %copy-start.2 = (f32[8,18,192]{2,0,1:T(8,128)S(1)}, f32[8,18,192]{2,0,1:T(8,128)}, u32[]{:S(2)}) copy-start(f32[8,18,192]{2,0,1:T(8,128)} %param.6) | copy-start | bytes 331780
  60.1 14.7 %copy-start.3 = (f32[8,18,192]{2,0,1:T(8,128)S(1)}, f32[8,18,192]{2,0,1:T(8,128)}, u32[]{:S(2)}) copy-start(f32[8,18,192]{2,0,1:T(8,128)} %param.7) | copy-start | bytes 331780
  61.4 29.0 %all-to-all-start.1 = ((f32[64,1,660]{2,1,0:T(1,128)}), f32[64,1,660]{2,1,0:T(1,128)S(1)}, u32[]{:S(2)}, u32[]{:S(2)}) async-start(f32[64,1,660]{2,1,0:T(1,128)} %copy.49), calls=%async_computation.1 | async-start | bytes 393216 | tf_op jit(solution)/shard_map/all_to_all | solution.py:89
  71.8 31.8 %collective-permute-start = (f32[8,1,192]{2,1,0:T(1,128)S(1)}, f32[8,1,192]{2,1,0:T(1,128)S(1)}, u32[]{:S(2)}, u32[]{:S(2)}) collective-permute-start(f32[8,1,192]{2,1,0:T(1,128)S(1)} %copy.51), channel_id=1, source_target_pairs={{0,1},{1,2},{2,3},{3,4},{4,5},{5,6},{6,7},{7,8},{8,9},{9,10},{10,1... | collective-permute-start | bytes 18440 | tf_op jit(solution)/shard_map/ppermute | solution.py:14
  91.3 12.7 %collective-permute-start.1 = (f32[3,18,192]{2,1,0:T(8,128)S(1)}, f32[3,18,192]{2,1,0:T(8,128)S(1)}, u32[]{:S(2)}, u32[]{:S(2)}) collective-permute-start(f32[3,18,192]{2,1,0:T(8,128)S(1)} %pad_maximum_fusion.19), channel_id=1, source_target_pairs={{0,64},{64,128},{128,192},{192,256},{256,320},{320,384},{384,448},... | collective-permute-start | bytes 124424 | tf_op jit(solution)/shard_map/ppermute | solution.py:14
  101.7 5.4 %collective-permute-start.2 = (f32[2,18,192]{2,1,0:T(8,128)S(1)}, f32[2,18,192]{2,1,0:T(8,128)S(1)}, u32[]{:S(2)}, u32[]{:S(2)}) collective-permute-start(f32[2,18,192]{2,1,0:T(8,128)S(1)} %get-tuple-element.10), channel_id=1, source_target_pairs={{64,0},{128,64},{192,128},{256,192},{320,256},{384,320},{448,384},... | collective-permute-start | bytes 82952 | tf_op jit(solution)/shard_map/ppermute | solution.py:14

commit v10 on v9

--- a/solution.py
+++ b/solution.py
@@ -42,13 +42,14 @@
     n_lat = n_rows * lat_count
     half = n_full // 2
     group = n_comp // lon_count
-    n_send = n_rows + 2
+    n_send = n_rows + 4
     n_win = n_cols + 4
 
     top = n_full // 8 + (half - 1 - n_full // 8) * (n_lat // 4 - 1) // (n_lat // 2)
     n_waves = min(top, half - 1) + 1
 
     east_halo = shifted_from(courant_east[:, -1:], "lon", 1)
+    north_halo = shifted_from(courant_north[-1:], "lat", 1, wrap=False)
 
     outgoing = state.reshape(n_rows * n_cols, n_comp).T.reshape(lon_count, -1)
     incoming = lax.all_to_all(outgoing, "lon", split_axis=0, concat_axis=0, tiled=True)
@@ -76,10 +77,13 @@
     smooth = jnp.where(keep, filtered, jnp.transpose(blocks, (1, 0, 2)))
     smooth = smooth.reshape(group, n_rows, n_full)
 
-    south_pole = smooth[:, 1::-1]
-    north_pole = smooth[:, : n_rows - 3 : -1]
-    pole = jnp.roll(jnp.where(lat_index == 0, south_pole, north_pole), half, axis=2)
-    rows_out = jnp.concatenate([pole, smooth], axis=1)
+    from_south = shifted_from(smooth[:, -2:], "lat", 1, wrap=False)
+    from_north = shifted_from(smooth[:, :2], "lat", -1, wrap=False)
+    south_pole = jnp.roll(smooth[:, 1::-1], half, axis=2)
+    north_pole = jnp.roll(smooth[:, : n_rows - 3 : -1], half, axis=2)
+    low = jnp.where(lat_index == 0, south_pole, from_south)
+    high = jnp.where(lat_index == lat_count - 1, north_pole, from_north)
+    rows_out = jnp.concatenate([low, smooth, high], axis=1)
 
     tiles = rows_out.reshape(group, n_send, lon_count, n_cols)
     left = jnp.roll(tiles[..., -2:], 1, axis=2)
@@ -88,13 +92,8 @@
     windows = jnp.transpose(windows, (2, 0, 1, 3)).reshape(lon_count, -1)
     back = lax.all_to_all(windows, "lon", split_axis=0, concat_axis=0, tiled=True)
     ext = back.reshape(n_comp, n_send * n_win).T.reshape(n_send, n_win, n_comp)
-    own = ext[2:]
+    own = ext[2:-2]
     centre = own[:, 2:-2]
-
-    from_south = shifted_from(
-        jnp.concatenate([centre[-2:], courant_north[-1:]], axis=0), "lat", 1, wrap=False
-    )
-    from_north = shifted_from(centre[:2], "lat", -1, wrap=False)
 
     zonal_c = jnp.concatenate([east_halo, courant_east], axis=1)
     east = face_flux(
@@ -106,11 +105,8 @@
     )
     zonal = -(east[:, 1:] - east[:, :-1])
 
-    pole_rows = ext[:2, 2:-2]
-    south = jnp.where(lat_index == 0, pole_rows, from_south[:2])
-    north = jnp.where(lat_index == lat_count - 1, pole_rows, from_north)
-    merid_p = jnp.concatenate([south, centre, north], axis=0)
-    south_c = jnp.where(lat_index == 0, 0.0, from_south[2:3])
+    merid_p = ext[:, 2:-2]
+    south_c = jnp.where(lat_index == 0, 0.0, north_halo)
     merid_c = jnp.concatenate([south_c, courant_north], axis=0)
     north_flux = face_flux(
         merid_p[0 : n_rows + 1],

time: 109 us -> 109 us (level)
  the two profiles are of different devices: /device:TPU:1 before, /device:TPU:73 now
where the time goes in v10:
time: 109 us; the launch traced here: 108 us
  starting transfers between devices  48.9 us (45%)
  waiting for transfers between devices  31.8 us (29%)
  local copies, waits for them, and re-layouts  18.6 us (17%)
  matrix products  5.22 us (5%)
  other arithmetic  3.34 us (3%)
    all_to_all x1, starting transfers between devices, local(): lax.all_to_all(outgoing, 'lon', split_axis=0, concat_axis=0, tiled=True)  26.2 us
    all_to_all x1, waiting for transfers between devices, local(): lax.all_to_all(windows, 'lon', split_axis=0, concat_axis=0, tiled=True)  20.7 us
    ppermute x4, starting transfers between devices, shifted_from(): return lax.ppermute(block, axis, route)  13.1 us
    all_to_all x1, starting transfers between devices, local(): lax.all_to_all(windows, 'lon', split_axis=0, concat_axis=0, tiled=True)  9.59 us
    all_to_all x1, waiting for transfers between devices, local(): lax.all_to_all(outgoing, 'lon', split_axis=0, concat_axis=0, tiled=True)  8.42 us
    add x2, local copies, waits for them, and re-layouts, build_table(): sin_t = (sa * cb + ca * sb).reshape(n_full, n_waves)  3.69 us
    sub x2, local copies, waits for them, and re-layouts, build_table(): cos_t = (ca * cb - sa * sb).reshape(n_full, n_waves)  3.66 us
    dot_general x1, matrix products, local(): lax.dot_general(coeffs, fourier.reshape(lon_count, n_cols, -1), (((1,), (...  2.97 us
  transfers between devices with their start and end apart: 6, of which 3 were waited for; matrix products, arithmetic and copies ran while one was open for 11% of the time, Pallas kernels for 0%

profile of v10, /device:TPU:73, one launch (start us, length us, event | category | flops | bytes accessed | tf_op | source)
XLA Modules:
  0.0 108.3 jit_solution(12808011130165154947)
XLA Ops:
  0.0 1.0 copy.26
  1.0 0.1 copy.27
  1.1 1.0 all_to_all.16
  2.1 26.2 %all-to-all-start = ((f32[64,1,432]{2,1,0:T(1,128)}), f32[64,1,432]{2,1,0:T(1,128)}, u32[]{:S(2)}, u32[]{:S(2)}) async-start(f32[64,1,432]{2,1,0:T(1,128)} %all_to_all.16), calls=%async_computation | async-start | bytes 262144 | tf_op jit(solution)/shard_map/all_to_all | solution.py:55
  28.4 0.2 fusion.37
  28.6 0.3 fusion.31
  28.9 0.5 multiply_subtract_fusion
  29.4 1.7 %sub.43 = f32[64,18,353]{2,1,0:T(8,128)} reshape(f32[36,32,353]{2,1,0:T(8,128)S(1)} %get-tuple-element.5) | data formatting | bytes 3253248 | tf_op jit(solution)/shard_map/sub | solution.py:31
  31.1 2.0 %copy.24 = f32[64,18,353]{2,0,1:T(8,128)S(1)} copy(f32[64,18,353]{2,1,0:T(8,128)} %sub.43) | data formatting | bytes 3253248 | tf_op jit(solution)/shard_map/sub | solution.py:31
  33.1 1.7 %add.86 = f32[64,18,353]{2,1,0:T(8,128)} reshape(f32[36,32,353]{2,1,0:T(8,128)S(1)} %get-tuple-element.6) | data formatting | bytes 3253248 | tf_op jit(solution)/shard_map/add | solution.py:32
  34.8 2.0 %copy.25 = f32[64,18,353]{2,0,1:T(8,128)S(1)} copy(f32[64,18,353]{2,1,0:T(8,128)} %add.86) | data formatting | bytes 3253248 | tf_op jit(solution)/shard_map/add | solution.py:32
  37.0 0.7 pad_maximum_fusion.21
  37.7 8.4 %all-to-all-done = f32[64,1,432]{2,1,0:T(1,128)} async-done(((f32[64,1,432]{2,1,0:T(1,128)}), f32[64,1,432]{2,1,0:T(1,128)}, u32[]{:S(2)}, u32[]{:S(2)}) %all-to-all-start) | async-done | bytes 110624 | tf_op jit(solution)/shard_map/all_to_all | solution.py:55
  46.1 1.7 %copy.29 = f32[64,1,432]{0,2,1:T(8,128)} copy(f32[64,1,432]{2,1,0:T(1,128)} %all-to-all-done) | data formatting | bytes 221184 | tf_op jit(solution)/shard_map/all_to_all | solution.py:55
  47.8 1.7 %reshape.169 = f32[64,24,18]{0,2,1:T(8,128)} reshape(f32[64,1,432]{0,2,1:T(8,128)} %copy.29) | data formatting | bytes 221184 | tf_op jit(solution)/shard_map/reshape | solution.py:56
  49.5 2.3 %fusion.5 = f32[24,706,1]{1,0,2:T(8,128)S(1)} fusion(f32[64,18,353]{2,0,1:T(8,128)S(1)} %copy.25, f32[64,18,353]{2,0,1:T(8,128)S(1)} %copy.24, f32[64,24,18]{0,2,1:T(8,128)} %reshape.169, f32[8,706]{1,0:T(8,128)} %pad_maximum_fusion.21), kind=kOutput, calls=%fused_computation.8 | convolution fusion | flops 117947184 | bytes 3454208 | tf_op jit(solution)/shard_map/dot_general | solution.py:63
  51.8 3.0 %fusion.2 = f32[24,64,18]{1,0,2:T(8,128)} fusion(f32[24,706,1]{1,0,2:T(8,128)S(1)} %fusion.5, f32[64,18,353]{2,0,1:T(8,128)S(1)} %copy.25, f32[64,18,353]{2,0,1:T(8,128)S(1)} %copy.24, f32[64,24,18]{0,2,1:T(8,128)S(1)} %copy-done.1, pred[24]{0:T(512)(128)(4,1)S(1)} %eq.35), kind=kOutput, calls=%fused_computation.5 | convolution fusion | flops 117957888 | bytes 3542232 | tf_op jit(solution)/shard_map/dot_general | solution.py:70
  54.7 1.3 %copy.32 = f32[24,64,18]{2,1,0:T(8,128)S(1)} copy(f32[24,64,18]{1,0,2:T(8,128)} %fusion.2) | data formatting | bytes 221184 | tf_op jit(solution)/shard_map/jit(_where)/select_n | solution.py:77
  56.1 0.4 reshape.170
  56.5 5.7 %collective-permute-start = (f32[3,2,1152]{2,1,0:T(2,128)S(1)}, f32[3,2,1152]{2,1,0:T(2,128)S(1)}, u32[]{:S(2)}, u32[]{:S(2)}) collective-permute-start(f32[3,2,1152]{2,1,0:T(2,128)S(1)} %get-tuple-element.11), channel_id=1, source_target_pairs={{0,64},{64,128},{128,192},{192,256},{256,320},{320,384},{384,448},... | collective-permute-start | bytes 82952 | tf_op jit(solution)/shard_map/ppermute | solution.py:14
  62.1 0.1 fusion.48
  62.2 0.2 slice.120
  62.4 0.2 slice.122
  62.6 0.2 slice.125
  62.8 0.2 slice.127
  63.0 1.9 %collective-permute-start.1 = (f32[3,2,1152]{2,1,0:T(2,128)S(1)}, f32[3,2,1152]{2,1,0:T(2,128)S(1)}, u32[]{:S(2)}, u32[]{:S(2)}) collective-permute-start(f32[3,2,1152]{2,1,0:T(2,128)S(1)} %get-tuple-element.12), channel_id=1, source_target_pairs={{64,0},{128,64},{192,128},{256,192},{320,256},{384,320},{448,384},... | collective-permute-start | bytes 82952 | tf_op jit(solution)/shard_map/ppermute | solution.py:14
  65.0 0.1 maximum_select_fusion
  65.1 0.2 concatenate.44
  65.3 0.1 copy.33
  65.5 2.7 %collective-permute-done.1 = f32[3,2,1152]{2,1,0:T(2,128)S(1)} collective-permute-done((f32[3,2,1152]{2,1,0:T(2,128)S(1)}, f32[3,2,1152]{2,1,0:T(2,128)S(1)}, u32[]{:S(2)}, u32[]{:S(2)}) %collective-permute-start.1) | collective-permute-done | bytes 27680 | tf_op jit(solution)/shard_map/ppermute | solution.py:14
  68.3 0.2 concatenate.47
  68.5 0.1 copy.35
  68.7 0.2 fusion.8
  68.9 0.9 copy.36
  69.8 9.6 %all-to-all-start.1 = ((f32[64,1,792]{2,1,0:T(1,128)}), f32[64,1,792]{2,1,0:T(1,128)S(1)}, u32[]{:S(2)}, u32[]{:S(2)}) async-start(f32[64,1,792]{2,1,0:T(1,128)} %copy.36), calls=%async_computation.1 | async-start | bytes 458752 | tf_op jit(solution)/shard_map/all_to_all | solution.py:93
  79.5 2.5 %collective-permute-start.3 = (f32[1,18,192]{2,1,0:T(8,128)S(1)}, f32[1,18,192]{2,1,0:T(8,128)S(1)}, u32[]{:S(2)}, u32[]{:S(2)}) collective-permute-start(f32[1,18,192]{2,1,0:T(8,128)S(1)} %slice.165), channel_id=1, source_target_pairs={{0,64},{64,128},{128,192},{192,256},{256,320},{320,384},{384,448},... | collective-permute-start | bytes 41480 | tf_op jit(solution)/shard_map/ppermute | solution.py:14
  82.0 3.1 %collective-permute-start.2 = (f32[8,1,192]{2,1,0:T(1,128)S(1)}, f32[8,1,192]{2,1,0:T(1,128)S(1)}, u32[]{:S(2)}, u32[]{:S(2)}) collective-permute-start(f32[8,1,192]{2,1,0:T(1,128)S(1)} %copy.38), channel_id=1, source_target_pairs={{0,1},{1,2},{2,3},{3,4},{4,5},{5,6},{6,7},{7,8},{8,9},{9,10},{10,1... | collective-permute-start | bytes 18440 | tf_op jit(solution)/shard_map/ppermute | solution.py:14
  85.1 0.1 fusion.45
  85.4 20.7 %all-to-all-done.1 = f32[64,1,792]{2,1,0:T(1,128)S(1)} async-done(((f32[64,1,792]{2,1,0:T(1,128)}), f32[64,1,792]{2,1,0:T(1,128)S(1)}, u32[]{:S(2)}, u32[]{:S(2)}) %all-to-all-start.1) | async-done | bytes 202784 | tf_op jit(solution)/shard_map/all_to_all | solution.py:93
  106.0 0.5 reduce
  106.6 0.2 reshape.171
  106.7 0.1 copy.42
  106.9 0.1 fusion.15
  107.0 0.1 slice.157
  107.2 0.1 copy.37
  107.3 0.1 fusion.24
  107.5 0.1 fusion.18
  107.6 0.7 copy.43
  (37 shorter events, 0.6 us)
Async XLA Ops:
  2.1 44.0 %all-to-all-start = ((f32[64,1,432]{2,1,0:T(1,128)}), f32[64,1,432]{2,1,0:T(1,128)}, u32[]{:S(2)}, u32[]{:S(2)}) async-start(f32[64,1,432]{2,1,0:T(1,128)} %all_to_all.16), calls=%async_computation | async-start | bytes 262144 | tf_op jit(solution)/shard_map/all_to_all | solution.py:55
  34.8 2.0 %copy-start.5 = (s32[8]{0:T(128)S(1)}, s32[8]{0:T(128)}, u32[]{:S(2)}) copy-start(s32[8]{0:T(128)} %param.9) | copy-start | bytes 100
  34.8 2.2 %copy-start.4 = (s32[8]{0:T(128)S(1)}, s32[8]{0:T(128)}, u32[]{:S(2)}) copy-start(s32[8]{0:T(128)} %param.8) | copy-start | bytes 100
  49.5 2.3 %copy-start.1 = (f32[64,24,18]{0,2,1:T(8,128)S(1)}, f32[64,24,18]{0,2,1:T(8,128)}, u32[]{:S(2)}) copy-start(f32[64,24,18]{0,2,1:T(8,128)} %reshape.169) | copy-start | bytes 331780
  54.7 10.2 %copy-start = (f32[24,64,18]{1,0,2:T(8,128)S(1)}, f32[24,64,18]{1,0,2:T(8,128)}, u32[]{:S(2)}) copy-start(f32[24,64,18]{1,0,2:T(8,128)} %fusion.2) | copy-start | bytes 331780
  56.5 8.6 %collective-permute-start = (f32[3,2,1152]{2,1,0:T(2,128)S(1)}, f32[3,2,1152]{2,1,0:T(2,128)S(1)}, u32[]{:S(2)}, u32[]{:S(2)}) collective-permute-start(f32[3,2,1152]{2,1,0:T(2,128)S(1)} %get-tuple-element.11), channel_id=1, source_target_pairs={{0,64},{64,128},{128,192},{192,256},{256,320},{320,384},{384,448},... | collective-permute-start | bytes 82952 | tf_op jit(solution)/shard_map/ppermute | solution.py:14
  63.0 5.2 %collective-permute-start.1 = (f32[3,2,1152]{2,1,0:T(2,128)S(1)}, f32[3,2,1152]{2,1,0:T(2,128)S(1)}, u32[]{:S(2)}, u32[]{:S(2)}) collective-permute-start(f32[3,2,1152]{2,1,0:T(2,128)S(1)} %get-tuple-element.12), channel_id=1, source_target_pairs={{64,0},{128,64},{192,128},{256,192},{320,256},{384,320},{448,384},... | collective-permute-start | bytes 82952 | tf_op jit(solution)/shard_map/ppermute | solution.py:14
  65.5 13.9 %copy-start.3 = (f32[8,18,192]{2,0,1:T(8,128)S(1)}, f32[8,18,192]{2,0,1:T(8,128)}, u32[]{:S(2)}) copy-start(f32[8,18,192]{2,0,1:T(8,128)} %param.7) | copy-start | bytes 331780
  68.5 13.5 %slice-start = ((f32[8,18,192]{2,0,1:T(8,128)}), f32[8,1,192]{2,0,1:T(8,128)S(1)}, s32[]{:S(2)}) async-start(f32[8,18,192]{2,0,1:T(8,128)} %param.6), calls=%async_computation.2 | async-start | bytes 16384 | tf_op jit(solution)/shard_map/slice | solution.py:51
  68.5 16.8 %copy-start.2 = (f32[8,18,192]{2,0,1:T(8,128)S(1)}, f32[8,18,192]{2,0,1:T(8,128)}, u32[]{:S(2)}) copy-start(f32[8,18,192]{2,0,1:T(8,128)} %param.6) | copy-start | bytes 331780
  69.8 36.2 %all-to-all-start.1 = ((f32[64,1,792]{2,1,0:T(1,128)}), f32[64,1,792]{2,1,0:T(1,128)S(1)}, u32[]{:S(2)}, u32[]{:S(2)}) async-start(f32[64,1,792]{2,1,0:T(1,128)} %copy.36), calls=%async_computation.1 | async-start | bytes 458752 | tf_op jit(solution)/shard_map/all_to_all | solution.py:93
  79.5 5.9 %collective-permute-start.3 = (f32[1,18,192]{2,1,0:T(8,128)S(1)}, f32[1,18,192]{2,1,0:T(8,128)S(1)}, u32[]{:S(2)}, u32[]{:S(2)}) collective-permute-start(f32[1,18,192]{2,1,0:T(8,128)S(1)} %slice.165), channel_id=1, source_target_pairs={{0,64},{64,128},{128,192},{192,256},{256,320},{320,384},{384,448},... | collective-permute-start | bytes 41480 | tf_op jit(solution)/shard_map/ppermute | solution.py:14
  82.0 25.3 %collective-permute-start.2 = (f32[8,1,192]{2,1,0:T(1,128)S(1)}, f32[8,1,192]{2,1,0:T(1,128)S(1)}, u32[]{:S(2)}, u32[]{:S(2)}) collective-permute-start(f32[8,1,192]{2,1,0:T(1,128)S(1)} %copy.38), channel_id=1, source_target_pairs={{0,1},{1,2},{2,3},{3,4},{4,5},{5,6},{6,7},{7,8},{8,9},{9,10},{10,1... | collective-permute-start | bytes 18440 | tf_op jit(solution)/shard_map/ppermute | solution.py:14

commit v11 on v10

--- a/solution.py
+++ b/solution.py
@@ -54,6 +54,7 @@
     outgoing = state.reshape(n_rows * n_cols, n_comp).T.reshape(lon_count, -1)
     incoming = lax.all_to_all(outgoing, "lon", split_axis=0, concat_axis=0, tiled=True)
     blocks = incoming.reshape(lon_count, group * n_rows, n_cols)
+    blocks, east_halo, north_halo = lax.optimization_barrier((blocks, east_halo, north_halo))
 
     fourier = build_table(n_full, n_waves, 32)
     waves = jnp.arange(n_waves, dtype=jnp.int32)

time: 109 us -> 119 us (1.092)
  starting transfers between devices: 48.9 us -> 53.2 us
  local copies, waits for them, and re-layouts: 18.6 us -> 22.7 us
  other arithmetic: 3.34 us -> 4.54 us
    all_to_all x1, waiting for transfers between devices: 20.7 us -> 25.6 us  [local(): lax.all_to_all(windows, 'lon', split_axis=0, concat_axis=0, tiled=True)]
    all_to_all x1, waiting for transfers between devices: 8.42 us -> 3.61 us  [local(): lax.all_to_all(outgoing, 'lon', split_axis=0, concat_axis=0, tiled=True)]
    all_to_all x1, starting transfers between devices: 9.59 us -> 13.6 us  [local(): lax.all_to_all(windows, 'lon', split_axis=0, concat_axis=0, tiled=True)]
    unnamed x15 -> x21, local copies, waits for them, and re-layouts: 1.08 us -> 3.04 us
  transfers between devices with their start and end apart: 6 -> 6, of which waited for: 3 -> 3; matrix products, arithmetic and copies ran while one was open for 11% -> 15% of each run, Pallas kernels for 0% -> 0%
where the time goes in v11:
time: 119 us; the launch traced here: 118 us
  starting transfers between devices  53.2 us (45%)
  waiting for transfers between devices  32 us (27%)
  local copies, waits for them, and re-layouts  22.7 us (19%)
  matrix products  5.29 us (4%)
  other arithmetic  4.54 us (4%)
    all_to_all x1, waiting for transfers between devices, local(): lax.all_to_all(windows, 'lon', split_axis=0, concat_axis=0, tiled=True)  25.6 us
    all_to_all x1, starting transfers between devices, local(): lax.all_to_all(outgoing, 'lon', split_axis=0, concat_axis=0, tiled=True)  25.3 us
    ppermute x4, starting transfers between devices, shifted_from(): return lax.ppermute(block, axis, route)  14.3 us
    all_to_all x1, starting transfers between devices, local(): lax.all_to_all(windows, 'lon', split_axis=0, concat_axis=0, tiled=True)  13.6 us
    add x2, local copies, waits for them, and re-layouts, build_table(): sin_t = (sa * cb + ca * sb).reshape(n_full, n_waves)  3.67 us
    sub x2, local copies, waits for them, and re-layouts, build_table(): cos_t = (ca * cb - sa * sb).reshape(n_full, n_waves)  3.67 us
    all_to_all x1, waiting for transfers between devices, local(): lax.all_to_all(outgoing, 'lon', split_axis=0, concat_axis=0, tiled=True)  3.61 us
    unnamed x21, local copies, waits for them, and re-layouts  3.04 us
  transfers between devices with their start and end apart: 6, of which 3 were waited for; matrix products, arithmetic and copies ran while one was open for 15% of the time, Pallas kernels for 0%

profile of v11, /device:TPU:73, one launch (start us, length us, event | category | flops | bytes accessed | tf_op | source)
XLA Modules:
  0.0 118.1 jit_solution(16137653318200898037)
XLA Ops:
  0.0 1.0 copy.29
  1.0 0.7 copy-done.2
  1.7 0.6 slice.151
  2.3 4.5 %collective-permute-start.1 = (f32[1,18,192]{2,1,0:T(8,128)}, f32[1,18,192]{2,1,0:T(8,128)}, u32[]{:S(2)}, u32[]{:S(2)}) collective-permute-start(f32[1,18,192]{2,1,0:T(8,128)} %slice.151), channel_id=1, source_target_pairs={{0,64},{64,128},{128,192},{192,256},{256,320},{320,384},{384,448},... | collective-permute-start | bytes 41480 | tf_op jit(solution)/shard_map/ppermute | solution.py:14
  6.9 1.0 copy.24
  8.0 1.0 all_to_all.16
  9.0 25.3 %all-to-all-start = ((f32[64,1,432]{2,1,0:T(1,128)}), f32[64,1,432]{2,1,0:T(1,128)}, u32[]{:S(2)}, u32[]{:S(2)}) async-start(f32[64,1,432]{2,1,0:T(1,128)} %all_to_all.16), calls=%async_computation | async-start | bytes 262144 | tf_op jit(solution)/shard_map/all_to_all | solution.py:55
  34.3 3.1 %collective-permute-start = (f32[8,1,192]{2,1,0:T(1,128)S(1)}, f32[8,1,192]{2,1,0:T(1,128)S(1)}, u32[]{:S(2)}, u32[]{:S(2)}) collective-permute-start(f32[8,1,192]{2,1,0:T(1,128)S(1)} %copy.28), channel_id=1, source_target_pairs={{0,1},{1,2},{2,3},{3,4},{4,5},{5,6},{6,7},{7,8},{8,9},{9,10},{10,1... | collective-permute-start | bytes 18440 | tf_op jit(solution)/shard_map/ppermute | solution.py:14
  37.4 0.3 fusion.30
  37.8 0.5 broadcast_compare_fusion
  38.3 0.2 fusion.36
  38.6 0.5 multiply_subtract_fusion
  39.1 0.7 pad_maximum_fusion.19
  39.8 1.7 %sub.43 = f32[64,18,353]{2,1,0:T(8,128)} reshape(f32[36,32,353]{2,1,0:T(8,128)S(1)} %get-tuple-element.11) | data formatting | bytes 3253248 | tf_op jit(solution)/shard_map/sub | solution.py:31
  41.4 2.0 %copy.30 = f32[64,18,353]{2,0,1:T(8,128)S(1)} copy(f32[64,18,353]{2,1,0:T(8,128)} %sub.43) | data formatting | bytes 3253248 | tf_op jit(solution)/shard_map/sub | solution.py:31
  43.4 1.7 %add.86 = f32[64,18,353]{2,1,0:T(8,128)} reshape(f32[36,32,353]{2,1,0:T(8,128)S(1)} %get-tuple-element.12) | data formatting | bytes 3253248 | tf_op jit(solution)/shard_map/add | solution.py:32
  45.1 2.0 %copy.31 = f32[64,18,353]{2,0,1:T(8,128)S(1)} copy(f32[64,18,353]{2,1,0:T(8,128)} %add.86) | data formatting | bytes 3253248 | tf_op jit(solution)/shard_map/add | solution.py:32
  47.1 0.5 tile.6
  47.7 1.2 %eq.35 = pred[24]{0:T(512)(128)(4,1)} reshape(pred[3,8]{1,0:T(4,128)(4,1)} %tile.6) | data formatting | bytes 48 | tf_op jit(solution)/shard_map/eq | solution.py:77
  48.9 3.6 %all-to-all-done = f32[64,1,432]{2,1,0:T(1,128)} async-done(((f32[64,1,432]{2,1,0:T(1,128)}), f32[64,1,432]{2,1,0:T(1,128)}, u32[]{:S(2)}, u32[]{:S(2)}) %all-to-all-start) | async-done | bytes 110624 | tf_op jit(solution)/shard_map/all_to_all | solution.py:55
  52.5 1.7 %copy.27 = f32[64,1,432]{0,2,1:T(8,128)} copy(f32[64,1,432]{2,1,0:T(1,128)} %all-to-all-done) | data formatting | bytes 221184 | tf_op jit(solution)/shard_map/all_to_all | solution.py:55
  54.2 1.7 %reshape.169 = f32[64,24,18]{0,2,1:T(8,128)} reshape(f32[64,1,432]{0,2,1:T(8,128)} %copy.27) | data formatting | bytes 221184 | tf_op jit(solution)/shard_map/reshape | solution.py:56
  55.9 2.3 %fusion.4 = f32[24,706,1]{1,0,2:T(8,128)S(1)} fusion(f32[64,18,353]{2,0,1:T(8,128)S(1)} %copy.31, f32[64,18,353]{2,0,1:T(8,128)S(1)} %copy.30, f32[64,24,18]{0,2,1:T(8,128)} %reshape.169, f32[8,706]{1,0:T(8,128)} %pad_maximum_fusion.19), kind=kOutput, calls=%fused_computation.7 | convolution fusion | flops 117947184 | bytes 3454208 | tf_op jit(solution)/shard_map/dot_general | solution.py:64
  58.2 3.0 %bitcast_select_fusion = f32[24,64,18]{1,0,2:T(8,128)} fusion(f32[64,24,18]{0,2,1:T(8,128)S(1)} %copy-done.1, pred[24]{0:T(512)(128)(4,1)S(1)} %copy-done.5, f32[24,706,1]{1,0,2:T(8,128)S(1)} %fusion.4, f32[64,18,353]{2,0,1:T(8,128)S(1)} %copy.31, f32[64,18,353]{2,0,1:T(8,128)S(1)} %copy.30), kind=kOutput, calls=%fused_computation.28 | convolution fusion | flops 117957888 | bytes 3542232 | tf_op jit(solution)/shard_map/dot_general | solution.py:71
  61.2 1.3 %copy.34 = f32[24,64,18]{2,1,0:T(8,128)S(1)} copy(f32[24,64,18]{1,0,2:T(8,128)} %bitcast_select_fusion) | data formatting | bytes 221184 | tf_op jit(solution)/shard_map/jit(_where)/select_n | solution.py:78
  62.5 0.4 reshape.170
  62.9 4.8 %collective-permute-start.2 = (f32[3,2,1152]{2,1,0:T(2,128)S(1)}, f32[3,2,1152]{2,1,0:T(2,128)S(1)}, u32[]{:S(2)}, u32[]{:S(2)}) collective-permute-start(f32[3,2,1152]{2,1,0:T(2,128)S(1)} %get-tuple-element.17), channel_id=1, source_target_pairs={{0,64},{64,128},{128,192},{192,256},{256,320},{320,384},{384,448},... | collective-permute-start | bytes 82952 | tf_op jit(solution)/shard_map/ppermute | solution.py:14
  67.8 0.2 slice.122
  68.0 0.2 slice.124
  68.2 0.2 slice.127
  68.4 0.2 slice.129
  68.6 1.9 %collective-permute-start.3 = (f32[3,2,1152]{2,1,0:T(2,128)S(1)}, f32[3,2,1152]{2,1,0:T(2,128)S(1)}, u32[]{:S(2)}, u32[]{:S(2)}) collective-permute-start(f32[3,2,1152]{2,1,0:T(2,128)S(1)} %get-tuple-element.18), channel_id=1, source_target_pairs={{64,0},{128,64},{192,128},{256,192},{320,256},{384,320},{448,384},... | collective-permute-start | bytes 82952 | tf_op jit(solution)/shard_map/ppermute | solution.py:14
  70.7 0.2 concatenate.44
  70.9 0.1 copy.35
  71.0 2.7 %collective-permute-done.3 = f32[3,2,1152]{2,1,0:T(2,128)S(1)} collective-permute-done((f32[3,2,1152]{2,1,0:T(2,128)S(1)}, f32[3,2,1152]{2,1,0:T(2,128)S(1)}, u32[]{:S(2)}, u32[]{:S(2)}) %collective-permute-start.3) | collective-permute-done | bytes 27680 | tf_op jit(solution)/shard_map/ppermute | solution.py:14
  73.8 0.2 concatenate.47
  74.2 0.2 fusion.7
  74.5 0.9 copy.38
  75.3 13.6 %all-to-all-start.1 = ((f32[64,1,792]{2,1,0:T(1,128)}), f32[64,1,792]{2,1,0:T(1,128)S(1)}, u32[]{:S(2)}, u32[]{:S(2)}) async-start(f32[64,1,792]{2,1,0:T(1,128)} %copy.38), calls=%async_computation.1 | async-start | bytes 458752 | tf_op jit(solution)/shard_map/all_to_all | solution.py:94
  89.1 0.8 broadcast_select_fusion
  89.9 25.6 %all-to-all-done.1 = f32[64,1,792]{2,1,0:T(1,128)S(1)} async-done(((f32[64,1,792]{2,1,0:T(1,128)}), f32[64,1,792]{2,1,0:T(1,128)S(1)}, u32[]{:S(2)}, u32[]{:S(2)}) %all-to-all-start.1) | async-done | bytes 202784 | tf_op jit(solution)/shard_map/all_to_all | solution.py:94
  115.5 0.5 reduce
  116.0 0.2 reshape.171
  116.3 0.1 copy.42
  116.7 0.1 fusion.23
  116.8 0.3 copy-done.3
  117.1 0.1 fusion.14
  117.4 0.7 copy.43
  (43 shorter events, 1.3 us)
Async XLA Ops:
  0.0 34.3 %slice-start = ((f32[8,18,192]{2,0,1:T(8,128)}), f32[8,1,192]{2,0,1:T(8,128)S(1)}, s32[]{:S(2)}) async-start(f32[8,18,192]{2,0,1:T(8,128)} %param.6), calls=%async_computation.2 | async-start | bytes 16384 | tf_op jit(solution)/shard_map/slice | solution.py:51
  0.0 37.8 %copy-start.7 = (s32[8]{0:T(128)S(1)}, s32[8]{0:T(128)}, u32[]{:S(2)}) copy-start(s32[8]{0:T(128)} %param.9) | copy-start | bytes 100
  0.0 38.3 %copy-start.6 = (s32[8]{0:T(128)S(1)}, s32[8]{0:T(128)}, u32[]{:S(2)}) copy-start(s32[8]{0:T(128)} %param.8) | copy-start | bytes 100
  1.0 0.7 copy-start.2
  2.3 53.6 %collective-permute-start.1 = (f32[1,18,192]{2,1,0:T(8,128)}, f32[1,18,192]{2,1,0:T(8,128)}, u32[]{:S(2)}, u32[]{:S(2)}) collective-permute-start(f32[1,18,192]{2,1,0:T(8,128)} %slice.151), channel_id=1, source_target_pairs={{0,64},{64,128},{128,192},{192,256},{256,320},{320,384},{384,448},... | collective-permute-start | bytes 41480 | tf_op jit(solution)/shard_map/ppermute | solution.py:14
  9.0 43.5 %all-to-all-start = ((f32[64,1,432]{2,1,0:T(1,128)}), f32[64,1,432]{2,1,0:T(1,128)}, u32[]{:S(2)}, u32[]{:S(2)}) async-start(f32[64,1,432]{2,1,0:T(1,128)} %all_to_all.16), calls=%async_computation | async-start | bytes 262144 | tf_op jit(solution)/shard_map/all_to_all | solution.py:55
  34.3 21.5 %collective-permute-start = (f32[8,1,192]{2,1,0:T(1,128)S(1)}, f32[8,1,192]{2,1,0:T(1,128)S(1)}, u32[]{:S(2)}, u32[]{:S(2)}) collective-permute-start(f32[8,1,192]{2,1,0:T(1,128)S(1)} %copy.28), channel_id=1, source_target_pairs={{0,1},{1,2},{2,3},{3,4},{4,5},{5,6},{6,7},{7,8},{8,9},{9,10},{10,1... | collective-permute-start | bytes 18440 | tf_op jit(solution)/shard_map/ppermute | solution.py:14
  45.1 2.0 %copy-start.8 = (pred[8]{0:T(512)(128)(4,1)S(1)}, pred[8]{0:T(512)(128)(4,1)}, u32[]{:S(2)}) copy-start(pred[8]{0:T(512)(128)(4,1)} %broadcast_compare_fusion) | copy-start | bytes 28
  55.9 2.4 %copy-start.1 = (f32[64,24,18]{0,2,1:T(8,128)S(1)}, f32[64,24,18]{0,2,1:T(8,128)}, u32[]{:S(2)}) copy-start(f32[64,24,18]{0,2,1:T(8,128)} %reshape.169) | copy-start | bytes 331780
  55.9 2.4 %copy-start.5 = (pred[24]{0:T(512)(128)(4,1)S(1)}, pred[24]{0:T(512)(128)(4,1)}, u32[]{:S(2)}) copy-start(pred[24]{0:T(512)(128)(4,1)} %eq.35) | copy-start | bytes 76
  61.2 9.3 %copy-start = (f32[24,64,18]{1,0,2:T(8,128)S(1)}, f32[24,64,18]{1,0,2:T(8,128)}, u32[]{:S(2)}) copy-start(f32[24,64,18]{1,0,2:T(8,128)} %bitcast_select_fusion) | copy-start | bytes 331780
  62.9 7.7 %collective-permute-start.2 = (f32[3,2,1152]{2,1,0:T(2,128)S(1)}, f32[3,2,1152]{2,1,0:T(2,128)S(1)}, u32[]{:S(2)}, u32[]{:S(2)}) collective-permute-start(f32[3,2,1152]{2,1,0:T(2,128)S(1)} %get-tuple-element.17), channel_id=1, source_target_pairs={{0,64},{64,128},{128,192},{192,256},{256,320},{320,384},{384,448},... | collective-permute-start | bytes 82952 | tf_op jit(solution)/shard_map/ppermute | solution.py:14
  68.6 5.2 %collective-permute-start.3 = (f32[3,2,1152]{2,1,0:T(2,128)S(1)}, f32[3,2,1152]{2,1,0:T(2,128)S(1)}, u32[]{:S(2)}, u32[]{:S(2)}) collective-permute-start(f32[3,2,1152]{2,1,0:T(2,128)S(1)} %get-tuple-element.18), channel_id=1, source_target_pairs={{64,0},{128,64},{192,128},{256,192},{320,256},{384,320},{448,384},... | collective-permute-start | bytes 82952 | tf_op jit(solution)/shard_map/ppermute | solution.py:14
  71.0 17.9 %copy-start.4 = (f32[8,18,192]{2,0,1:T(8,128)S(1)}, f32[8,18,192]{2,0,1:T(8,128)}, u32[]{:S(2)}) copy-start(f32[8,18,192]{2,0,1:T(8,128)} %param.6) | copy-start | bytes 331780
  75.3 40.2 %all-to-all-start.1 = ((f32[64,1,792]{2,1,0:T(1,128)}), f32[64,1,792]{2,1,0:T(1,128)S(1)}, u32[]{:S(2)}, u32[]{:S(2)}) async-start(f32[64,1,792]{2,1,0:T(1,128)} %copy.38), calls=%async_computation.1 | async-start | bytes 458752 | tf_op jit(solution)/shard_map/all_to_all | solution.py:94
  116.2 0.9 copy-start.3

commit v12 on v10

--- a/solution.py
+++ b/solution.py
@@ -42,18 +42,22 @@
     n_lat = n_rows * lat_count
     half = n_full // 2
     group = n_comp // lon_count
-    n_send = n_rows + 4
+    n_send = n_rows + 5
     n_win = n_cols + 4
 
     top = n_full // 8 + (half - 1 - n_full // 8) * (n_lat // 4 - 1) // (n_lat // 2)
     n_waves = min(top, half - 1) + 1
 
-    east_halo = shifted_from(courant_east[:, -1:], "lon", 1)
-    north_halo = shifted_from(courant_north[-1:], "lat", 1, wrap=False)
-
-    outgoing = state.reshape(n_rows * n_cols, n_comp).T.reshape(lon_count, -1)
+    sent = jnp.concatenate([state, courant_north[-1:]], axis=0)
+    lead = sent.reshape((n_rows + 1) * n_cols, n_comp).T.reshape(lon_count, -1)
+    tail = courant_east[:, -1].T.reshape(lon_count, -1)
+    outgoing = jnp.concatenate([lead, tail], axis=1)
     incoming = lax.all_to_all(outgoing, "lon", split_axis=0, concat_axis=0, tiled=True)
-    blocks = incoming.reshape(lon_count, group * n_rows, n_cols)
+    n_lead = group * (n_rows + 1) * n_cols
+    lead_in = incoming[:, :n_lead].reshape(lon_count, group, n_rows + 1, n_cols)
+    blocks = lead_in[:, :, :n_rows].reshape(lon_count, group * n_rows, n_cols)
+    face_row = jnp.transpose(lead_in[:, :, n_rows], (1, 0, 2)).reshape(group, 1, n_full)
+    face_col = jnp.roll(incoming[:, n_lead:], 1, axis=0)
 
     fourier = build_table(n_full, n_waves, 32)
     waves = jnp.arange(n_waves, dtype=jnp.int32)
@@ -77,21 +81,28 @@
     smooth = jnp.where(keep, filtered, jnp.transpose(blocks, (1, 0, 2)))
     smooth = smooth.reshape(group, n_rows, n_full)
 
-    from_south = shifted_from(smooth[:, -2:], "lat", 1, wrap=False)
+    from_south = shifted_from(
+        jnp.concatenate([smooth[:, -2:], face_row], axis=1), "lat", 1, wrap=False
+    )
     from_north = shifted_from(smooth[:, :2], "lat", -1, wrap=False)
     south_pole = jnp.roll(smooth[:, 1::-1], half, axis=2)
     north_pole = jnp.roll(smooth[:, : n_rows - 3 : -1], half, axis=2)
-    low = jnp.where(lat_index == 0, south_pole, from_south)
+    low = jnp.where(lat_index == 0, south_pole, from_south[:, :2])
     high = jnp.where(lat_index == lat_count - 1, north_pole, from_north)
-    rows_out = jnp.concatenate([low, smooth, high], axis=1)
+    rows_out = jnp.concatenate([low, smooth, high, from_south[:, 2:]], axis=1)
 
     tiles = rows_out.reshape(group, n_send, lon_count, n_cols)
     left = jnp.roll(tiles[..., -2:], 1, axis=2)
     right = jnp.roll(tiles[..., :2], -1, axis=2)
     windows = jnp.concatenate([left, tiles, right], axis=3)
     windows = jnp.transpose(windows, (2, 0, 1, 3)).reshape(lon_count, -1)
+    windows = jnp.concatenate([windows, face_col], axis=1)
     back = lax.all_to_all(windows, "lon", split_axis=0, concat_axis=0, tiled=True)
-    ext = back.reshape(n_comp, n_send * n_win).T.reshape(n_send, n_win, n_comp)
+    n_back = group * n_send * n_win
+    ext = back[:, :n_back].reshape(n_comp, -1).T.reshape(n_send, n_win, n_comp)
+    east_halo = back[:, n_back:].reshape(n_comp, n_rows).T[:, None, :]
+    north_halo = ext[n_send - 1 :, 2:-2]
+    ext = ext[: n_send - 1]
     own = ext[2:-2]
     centre = own[:, 2:-2]
 

time: 109 us -> 115 us (1.055)
  the two profiles are of different devices: /device:TPU:73 before, /device:TPU:72 now
where the time goes in v12:
time: 115 us; the launch traced here: 114 us
  starting transfers between devices  40.6 us (35%)
  waiting for transfers between devices  38.3 us (33%)
  local copies, waits for them, and re-layouts  26.1 us (23%)
  matrix products  5.01 us (4%)
  other arithmetic  3.94 us (3%)
    all_to_all x1, starting transfers between devices, local(): lax.all_to_all(outgoing, 'lon', split_axis=0, concat_axis=0, tiled=True)  26.7 us
    all_to_all x1, waiting for transfers between devices, local(): lax.all_to_all(windows, 'lon', split_axis=0, concat_axis=0, tiled=True)  26.3 us
    all_to_all x1, waiting for transfers between devices, local(): lax.all_to_all(outgoing, 'lon', split_axis=0, concat_axis=0, tiled=True)  9.91 us
    all_to_all x1, starting transfers between devices, local(): lax.all_to_all(windows, 'lon', split_axis=0, concat_axis=0, tiled=True)  9.55 us
    ppermute x2, starting transfers between devices, shifted_from(): return lax.ppermute(block, axis, route)  4.31 us
    add x2, local copies, waits for them, and re-layouts, build_table(): sin_t = (sa * cb + ca * sb).reshape(n_full, n_waves)  3.68 us
    sub x2, local copies, waits for them, and re-layouts, build_table(): cos_t = (ca * cb - sa * sb).reshape(n_full, n_waves)  3.66 us
    dot_general x1, matrix products, local(): lax.dot_general(coeffs, fourier.reshape(lon_count, n_cols, -1), (((1,), (...  2.97 us
  transfers between devices with their start and end apart: 4, of which 3 were waited for; matrix products, arithmetic and copies ran while one was open for 11% of the time, Pallas kernels for 0%

profile of v12, /device:TPU:72, one launch (start us, length us, event | category | flops | bytes accessed | tf_op | source)
XLA Modules:
  0.0 114.5 jit_solution(507750310088553447)
XLA Ops:
  0.0 0.9 slice.161
  0.9 0.9 pad_maximum_fusion.23
  2.2 0.7 slice_bitcast_fusion.1
  3.2 0.8 copy.53
  4.0 26.7 %all-to-all-start = ((f32[64,1,510]{2,1,0:T(1,128)}), f32[64,1,510]{2,1,0:T(1,128)}, u32[]{:S(2)}, u32[]{:S(2)}) async-start(f32[64,1,510]{2,1,0:T(1,128)} %copy.53), calls=%async_computation | async-start | bytes 262144 | tf_op jit(solution)/shard_map/all_to_all | solution.py:55
  30.8 0.2 fusion.38
  31.0 0.3 fusion.32
  31.4 0.5 multiply_subtract_fusion
  32.0 1.7 %sub.43 = f32[64,18,353]{2,1,0:T(8,128)} reshape(f32[36,32,353]{2,1,0:T(8,128)S(1)} %get-tuple-element.5) | data formatting | bytes 3253248 | tf_op jit(solution)/shard_map/sub | solution.py:31
  33.7 2.0 %copy.56 = f32[64,18,353]{2,0,1:T(8,128)S(1)} copy(f32[64,18,353]{2,1,0:T(8,128)} %sub.43) | data formatting | bytes 3253248 | tf_op jit(solution)/shard_map/sub | solution.py:31
  35.7 1.7 %add.86 = f32[64,18,353]{2,1,0:T(8,128)} reshape(f32[36,32,353]{2,1,0:T(8,128)S(1)} %get-tuple-element.6) | data formatting | bytes 3253248 | tf_op jit(solution)/shard_map/add | solution.py:32
  37.3 2.0 %copy.57 = f32[64,18,353]{2,0,1:T(8,128)S(1)} copy(f32[64,18,353]{2,1,0:T(8,128)} %add.86) | data formatting | bytes 3253248 | tf_op jit(solution)/shard_map/add | solution.py:32
  39.5 0.7 pad_maximum_fusion.27
  40.2 9.9 %all-to-all-done = f32[64,1,510]{2,1,0:T(1,128)} async-done(((f32[64,1,510]{2,1,0:T(1,128)}), f32[64,1,510]{2,1,0:T(1,128)}, u32[]{:S(2)}, u32[]{:S(2)}) %all-to-all-start) | async-done | bytes 130592 | tf_op jit(solution)/shard_map/all_to_all | solution.py:55
  50.1 1.6 %copy.85 = f32[64,1,510]{2,0,1:T(8,128)} copy(f32[64,1,510]{2,1,0:T(1,128)} %all-to-all-done) | data formatting | bytes 261120
  51.7 1.7 %copy.54 = f32[64,486]{0,1:T(8,128)} copy(f32[64,486]{1,0:T(8,128)} %bitcast.55) | data formatting | bytes 248832 | tf_op jit(solution)/shard_map/slice | solution.py:57
  53.4 1.7 %reshape.185 = f32[64,3,9,18]{0,3,2,1:T(8,128)} reshape(f32[64,486]{0,1:T(8,128)} %copy.54) | data formatting | bytes 248832 | tf_op jit(solution)/shard_map/reshape | solution.py:57
  55.1 1.0 slice.206
  56.1 1.4 %slice_bitcast_fusion = f32[3,64,18]{1,2,0:T(8,128)} fusion(f32[64,3,9,18]{0,3,2,1:T(8,128)} %reshape.185), kind=kLoop, calls=%fused_computation.72 | loop fusion | bytes 27648 | tf_op jit(solution)/shard_map/transpose | solution.py:59
  57.5 2.0 %fusion.5 = f32[24,706,1]{1,0,2:T(8,128)S(1)} fusion(f32[64,18,353]{2,0,1:T(8,128)S(1)} %copy.57, f32[64,18,353]{2,0,1:T(8,128)S(1)} %copy.56, f32[64,3,8,18]{0,3,2,1:T(8,128)S(1)} %slice.206, f32[8,706]{1,0:T(8,128)} %pad_maximum_fusion.27), kind=kOutput, calls=%fused_computation.8 | convolution fusion | flops 117947184 | bytes 3454208 | tf_op jit(solution)/shard_map/dot_general | solution.py:67
  59.5 3.0 %fusion.2 = f32[24,64,18]{1,0,2:T(8,128)} fusion(f32[24,706,1]{1,0,2:T(8,128)S(1)} %fusion.5, f32[64,18,353]{2,0,1:T(8,128)S(1)} %copy.57, f32[64,18,353]{2,0,1:T(8,128)S(1)} %copy.56, f32[64,3,8,18]{0,3,2,1:T(8,128)S(1)} %slice.206, pred[24]{0:T(512)(128)(4,1)S(1)} %eq.35), kind=kOutput, calls=%fused_computation.5 | convolution fusion | flops 117957888 | bytes 3542232 | tf_op jit(solution)/shard_map/dot_general | solution.py:74
  62.5 1.3 %copy.58 = f32[24,64,18]{2,1,0:T(8,128)S(1)} copy(f32[24,64,18]{1,0,2:T(8,128)} %fusion.2) | data formatting | bytes 221184 | tf_op jit(solution)/shard_map/jit(_where)/select_n | solution.py:81
  63.8 0.4 reshape.187
  64.4 0.1 reshape.195
  64.6 1.9 %collective-permute-start.1 = (f32[3,2,1152]{2,1,0:T(2,128)S(1)}, f32[3,2,1152]{2,1,0:T(2,128)S(1)}, u32[]{:S(2)}, u32[]{:S(2)}) collective-permute-start(f32[3,2,1152]{2,1,0:T(2,128)S(1)} %get-tuple-element.11), channel_id=1, source_target_pairs={{64,0},{128,64},{192,128},{256,192},{320,256},{384,320},{448,384},... | collective-permute-start | bytes 82952 | tf_op jit(solution)/shard_map/ppermute | solution.py:14
  66.6 0.8 slice.217
  67.4 0.8 slice.216
  68.1 2.4 %collective-permute-start = (f32[3,3,1152]{2,1,0:T(4,128)S(1)}, f32[3,3,1152]{2,1,0:T(4,128)S(1)}, u32[]{:S(2)}, u32[]{:S(2)}) collective-permute-start(f32[3,3,1152]{2,1,0:T(4,128)S(1)} %pad_maximum_fusion.26), channel_id=1, source_target_pairs={{0,64},{64,128},{128,192},{192,256},{256,320},{320,384},{384,448},... | collective-permute-start | bytes 124424 | tf_op jit(solution)/shard_map/ppermute | solution.py:14
  70.6 0.2 slice.166
  70.8 0.2 slice.168
  71.0 0.2 slice.173
  71.2 0.2 slice.175
  71.7 0.2 concatenate.68
  71.9 0.1 copy.63
  72.0 2.1 %collective-permute-done = f32[3,3,1152]{2,1,0:T(4,128)S(1)} collective-permute-done((f32[3,3,1152]{2,1,0:T(4,128)S(1)}, f32[3,3,1152]{2,1,0:T(4,128)S(1)}, u32[]{:S(2)}, u32[]{:S(2)}) %collective-permute-start) | collective-permute-done | bytes 41504 | tf_op jit(solution)/shard_map/ppermute | solution.py:14
  74.2 0.2 concatenate.65
  74.5 0.1 copy.61
  74.6 0.1 concatenate.69
  74.9 0.2 fusion.8
  75.3 0.9 copy.67
  76.1 9.6 %all-to-all-start.1 = ((f32[64,1,882]{2,1,0:T(1,128)}), f32[64,1,882]{2,1,0:T(1,128)S(1)}, u32[]{:S(2)}, u32[]{:S(2)}) async-start(f32[64,1,882]{2,1,0:T(1,128)} %copy.67), calls=%async_computation.1 | async-start | bytes 458752 | tf_op jit(solution)/shard_map/all_to_all | solution.py:100
  86.0 26.3 %all-to-all-done.1 = f32[64,1,882]{2,1,0:T(1,128)S(1)} async-done(((f32[64,1,882]{2,1,0:T(1,128)}), f32[64,1,882]{2,1,0:T(1,128)S(1)}, u32[]{:S(2)}, u32[]{:S(2)}) %all-to-all-start.1) | async-done | bytes 225824 | tf_op jit(solution)/shard_map/all_to_all | solution.py:100
  112.4 0.2 reshape.190
  112.7 0.1 copy.71
  113.2 0.1 copy.73
  113.4 0.1 fusion.25
  113.5 0.1 fusion.15
  113.8 0.7 copy.74
  (56 shorter events, 2.8 us)
Async XLA Ops:
  4.0 46.1 %all-to-all-start = ((f32[64,1,510]{2,1,0:T(1,128)}), f32[64,1,510]{2,1,0:T(1,128)}, u32[]{:S(2)}, u32[]{:S(2)}) async-start(f32[64,1,510]{2,1,0:T(1,128)} %copy.53), calls=%async_computation | async-start | bytes 262144 | tf_op jit(solution)/shard_map/all_to_all | solution.py:55
  31.3 0.7 copy-start.5
  37.3 2.1 %copy-start.4 = (s32[8]{0:T(128)S(1)}, s32[8]{0:T(128)}, u32[]{:S(2)}) copy-start(s32[8]{0:T(128)} %param.8) | copy-start | bytes 100
  62.5 1.8 %copy-start.3 = (f32[3,64,18]{1,2,0:T(8,128)S(1)}, f32[3,64,18]{1,2,0:T(8,128)}, u32[]{:S(2)}) copy-start(f32[3,64,18]{1,2,0:T(8,128)} %slice_bitcast_fusion) | copy-start | bytes 41476
  62.5 8.9 %copy-start = (f32[24,64,18]{1,0,2:T(8,128)S(1)}, f32[24,64,18]{1,0,2:T(8,128)}, u32[]{:S(2)}) copy-start(f32[24,64,18]{1,0,2:T(8,128)} %fusion.2) | copy-start | bytes 331780
  64.6 7.0 %collective-permute-start.1 = (f32[3,2,1152]{2,1,0:T(2,128)S(1)}, f32[3,2,1152]{2,1,0:T(2,128)S(1)}, u32[]{:S(2)}, u32[]{:S(2)}) collective-permute-start(f32[3,2,1152]{2,1,0:T(2,128)S(1)} %get-tuple-element.11), channel_id=1, source_target_pairs={{64,0},{128,64},{192,128},{256,192},{320,256},{384,320},{448,384},... | collective-permute-start | bytes 82952 | tf_op jit(solution)/shard_map/ppermute | solution.py:14
  68.1 6.0 %collective-permute-start = (f32[3,3,1152]{2,1,0:T(4,128)S(1)}, f32[3,3,1152]{2,1,0:T(4,128)S(1)}, u32[]{:S(2)}, u32[]{:S(2)}) collective-permute-start(f32[3,3,1152]{2,1,0:T(4,128)S(1)} %pad_maximum_fusion.26), channel_id=1, source_target_pairs={{0,64},{64,128},{128,192},{192,256},{256,320},{320,384},{384,448},... | collective-permute-start | bytes 124424 | tf_op jit(solution)/shard_map/ppermute | solution.py:14
  74.9 10.8 %copy-start.2 = (f32[8,18,192]{2,0,1:T(8,128)S(1)}, f32[8,18,192]{2,0,1:T(8,128)}, u32[]{:S(2)}) copy-start(f32[8,18,192]{2,0,1:T(8,128)} %param.6) | copy-start | bytes 331780
  75.1 10.6 %copy-start.1 = (f32[8,18,192]{2,0,1:T(8,128)S(1)}, f32[8,18,192]{2,0,1:T(8,128)}, u32[]{:S(2)}) copy-start(f32[8,18,192]{2,0,1:T(8,128)} %param.7) | copy-start | bytes 331780
  76.1 36.1 %all-to-all-start.1 = ((f32[64,1,882]{2,1,0:T(1,128)}), f32[64,1,882]{2,1,0:T(1,128)S(1)}, u32[]{:S(2)}, u32[]{:S(2)}) async-start(f32[64,1,882]{2,1,0:T(1,128)} %copy.67), calls=%async_computation.1 | async-start | bytes 458752 | tf_op jit(solution)/shard_map/all_to_all | solution.py:100
